TPU v7x, 256 devices: a whole 4x4x8 slice. The times are simulated.
256 devices in a mesh: band: 2 (over y_hi), domain: 128 (over y_lo, x, z, core).
Axes of the slice: x: 4, y: 4 (y_hi: 2, y_lo: 2; y = y_hi * 2 + y_lo), z: 8, core: 2. Of those that a mesh axis runs over, the one named last changes fastest.
Arguments:
- targets: float32 [4, 36864, 192], P('band', 'domain'), may hold values from -5 to 5
- partner_pool: bfloat16 [64, 36864, 192], P('band', 'domain'), may hold values from -5 to 5
- owners: int32 [2], replicated, may hold values from 0 to 1, as said below
- warm_start: bfloat16 [2, 8, 4, 36864, 192], P(None, None, 'band', 'domain'), may hold values from -6 to 6
Outputs:
- exchange: float32 [4, 36864, 192], P('band', 'domain')
Inputs may be any that keep to these rules, and one draw needn't show every extreme that they name: The 2 broadcast blocks have distinct owners.
All inputs are finite; a program needn't handle non-finite values.
Results may differ from a plain program's by a relative error of at most 0.0006.
Values may be sent and summed in bfloat16 or wider, within the bound.
No kernel may reach another device: no remote copies, remote signals or barrier semaphores. Data moves between devices by JAX's collectives and lax.ppermute only.
A program may use at most 192 MiB of HBM per device.

v0:
```python
import math

import jax
import jax.numpy as jnp
from jax import lax
from jax.sharding import PartitionSpec as P

ORB = 8
STEPS = 2
SWEEPS = 3
GX = 192
GY = 192
GZ = 192


coupling = 4.0 * math.pi


def spread(block, axis, owner):
    block = jnp.where(lax.axis_index(axis) == owner, block, jnp.zeros_like(block))
    return lax.psum(block, axis)


def padded(block, sides, width):
    for axis, dim in sides:
        count = lax.axis_size(axis)
        forward = [(i, i + 1) for i in range(count - 1)]
        forward.append((count - 1, 0))
        backward = [(target, source) for source, target in forward]
        low = lax.ppermute(
            lax.slice_in_dim(block, block.shape[dim] - width, None, axis=dim), axis, forward
        )
        high = lax.ppermute(lax.slice_in_dim(block, 0, width, axis=dim), axis, backward)
        block = jnp.concatenate([low, block, high], axis=dim)
    return block


def row_sweep(widened, source, first_row):
    row_count = source.shape[1]
    line = GY
    centre = widened[:, line : line + row_count]
    beside = widened[:, :row_count] + widened[:, 2 * line : 2 * line + row_count]
    column = (first_row + jnp.arange(row_count, dtype=jnp.int32)) % line
    at_end = (column == line - 1)[None, :, None]
    at_start = (column == 0)[None, :, None]
    upper = jnp.where(
        at_end, widened[:, 1 : row_count + 1], widened[:, line + 1 : line + row_count + 1]
    )
    lower = jnp.where(
        at_start,
        widened[:, 2 * line - 1 : 2 * line - 1 + row_count],
        widened[:, line - 1 : line - 1 + row_count],
    )
    beside = beside + upper + lower + jnp.roll(centre, 1, 2) + jnp.roll(centre, -1, 2)
    return (beside + coupling * source) / 6.0


def fetch_block(partner_pool, owners, block_index):
    own_block = partner_pool[block_index * ORB : (block_index + 1) * ORB]
    return spread(own_block, "band", owners[block_index]).astype(jnp.float32)


def pair_products(partner, targets):
    density = partner[:, None] * targets[None]
    return (density, jnp.sum(density, axis=(2, 3)))


def solve_block(partner, density, mean_value, warm_block, first_row):
    block_width = partner.shape[0]
    target_count = density.shape[1]
    pair_count = block_width * target_count
    planes = density.shape[2:]
    source = density.reshape((pair_count,) + planes) - mean_value.reshape(pair_count, 1, 1)
    potential = warm_block.reshape((pair_count,) + planes).astype(jnp.float32)
    for sweep_index in range(SWEEPS):
        widened = padded(potential.astype(jnp.bfloat16), (("domain", 1),), GY).astype(
            potential.dtype
        )
        potential = row_sweep(widened, source, first_row)
    potential = potential.reshape((block_width, target_count) + planes)
    return jnp.sum(potential * partner[:, None], axis=0)


def body(targets, partner_pool, owners, warm_start):
    row_count = targets.shape[1]
    first_row = lax.axis_index("domain") * row_count
    cell_count = GX * GY * GZ
    exchange = jnp.zeros(targets.shape, jnp.float32)
    for block_index in range(STEPS):
        partner = fetch_block(partner_pool, owners, block_index)
        density, local_sums = pair_products(partner, targets)
        totals = lax.psum(local_sums, "domain")
        exchange = exchange - solve_block(
            partner, density, totals / cell_count, warm_start[block_index], first_row
        )
    return exchange


def solution(mesh):
    return jax.shard_map(
        body,
        mesh=mesh,
        in_specs=(
            P("band", "domain", None),
            P("band", "domain", None),
            P(),
            P(None, None, "band", "domain", None),
        ),
        out_specs=P("band", "domain", None),
        check_vma=False,
    )
```

profile of v0, /device:TPU:16, one launch (start us, length us, event | category | flops | bytes accessed | tf_op | source)
XLA Modules:
  0.0 643.9 jit_solution(16177434050569279853)
XLA Ops:
  11.4 8.2 %collective-permute-start.1 = (bf16[16,192,192]{2,1,0:T(8,128)(2,1)}, bf16[16,192,192]{2,1,0:T(8,128)(2,1)}, u32[]{:S(2)}, u32[]{:S(2)}) collective-permute-start(bf16[16,192,192]{2,1,0:T(8,128)(2,1)} %get-tuple-element.46), channel_id=1, source_target_pairs={{1,0},{2,1},{3,2},{4,3},{5,4},{6,5},{7,6},{8,7},{9,8},{10,9},{11,1... | collective-permute-start | bytes 3538952 | tf_op jit(solution)/shard_map/ppermute | solution.py:33
  21.1 6.5 %collective-permute-start.7 = (bf16[16,192,192]{2,1,0:T(8,128)(2,1)S(1)}, bf16[16,192,192]{2,1,0:T(8,128)(2,1)}, u32[]{:S(2)}, u32[]{:S(2)}) collective-permute-start(bf16[16,192,192]{2,1,0:T(8,128)(2,1)S(1)} %get-tuple-element.52), channel_id=1, source_target_pairs={{1,0},{2,1},{3,2},{4,3},{5,4},{6,5},{7,6},{8,7},{9,8},{10,9},{11,1... | collective-permute-start | bytes 3538952 | tf_op jit(solution)/shard_map/ppermute | solution.py:33
  32.8 5.2 collective-permute-done
  45.9 9.0 %collective-permute-done.6 = bf16[16,192,192]{2,1,0:T(8,128)(2,1)} collective-permute-done((bf16[16,192,192]{2,1,0:T(8,128)(2,1)}, bf16[16,192,192]{2,1,0:T(8,128)(2,1)}, u32[]{:S(2)}, u32[]{:S(2)}) %collective-permute-start.6) | collective-permute-done | bytes 1179680 | tf_op jit(solution)/shard_map/ppermute | solution.py:30
  62.2 10.6 %fusion.51 = (f32[16,288,191]{2,1,0:T(8,128)}, f32[16,288,191]{2,1,0:T(8,128)}) fusion(f32[16,672,192]{2,1,0:T(8,128)} %copy-done.3), kind=kLoop, calls=%fused_computation.90 | loop fusion | bytes 14082048 | tf_op jit(solution)/shard_map/jit(_roll_static)/slice | solution.py:54
  72.7 5.3 fusion.57
  78.0 40.9 %all-reduce.4.cloned.1.call-done = (bf16[8,288,192]{2,1,0:T(8,128)(2,1)}, bf16[8,288,192]{2,1,0:T(8,128)(2,1)}) async-done(((bf16[8,288,192]{2,1,0:T(8,128)(2,1)}, bf16[8,288,192]{2,1,0:T(8,128)(2,1)}), (bf16[8,288,192]{2,1,0:T(8,128)(2,1)}, bf16[8,288,192]{2,1,0:T(8,128)(2,1)})) %all-reduce.4.cloned.1.call-update) | async-done | bytes 1769488 | tf_op jit(solution)/shard_map/psum | solution.py:21
  127.6 286.3 %all-reduce = (f32[8,2]{1,0:T(8,128)S(1)}, f32[8,2]{1,0:T(8,128)S(1)}) all-reduce(f32[8,2]{1,0:T(8,128)S(1)} %get-tuple-element.6, f32[8,2]{1,0:T(8,128)S(1)} %get-tuple-element.5), channel_id=1, replica_groups=mesh['band'=2,'domain'=128] {'domain'}, use_global_device_ids=true, to_apply=%region_6.7 | all-reduce | flops 32 | bytes 256 | tf_op jit(solution)/shard_map/psum | solution.py:92
  414.0 18.2 %fusion.38 = bf16[16,288,192]{2,1,0:T(8,128)(2,1)S(1)} fusion(f32[16,672,192]{2,1,0:T(8,128)} %copy-done.3, f32[16,288,191]{2,1,0:T(8,128)} %get-tuple-element.20, f32[16,288,1]{2,1,0:T(8,128)} %get-tuple-element.22, f32[16,288,1]{2,1,0:T(8,128)} %get-tuple-element.21, f32[16,288,191]{2,1,0:T(8,128)} %get-tuple-element.19, ...), kind=kLoop, calls=%fused_computation.60 | loop fusion | flops 12386304 | bytes 33620608 | tf_op jit(solution)/shard_map/convert_element_type | solution.py:76
  434.6 6.0 collective-permute-start.3
  440.6 19.7 %fusion.18 = bf16[16,288,192]{2,1,0:T(8,128)(2,1)} fusion(f32[16,672,192]{2,1,0:T(8,128)} %copy-done.2, f32[16,288,191]{2,1,0:T(8,128)} %get-tuple-element.32, f32[16,288,1]{2,1,0:T(8,128)} %get-tuple-element.34, f32[16,288,1]{2,1,0:T(8,128)} %get-tuple-element.33, f32[16,288,191]{2,1,0:T(8,128)} %get-tuple-element.31, ...), kind=kLoop, calls=%fused_computation.31 | loop fusion | flops 12386304 | bytes 33620608 | tf_op jit(solution)/shard_map/convert_element_type | solution.py:76
  464.2 6.2 collective-permute-start.9
  477.7 5.3 fusion.49
  483.1 5.4 collective-permute-done.8
  491.9 5.8 fusion.55
  501.8 18.2 %fusion.31 = bf16[16,288,192]{2,1,0:T(8,128)(2,1)S(1)} fusion(f32[16,672,192]{2,1,0:T(8,128)} %copy-done.5, f32[16,288,191]{2,1,0:T(8,128)} %get-tuple-element.16, f32[16,288,1]{2,1,0:T(8,128)} %get-tuple-element.18, f32[16,288,1]{2,1,0:T(8,128)} %get-tuple-element.17, f32[16,288,191]{2,1,0:T(8,128)} %get-tuple-element.15, ...), kind=kLoop, calls=%fused_computation.50 | loop fusion | flops 12386304 | bytes 33620608 | tf_op jit(solution)/shard_map/convert_element_type | solution.py:76
  522.2 6.4 collective-permute-start.5
  528.5 19.5 %fusion.11 = bf16[16,288,192]{2,1,0:T(8,128)(2,1)} fusion(f32[16,672,192]{2,1,0:T(8,128)} %copy-done.4, f32[16,288,191]{2,1,0:T(8,128)} %get-tuple-element.28, f32[16,288,1]{2,1,0:T(8,128)} %get-tuple-element.30, f32[16,288,1]{2,1,0:T(8,128)} %get-tuple-element.29, f32[16,288,191]{2,1,0:T(8,128)} %get-tuple-element.27, ...), kind=kLoop, calls=%fused_computation.21 | loop fusion | flops 12386304 | bytes 33620608 | tf_op jit(solution)/shard_map/convert_element_type | solution.py:76
  552.0 6.0 collective-permute-start.11
  565.0 5.3 fusion.47
  570.4 5.8 collective-permute-done.10
  579.6 5.8 fusion.53
  589.5 20.2 %fusion.24 = f32[16,288,192]{2,1,0:T(8,128)} fusion(f32[16,672,192]{2,1,0:T(8,128)} %copy-done, f32[16,288,191]{2,1,0:T(8,128)} %get-tuple-element.12, f32[16,288,1]{2,1,0:T(8,128)} %get-tuple-element.14, f32[16,288,1]{2,1,0:T(8,128)} %get-tuple-element.13, f32[16,288,191]{2,1,0:T(8,128)} %get-tuple-element.11, f32[8,2,288,192]{3,2,1,0:T(8,128)} %get-tuple-element.39, ...), kind=kLoop, calls=%fused_computation.40 | loop fusion | flops 11501568 | bytes 35390080 | tf_op jit(solution)/shard_map/div | solution.py:55
  612.7 20.0 %fusion.4 = f32[16,288,192]{2,1,0:T(8,128)} fusion(f32[16,672,192]{2,1,0:T(8,128)} %copy-done.1, f32[16,288,191]{2,1,0:T(8,128)} %get-tuple-element.24, f32[16,288,1]{2,1,0:T(8,128)} %get-tuple-element.26, f32[16,288,1]{2,1,0:T(8,128)} %get-tuple-element.25, f32[16,288,191]{2,1,0:T(8,128)} %get-tuple-element.23, f32[8,2,288,192]{3,2,1,0:T(8,128)} %get-tuple-element.40, ...), kind=kLoop, calls=%fused_computation.11 | loop fusion | flops 11501568 | bytes 35390080 | tf_op jit(solution)/shard_map/div | solution.py:55
  (80 shorter events, 82.7 us)
Async XLA Ops:
  6.5 112.4 %all-reduce.4.cloned.1.call-start = ((), (), s32[]{:S(2)}) async-start(), calls=%async_computation | async-start | bytes 4718592 | tf_op jit(solution)/shard_map/psum | solution.py:21
  9.2 11.8 %copy-start.8 = (bf16[1,8,2,288,192]{4,3,2,1,0:T(8,128)(2,1)}, bf16[1,8,2,288,192]{4,3,2,1,0:T(8,128)(2,1)S(1)}, u32[]{:S(2)}) copy-start(bf16[1,8,2,288,192]{4,3,2,1,0:T(8,128)(2,1)S(1)} %get-tuple-element.36) | copy-start | bytes 5308420
  9.2 11.8 %copy-start.9 = (bf16[1,8,2,288,192]{4,3,2,1,0:T(8,128)(2,1)}, bf16[1,8,2,288,192]{4,3,2,1,0:T(8,128)(2,1)S(1)}, u32[]{:S(2)}) copy-start(bf16[1,8,2,288,192]{4,3,2,1,0:T(8,128)(2,1)S(1)} %get-tuple-element.35) | copy-start | bytes 5308420
  11.4 16.2 %copy-start.15 = (s32[2]{0:T(128)S(1)}, s32[2]{0:T(128)}, u32[]{:S(2)}) copy-start(s32[2]{0:T(128)} %param.6) | copy-start | bytes 28
  11.4 26.6 %collective-permute-start = (bf16[16,192,192]{2,1,0:T(8,128)(2,1)}, bf16[16,192,192]{2,1,0:T(8,128)(2,1)}, u32[]{:S(2)}, u32[]{:S(2)}) collective-permute-start(bf16[16,192,192]{2,1,0:T(8,128)(2,1)} %get-tuple-element.45), channel_id=1, source_target_pairs={{0,1},{1,2},{2,3},{3,4},{4,5},{5,6},{6,7},{7,8},{8,9},{9,10},{10,1... | collective-permute-start | bytes 3538952 | tf_op jit(solution)/shard_map/ppermute | solution.py:30
  11.4 26.6 %collective-permute-start.1 = (bf16[16,192,192]{2,1,0:T(8,128)(2,1)}, bf16[16,192,192]{2,1,0:T(8,128)(2,1)}, u32[]{:S(2)}, u32[]{:S(2)}) collective-permute-start(bf16[16,192,192]{2,1,0:T(8,128)(2,1)} %get-tuple-element.46), channel_id=1, source_target_pairs={{1,0},{2,1},{3,2},{4,3},{5,4},{6,5},{7,6},{8,7},{9,8},{10,9},{11,1... | collective-permute-start | bytes 3538952 | tf_op jit(solution)/shard_map/ppermute | solution.py:33
  21.1 33.9 %collective-permute-start.6 = (bf16[16,192,192]{2,1,0:T(8,128)(2,1)}, bf16[16,192,192]{2,1,0:T(8,128)(2,1)}, u32[]{:S(2)}, u32[]{:S(2)}) collective-permute-start(bf16[16,192,192]{2,1,0:T(8,128)(2,1)} %get-tuple-element.51), channel_id=1, source_target_pairs={{0,1},{1,2},{2,3},{3,4},{4,5},{5,6},{6,7},{7,8},{8,9},{9,10},{10,1... | collective-permute-start | bytes 3538952 | tf_op jit(solution)/shard_map/ppermute | solution.py:30
  21.1 33.9 %collective-permute-start.7 = (bf16[16,192,192]{2,1,0:T(8,128)(2,1)S(1)}, bf16[16,192,192]{2,1,0:T(8,128)(2,1)}, u32[]{:S(2)}, u32[]{:S(2)}) collective-permute-start(bf16[16,192,192]{2,1,0:T(8,128)(2,1)S(1)} %get-tuple-element.52), channel_id=1, source_target_pairs={{1,0},{2,1},{3,2},{4,3},{5,4},{6,5},{7,6},{8,7},{9,8},{10,9},{11,1... | collective-permute-start | bytes 3538952 | tf_op jit(solution)/shard_map/ppermute | solution.py:33
  42.4 12.5 %copy-start.3 = (f32[16,672,192]{2,1,0:T(8,128)}, f32[16,672,192]{2,1,0:T(8,128)S(1)}, u32[]{:S(2)}) copy-start(f32[16,672,192]{2,1,0:T(8,128)S(1)} %maximum_convert_fusion) | copy-start | bytes 24772612
  58.7 14.0 %copy-start.2 = (f32[16,672,192]{2,1,0:T(8,128)}, f32[16,672,192]{2,1,0:T(8,128)S(1)}, u32[]{:S(2)}) copy-start(f32[16,672,192]{2,1,0:T(8,128)S(1)} %maximum_convert_fusion.3) | copy-start | bytes 24772612
  78.0 44.7 %copy-start.14 = (f32[2,288,192]{2,1,0:T(8,128)S(1)}, f32[2,288,192]{2,1,0:T(8,128)}, u32[]{:S(2)}) copy-start(f32[2,288,192]{2,1,0:T(8,128)} %param.4) | copy-start | bytes 1327108
  432.3 28.0 %copy-start.6 = (bf16[16,288,192]{2,1,0:T(8,128)(2,1)}, bf16[16,288,192]{2,1,0:T(8,128)(2,1)S(1)}, u32[]{:S(2)}) copy-start(bf16[16,288,192]{2,1,0:T(8,128)(2,1)S(1)} %fusion.38) | copy-start | bytes 5308420
  434.4 35.9 %collective-permute-start.2 = (bf16[16,192,192]{2,1,0:T(8,128)(2,1)}, bf16[16,192,192]{2,1,0:T(8,128)(2,1)}, u32[]{:S(2)}, u32[]{:S(2)}) collective-permute-start(bf16[16,192,192]{2,1,0:T(8,128)(2,1)} %get-tuple-element.43), channel_id=1, source_target_pairs={{0,1},{1,2},{2,3},{3,4},{4,5},{5,6},{6,7},{7,8},{8,9},{9,10},{10,1... | collective-permute-start | bytes 3538952 | tf_op jit(solution)/shard_map/ppermute | solution.py:30
  434.6 35.8 %collective-permute-start.3 = (bf16[16,192,192]{2,1,0:T(8,128)(2,1)}, bf16[16,192,192]{2,1,0:T(8,128)(2,1)}, u32[]{:S(2)}, u32[]{:S(2)}) collective-permute-start(bf16[16,192,192]{2,1,0:T(8,128)(2,1)} %get-tuple-element.44), channel_id=1, source_target_pairs={{1,0},{2,1},{3,2},{4,3},{5,4},{6,5},{7,6},{8,7},{9,8},{10,9},{11,1... | collective-permute-start | bytes 3538952 | tf_op jit(solution)/shard_map/ppermute | solution.py:33
  464.2 24.3 %collective-permute-start.8 = (bf16[16,192,192]{2,1,0:T(8,128)(2,1)}, bf16[16,192,192]{2,1,0:T(8,128)(2,1)S(1)}, u32[]{:S(2)}, u32[]{:S(2)}) collective-permute-start(bf16[16,192,192]{2,1,0:T(8,128)(2,1)} %get-tuple-element.49), channel_id=1, source_target_pairs={{0,1},{1,2},{2,3},{3,4},{4,5},{5,6},{6,7},{7,8},{8,9},{9,10},{10,1... | collective-permute-start | bytes 3538952 | tf_op jit(solution)/shard_map/ppermute | solution.py:30
  464.2 24.4 %collective-permute-start.9 = (bf16[16,192,192]{2,1,0:T(8,128)(2,1)}, bf16[16,192,192]{2,1,0:T(8,128)(2,1)}, u32[]{:S(2)}, u32[]{:S(2)}) collective-permute-start(bf16[16,192,192]{2,1,0:T(8,128)(2,1)} %get-tuple-element.50), channel_id=1, source_target_pairs={{1,0},{2,1},{3,2},{4,3},{5,4},{6,5},{7,6},{8,7},{9,8},{10,9},{11,1... | collective-permute-start | bytes 3538952 | tf_op jit(solution)/shard_map/ppermute | solution.py:33
  474.1 9.0 %copy-start.5 = (f32[16,672,192]{2,1,0:T(8,128)}, f32[16,672,192]{2,1,0:T(8,128)S(1)}, u32[]{:S(2)}) copy-start(f32[16,672,192]{2,1,0:T(8,128)S(1)} %maximum_convert_fusion.1) | copy-start | bytes 24772612
  520.0 28.0 %copy-start.7 = (bf16[16,288,192]{2,1,0:T(8,128)(2,1)}, bf16[16,288,192]{2,1,0:T(8,128)(2,1)S(1)}, u32[]{:S(2)}) copy-start(bf16[16,288,192]{2,1,0:T(8,128)(2,1)S(1)} %fusion.31) | copy-start | bytes 5308420
  522.2 35.8 %collective-permute-start.4 = (bf16[16,192,192]{2,1,0:T(8,128)(2,1)}, bf16[16,192,192]{2,1,0:T(8,128)(2,1)}, u32[]{:S(2)}, u32[]{:S(2)}) collective-permute-start(bf16[16,192,192]{2,1,0:T(8,128)(2,1)} %get-tuple-element.41), channel_id=1, source_target_pairs={{0,1},{1,2},{2,3},{3,4},{4,5},{5,6},{6,7},{7,8},{8,9},{9,10},{10,1... | collective-permute-start | bytes 3538952 | tf_op jit(solution)/shard_map/ppermute | solution.py:30
  522.2 35.8 %collective-permute-start.5 = (bf16[16,192,192]{2,1,0:T(8,128)(2,1)}, bf16[16,192,192]{2,1,0:T(8,128)(2,1)}, u32[]{:S(2)}, u32[]{:S(2)}) collective-permute-start(bf16[16,192,192]{2,1,0:T(8,128)(2,1)} %get-tuple-element.42), channel_id=1, source_target_pairs={{1,0},{2,1},{3,2},{4,3},{5,4},{6,5},{7,6},{8,7},{9,8},{10,9},{11,1... | collective-permute-start | bytes 3538952 | tf_op jit(solution)/shard_map/ppermute | solution.py:33
  552.0 24.3 %collective-permute-start.10 = (bf16[16,192,192]{2,1,0:T(8,128)(2,1)}, bf16[16,192,192]{2,1,0:T(8,128)(2,1)S(1)}, u32[]{:S(2)}, u32[]{:S(2)}) collective-permute-start(bf16[16,192,192]{2,1,0:T(8,128)(2,1)} %get-tuple-element.47), channel_id=1, source_target_pairs={{0,1},{1,2},{2,3},{3,4},{4,5},{5,6},{6,7},{7,8},{8,9},{9,10},{10,1... | collective-permute-start | bytes 3538952 | tf_op jit(solution)/shard_map/ppermute | solution.py:30
  552.0 24.3 %collective-permute-start.11 = (bf16[16,192,192]{2,1,0:T(8,128)(2,1)}, bf16[16,192,192]{2,1,0:T(8,128)(2,1)}, u32[]{:S(2)}, u32[]{:S(2)}) collective-permute-start(bf16[16,192,192]{2,1,0:T(8,128)(2,1)} %get-tuple-element.48), channel_id=1, source_target_pairs={{1,0},{2,1},{3,2},{4,3},{5,4},{6,5},{7,6},{8,7},{9,8},{10,9},{11,1... | collective-permute-start | bytes 3538952 | tf_op jit(solution)/shard_map/ppermute | solution.py:33
  589.5 20.2 %copy-start.13 = (f32[8,288,192]{2,1,0:T(8,128)S(1)}, f32[8,288,192]{2,1,0:T(8,128)}, u32[]{:S(2)}) copy-start(f32[8,288,192]{2,1,0:T(8,128)} %copy-done.12) | copy-start | bytes 5308420
  612.7 20.0 %copy-start.11 = (f32[8,288,192]{2,1,0:T(8,128)S(1)}, f32[8,288,192]{2,1,0:T(8,128)}, u32[]{:S(2)}) copy-start(f32[8,288,192]{2,1,0:T(8,128)} %copy-done.10) | copy-start | bytes 5308420
  (5 other events, 34.7 us)
Sparse Core Ops, SparseCore 0:
  32.9 86.0 all-reduce.3
where the time goes:
time: 649 us; the launch traced here: 644 us
  blocking collectives  286 us (44%)
  other arithmetic  157 us (24%)
  local copies, waits for them, and re-layouts  79.4 us (12%)
  waiting for transfers between devices  66.5 us (10%)
  starting transfers between devices  39.3 us (6%)
  between operations  15.5 us (2%)
    psum x1, blocking collectives, body(): totals = lax.psum(local_sums, 'domain')  286 us
    convert_element_type x4, other arithmetic, solve_block(): potential.astype(jnp.bfloat16)  75.7 us
    slice x12, local copies, waits for them, and re-layouts, row_sweep(): jnp.roll(centre, -1, 2)  57.9 us
    psum x1, waiting for transfers between devices, spread(): return lax.psum(block, axis)  40.9 us
    div x2, other arithmetic, row_sweep(): return (beside + coupling * source) / 6.0  40.2 us
    ppermute x6, starting transfers between devices, padded(): lax.ppermute(lax.slice_in_dim(block, 0, width, axis=dim), axis, backward)  39.1 us
    ppermute x6, waiting for transfers between devices, padded(): lax.ppermute(lax.slice_in_dim(block, block.shape[dim] - width, None, axis...  25.4 us
    convert_element_type x6, other arithmetic, solve_block(): padded(potential.astype(jnp.bfloat16), (('domain', 1),), GY)  22.3 us
  transfers between devices with their start and end apart: 13, of which 6 were waited for; matrix products, arithmetic and copies ran while one was open for 17% of the time, Pallas kernels for 0%

commit v1 on v0

v1 whole, which is shorter than its diff:
```python
import functools
import math

import jax
import jax.numpy as jnp
from jax import lax
from jax.experimental import pallas as pl
from jax.experimental.pallas import tpu as pltpu
from jax.sharding import PartitionSpec as P

ORB = 8
STEPS = 2
SWEEPS = 3
GX = 192
GY = 192
GZ = 192


coupling = 4.0 * math.pi
OFFLOAD_WIDTH = 16384


def circulant(width):
    a = lax.broadcasted_iota(jnp.int32, (width, width), 0)
    b = lax.broadcasted_iota(jnp.int32, (width, width), 1)
    gap = (a - b + width) % width
    return ((gap == 1) | (gap == width - 1)).astype(jnp.bfloat16)


def stencil(y0, v, lo, hi, q, t_ref, wide):
    row_count = v.shape[0]
    halo = lo.shape[0]
    wide[0:halo, :] = lo
    wide[halo : halo + row_count, :] = v
    wide[halo + row_count : 2 * halo + row_count, :] = hi
    beside = wide[0:row_count, :] + wide[2 * halo : 2 * halo + row_count, :]
    down = wide[halo - 1 : halo - 1 + row_count, :]
    up = wide[halo + 1 : halo + 1 + row_count, :]
    down_wrap = wide[2 * halo - 1 : 2 * halo - 1 + row_count, :]
    up_wrap = wide[1 : 1 + row_count, :]
    y = lax.broadcasted_iota(jnp.int32, v.shape, 0) + y0
    for _ in range((row_count + GY - 2) // GY):
        y = jnp.where(y >= GY, y - GY, y)
    beside = beside + jnp.where(y == 0, down_wrap, down)
    beside = beside + jnp.where(y == GY - 1, up_wrap, up)
    high = v.astype(jnp.bfloat16)
    low = (v - high.astype(jnp.float32)).astype(jnp.bfloat16)
    tmat = t_ref[...]
    beside = beside + jnp.dot(high, tmat, preferred_element_type=jnp.float32)
    beside = beside + jnp.dot(low, tmat, preferred_element_type=jnp.float32)
    return (beside + coupling * q) * (1.0 / 6.0)


def sweep_kernel(final, sc_ref, v_ref, lo_ref, hi_ref, p_ref, t_ref, c_ref, *rest):
    y0 = sc_ref[0]
    part = p_ref[...].astype(jnp.float32)
    row_count = part.shape[0]
    halo = lo_ref.shape[-2]
    if final:
        acc_ref, wide = rest

        @pl.when(pl.program_id(0) == 0)
        def _():
            acc_ref[...] = jnp.zeros_like(acc_ref)

    else:
        out_ref, fwd_ref, bwd_ref, wide = rest
    for j in range(v_ref.shape[0]):
        q = part * t_ref[j]
        new = stencil(
            y0,
            v_ref[j].astype(jnp.float32),
            lo_ref[j].astype(jnp.float32),
            hi_ref[j].astype(jnp.float32),
            q,
            c_ref,
            wide,
        )
        if final:
            acc_ref[j] = acc_ref[j] + new * part
        else:
            out_ref[j] = new
            fwd_ref[j] = new[row_count - halo : row_count].astype(jnp.bfloat16)
            bwd_ref[j] = new[0:halo].astype(jnp.bfloat16)


def sweep_call(final, v, from_warm, lo, hi, partner, targets, tmat, scalars):
    orb, tgt, halo, width = lo.shape
    row_count = targets.shape[1]
    if from_warm:
        v_spec = pl.BlockSpec(
            (None, None, tgt, row_count, width), lambda i, sc: (sc[1], i, 0, 0, 0)
        )
    else:
        v_spec = pl.BlockSpec((None, tgt, row_count, width), lambda i, sc: (i, 0, 0, 0))
    h_spec = pl.BlockSpec((None, tgt, halo, width), lambda i, sc: (i, 0, 0, 0))
    p_spec = pl.BlockSpec((None, row_count, width), lambda i, sc: (sc[2] + i, 0, 0))
    t_spec = pl.BlockSpec((tgt, row_count, width), lambda i, sc: (0, 0, 0))
    c_spec = pl.BlockSpec((width, width), lambda i, sc: (0, 0))
    cells = orb * tgt * row_count * width
    if final:
        out_shape = jax.ShapeDtypeStruct((tgt, row_count, width), jnp.float32)
        out_specs = pl.BlockSpec((tgt, row_count, width), lambda i, sc: (0, 0, 0))
        out_bytes = tgt * row_count * width * 4
    else:
        out_shape = (
            jax.ShapeDtypeStruct((orb, tgt, row_count, width), jnp.float32),
            jax.ShapeDtypeStruct((orb, tgt, halo, width), jnp.bfloat16),
            jax.ShapeDtypeStruct((orb, tgt, halo, width), jnp.bfloat16),
        )
        out_specs = (
            pl.BlockSpec((None, tgt, row_count, width), lambda i, sc: (i, 0, 0, 0)),
            h_spec,
            h_spec,
        )
        out_bytes = cells * 4 + 2 * orb * tgt * halo * width * 2
    in_bytes = (
        cells * v.dtype.itemsize
        + 2 * orb * tgt * halo * width * 2
        + orb * row_count * width * 2
        + tgt * row_count * width * 4
    )
    grid_spec = pltpu.PrefetchScalarGridSpec(
        num_scalar_prefetch=1,
        grid=(orb,),
        in_specs=[v_spec, h_spec, h_spec, p_spec, t_spec, c_spec],
        out_specs=out_specs,
        scratch_shapes=[pltpu.VMEM((row_count + 2 * halo, width), jnp.float32)],
    )
    return pl.pallas_call(
        functools.partial(sweep_kernel, final),
        grid_spec=grid_spec,
        out_shape=out_shape,
        compiler_params=pltpu.CompilerParams(dimension_semantics=("arbitrary",)),
        cost_estimate=pl.CostEstimate(
            flops=cells * (4 * width + 24),
            transcendentals=0,
            bytes_accessed=in_bytes + out_bytes,
        ),
    )(scalars, v, lo, hi, partner, targets, tmat)


def exchange_halos(fwd, bwd):
    count = lax.axis_size("domain")
    forward = [(k, (k + 1) % count) for k in range(count)]
    backward = [((k + 1) % count, k) for k in range(count)]
    return lax.ppermute(fwd, "domain", forward), lax.ppermute(bwd, "domain", backward)


def solve_stream(warm_start, s, partner, pbase, targets, tmat, y0):
    row_count = targets.shape[1]
    halo = GY
    warm_block = lax.dynamic_index_in_dim(warm_start, s, 0, keepdims=False)
    lo, hi = exchange_halos(
        warm_block[:, :, row_count - halo :], warm_block[:, :, :halo]
    )
    scalars = jnp.stack([y0, s, pbase]).astype(jnp.int32)
    potential, fwd, bwd = sweep_call(
        False, warm_start, True, lo, hi, partner, targets, tmat, scalars
    )
    for sweep_index in range(1, SWEEPS - 1):
        lo, hi = exchange_halos(fwd, bwd)
        potential, fwd, bwd = sweep_call(
            False, potential, False, lo, hi, partner, targets, tmat, scalars
        )
    lo, hi = exchange_halos(fwd, bwd)
    return sweep_call(True, potential, False, lo, hi, partner, targets, tmat, scalars)


def pair_sums(block, targets):
    part = block.astype(jnp.float32)
    return jnp.sum(part[:, None] * targets[None], axis=(2, 3))


def mean_term(block, means):
    part = block.astype(jnp.float32)
    total = None
    for i in range(block.shape[0]):
        term = means[i][:, None, None] * part[i][None]
        total = term if total is None else total + term
    return total


def body(targets, partner_pool, owners, warm_start):
    row_count = targets.shape[1]
    cell_count = GX * GY * GZ
    domain = lax.axis_index("domain")
    band = lax.axis_index("band")
    y0 = (domain * row_count) % GY
    s_own = jnp.where(owners[0] == band, 0, 1).astype(jnp.int32)
    s_rem = 1 - s_own
    own_block = lax.dynamic_slice_in_dim(partner_pool, s_own * ORB, ORB, 0)
    rem_block = lax.ppermute(own_block, "band", [(0, 1), (1, 0)])
    tmat = circulant(targets.shape[2])
    zero = jnp.zeros((), jnp.int32)

    sums = jnp.stack([pair_sums(own_block, targets), pair_sums(rem_block, targets)])
    padded = jnp.zeros((OFFLOAD_WIDTH,), jnp.float32).at[: sums.size].set(sums.reshape(-1))
    totals = lax.psum(padded, "domain")[: sums.size].reshape(sums.shape)
    means = totals / cell_count

    own_acc = solve_stream(warm_start, s_own, partner_pool, s_own * ORB, targets, tmat, y0)
    rem_acc = solve_stream(warm_start, s_rem, rem_block, zero, targets, tmat, y0)
    correction = mean_term(own_block, means[0]) + mean_term(rem_block, means[1])
    return (0.5 * coupling) * correction - (own_acc + rem_acc)


def solution(mesh):
    return jax.shard_map(
        body,
        mesh=mesh,
        in_specs=(
            P("band", "domain", None),
            P("band", "domain", None),
            P(),
            P(None, None, "band", "domain", None),
        ),
        out_specs=P("band", "domain", None),
        check_vma=False,
    )
```

time: 649 us -> 1110 us (1.71)
  waiting for transfers between devices: 66.5 us -> 962 us
  blocking collectives: 286 us -> 0 us
  other arithmetic: 157 us -> 12.6 us
  Pallas kernels: 0 us -> 69.5 us
  local copies, waits for them, and re-layouts: 79.4 us -> 14.1 us
    psum x1, waiting for transfers between devices: 40.9 us -> 916 us  [body(): totals = lax.psum(padded, 'domain')[:sums.size].reshape(sums.shape)]
    psum x1 -> x0, blocking collectives: 286 us -> none  [body(): totals = lax.psum(local_sums, 'domain')]
    convert_element_type x12 -> x3, other arithmetic: 102 us -> 4.9 us  [the longest x2 4.15 us: pair_sums(): part = block.astype(jnp.float32)]
    slice x20 -> x2, local copies, waits for them, and re-layouts: 76.9 us -> 3.79 us  [solve_stream(): warm_block[:, :, :halo]]
    pallas_call x0 -> x6, Pallas kernels: none -> 69.5 us  [sweep_call(): pl.pallas_call(functools.partial(sweep_kernel, final), grid_spec=grid_spe...]
    div x4 -> x1, other arithmetic: 40.2 us -> 0.68 us  [body(): means = totals / cell_count]
    ppermute x12 -> x13, waiting for transfers between devices: 25.6 us -> 45.7 us  [the longest x1 40.2 us: body(): rem_block = lax.ppermute(own_block, 'band', [(0, 1), (1, 0)])]
    ppermute x12 -> x13, starting transfers between devices: 39.3 us -> 39.6 us  [the longest x6 39 us: exchange_halos(): lax.ppermute(bwd, 'domain', backward)]
  transfers between devices with their start and end apart: 13 -> 14, of which waited for: 6 -> 3; matrix products, arithmetic and copies ran while one was open for 17% -> 2% of each run, Pallas kernels for 0% -> 5%
where the time goes in v1:
time: 1110 us
  waiting for transfers between devices  962 us (87%)
  Pallas kernels  69.5 us (6%)
  starting transfers between devices  39.6 us (4%)
  between operations  14.2 us (1%)
  local copies, waits for them, and re-layouts  14.1 us (1%)
  other arithmetic  12.6 us (1%)
    psum x1, waiting for transfers between devices, body(): totals = lax.psum(padded, 'domain')[:sums.size].reshape(sums.shape)  916 us
    pallas_call x6, Pallas kernels, sweep_call(): pl.pallas_call(functools.partial(sweep_kernel, final), grid_spec=grid_spe...  69.5 us
    ppermute x1, waiting for transfers between devices, body(): rem_block = lax.ppermute(own_block, 'band', [(0, 1), (1, 0)])  40.2 us
    ppermute x6, starting transfers between devices, exchange_halos(): lax.ppermute(bwd, 'domain', backward)  39 us
  transfers between devices with their start and end apart: 14, of which 3 were waited for; matrix products, arithmetic and copies ran while one was open for 2% of the time, Pallas kernels for 5%

profile of v1, /device:TPU:16, one launch (start us, length us, event | category | flops | bytes accessed | tf_op | source)
XLA Modules:
  0.0 1112.0 jit_solution(8369599626041585570)
XLA Ops:
  7.2 2.7 dynamic-slice_bitcast_fusion
  9.9 1.9 fusion.9
  11.8 8.2 collective-permute-start.2
  20.0 1.9 fusion.8
  21.9 6.0 collective-permute-start.8
  27.8 2.6 fusion.7
  33.0 5.5 collective-permute-done.1.lo_ref
  38.5 11.6 %shard_map.46 = (f32[8,2,288,192]{3,2,1,0:T(8,128)}, bf16[8,2,192,192]{3,2,1,0:T(8,128)(2,1)}, bf16[8,2,192,192]{3,2,1,0:T(8,128)(2,1)}) custom-call(s32[3]{0:T(128)} %pad_add_fusion.sc_ref, bf16[2,8,2,288,192]{4,3,2,1,0:T(8,128)(2,1)} %v_ref.3, bf16[8,2,192,192]{3,2,1,0:T(8,128)(2,1)} %collective-permute-done.1.lo_ref, ...), custom_call_target="tpu_custom_call" | custom-call | flops 700710912 | bytes 11354112 | tf_op jit(solution)/shard_map/pallas_call | solution.py:130
  50.1 6.0 collective-permute-start.4
  56.2 40.2 %collective-permute-done.p_ref = bf16[8,288,192]{2,1,0:T(8,128)(2,1)S(1)} collective-permute-done((bf16[8,288,192]{2,1,0:T(8,128)(2,1)}, bf16[8,288,192]{2,1,0:T(8,128)(2,1)S(1)}, u32[]{:S(2)}, u32[]{:S(2)}) %collective-permute-start) | collective-permute-done | bytes 884768 | tf_op jit(solution)/shard_map/ppermute | solution.py:193
  97.4 11.6 %shard_map.49 = (f32[8,2,288,192]{3,2,1,0:T(8,128)}, bf16[8,2,192,192]{3,2,1,0:T(8,128)(2,1)}, bf16[8,2,192,192]{3,2,1,0:T(8,128)(2,1)}) custom-call(s32[3]{0:T(128)} %pad_add_fusion.1.sc_ref, bf16[2,8,2,288,192]{4,3,2,1,0:T(8,128)(2,1)} %v_ref.3, bf16[8,2,192,192]{3,2,1,0:T(8,128)(2,1)} %collective-permute-done.7.lo_ref, ...), custom_call_target="tpu_custom_call" | custom-call | flops 700710912 | bytes 11354112 | tf_op jit(solution)/shard_map/pallas_call | solution.py:130
  109.0 6.8 collective-permute-start.10
  115.9 1.2 slice_bitcast_fusion.15
  117.8 1.6 convert_element_type.22
  119.4 12.0 %shard_map.47 = (f32[8,2,288,192]{3,2,1,0:T(8,128)}, bf16[8,2,192,192]{3,2,1,0:T(8,128)(2,1)}, bf16[8,2,192,192]{3,2,1,0:T(8,128)(2,1)}) custom-call(s32[3]{0:T(128)} %pad_add_fusion.sc_ref, f32[8,2,288,192]{3,2,1,0:T(8,128)} %get-tuple-element.29.v_ref, bf16[8,2,192,192]{3,2,1,0:T(8,128)(2,1)} %collective-permute-done.3.lo_ref, ...), custom_call_target="tpu_custom_call" | custom-call | flops 700710912 | bytes 13123584 | tf_op jit(solution)/shard_map/pallas_call | solution.py:130
  131.4 6.0 collective-permute-start.6
  137.4 12.2 %shard_map.50 = (f32[8,2,288,192]{3,2,1,0:T(8,128)}, bf16[8,2,192,192]{3,2,1,0:T(8,128)(2,1)}, bf16[8,2,192,192]{3,2,1,0:T(8,128)(2,1)}) custom-call(s32[3]{0:T(128)} %pad_add_fusion.1.sc_ref, f32[8,2,288,192]{3,2,1,0:T(8,128)} %get-tuple-element.35.v_ref, bf16[8,2,192,192]{3,2,1,0:T(8,128)(2,1)} %collective-permute-done.9.lo_ref, ...), custom_call_target="tpu_custom_call" | custom-call | flops 700710912 | bytes 13123584 | tf_op jit(solution)/shard_map/pallas_call | solution.py:130
  149.6 6.0 collective-permute-start.12
  155.6 2.6 multiply_reduce_fusion.1
  159.2 2.9 slice_bitcast_fusion.7
  162.1 916.3 %all-reduce.3.cloned.1.call-done = f32[16384]{0:T(1024)} async-done(((f32[16384]{0:T(1024)}), f32[16384]{0:T(1024)}) %all-reduce.3.cloned.1.call-update) | async-done | bytes 65552 | tf_op jit(solution)/shard_map/psum | solution.py:199
  1079.8 11.0 shard_map.48
  1090.8 11.1 shard_map.51
  1102.0 3.2 add_subtract_fusion
  (52 shorter events, 6.9 us)
Async XLA Ops:
  6.5 1071.8 %all-reduce.3.cloned.1.call-start = ((), (), s32[]{:S(2)}) async-start(), calls=%async_computation | async-start | bytes 131072 | tf_op jit(solution)/shard_map/psum | solution.py:199
  11.8 26.7 %collective-permute-start.1 = (bf16[8,2,192,192]{3,2,1,0:T(8,128)(2,1)}, bf16[8,2,192,192]{3,2,1,0:T(8,128)(2,1)}, u32[]{:S(2)}, u32[]{:S(2)}) collective-permute-start(bf16[8,2,192,192]{3,2,1,0:T(8,128)(2,1)} %get-tuple-element.66), channel_id=1, source_target_pairs={{0,1},{1,2},{2,3},{3,4},{4,5},{5,6},{6,7},{7,8},{8,9},{9,10},{10,1... | collective-permute-start | bytes 3538952 | tf_op jit(solution)/shard_map/ppermute | solution.py:147
  11.8 26.7 %collective-permute-start.2 = (bf16[8,2,192,192]{3,2,1,0:T(8,128)(2,1)}, bf16[8,2,192,192]{3,2,1,0:T(8,128)(2,1)}, u32[]{:S(2)}, u32[]{:S(2)}) collective-permute-start(bf16[8,2,192,192]{3,2,1,0:T(8,128)(2,1)} %get-tuple-element.65), channel_id=1, source_target_pairs={{1,0},{2,1},{3,2},{4,3},{5,4},{6,5},{7,6},{8,7},{9,8},{10,9},{11,1... | collective-permute-start | bytes 3538952 | tf_op jit(solution)/shard_map/ppermute | solution.py:147
  21.9 74.5 %collective-permute-start.7 = (bf16[8,2,192,192]{3,2,1,0:T(8,128)(2,1)}, bf16[8,2,192,192]{3,2,1,0:T(8,128)(2,1)}, u32[]{:S(2)}, u32[]{:S(2)}) collective-permute-start(bf16[8,2,192,192]{3,2,1,0:T(8,128)(2,1)} %get-tuple-element.64), channel_id=1, source_target_pairs={{0,1},{1,2},{2,3},{3,4},{4,5},{5,6},{6,7},{7,8},{8,9},{9,10},{10,1... | collective-permute-start | bytes 3538952 | tf_op jit(solution)/shard_map/ppermute | solution.py:147
  21.9 74.5 %collective-permute-start.8 = (bf16[8,2,192,192]{3,2,1,0:T(8,128)(2,1)}, bf16[8,2,192,192]{3,2,1,0:T(8,128)(2,1)}, u32[]{:S(2)}, u32[]{:S(2)}) collective-permute-start(bf16[8,2,192,192]{3,2,1,0:T(8,128)(2,1)} %get-tuple-element.63), channel_id=1, source_target_pairs={{1,0},{2,1},{3,2},{4,3},{5,4},{6,5},{7,6},{8,7},{9,8},{10,9},{11,1... | collective-permute-start | bytes 3538952 | tf_op jit(solution)/shard_map/ppermute | solution.py:147
  30.4 65.9 %collective-permute-start = (bf16[8,288,192]{2,1,0:T(8,128)(2,1)}, bf16[8,288,192]{2,1,0:T(8,128)(2,1)S(1)}, u32[]{:S(2)}, u32[]{:S(2)}) collective-permute-start(bf16[8,288,192]{2,1,0:T(8,128)(2,1)} %get-tuple-element.44), channel_id=1, source_target_pairs={{0,128},{128,0},{1,129},{129,1},{2,130},{130,2},{3,131},{131,3},{4... | collective-permute-start | bytes 2654216 | tf_op jit(solution)/shard_map/ppermute | solution.py:193
  50.1 69.2 %collective-permute-start.3 = (bf16[8,2,192,192]{3,2,1,0:T(8,128)(2,1)}, bf16[8,2,192,192]{3,2,1,0:T(8,128)(2,1)}, u32[]{:S(2)}, u32[]{:S(2)}) collective-permute-start(bf16[8,2,192,192]{3,2,1,0:T(8,128)(2,1)} %get-tuple-element.30), channel_id=1, source_target_pairs={{0,1},{1,2},{2,3},{3,4},{4,5},{5,6},{6,7},{7,8},{8,9},{9,10},{10,1... | collective-permute-start | bytes 3538952 | tf_op jit(solution)/shard_map/ppermute | solution.py:147
  50.1 69.2 %collective-permute-start.4 = (bf16[8,2,192,192]{3,2,1,0:T(8,128)(2,1)}, bf16[8,2,192,192]{3,2,1,0:T(8,128)(2,1)}, u32[]{:S(2)}, u32[]{:S(2)}) collective-permute-start(bf16[8,2,192,192]{3,2,1,0:T(8,128)(2,1)} %get-tuple-element.31), channel_id=1, source_target_pairs={{1,0},{2,1},{3,2},{4,3},{5,4},{6,5},{7,6},{8,7},{9,8},{10,9},{11,1... | collective-permute-start | bytes 3538952 | tf_op jit(solution)/shard_map/ppermute | solution.py:147
  96.3 1.1 copy-start.1
  109.0 28.3 %collective-permute-start.9 = (bf16[8,2,192,192]{3,2,1,0:T(8,128)(2,1)}, bf16[8,2,192,192]{3,2,1,0:T(8,128)(2,1)}, u32[]{:S(2)}, u32[]{:S(2)}) collective-permute-start(bf16[8,2,192,192]{3,2,1,0:T(8,128)(2,1)} %get-tuple-element.36), channel_id=1, source_target_pairs={{0,1},{1,2},{2,3},{3,4},{4,5},{5,6},{6,7},{7,8},{8,9},{9,10},{10,1... | collective-permute-start | bytes 3538952 | tf_op jit(solution)/shard_map/ppermute | solution.py:147
  109.0 28.3 %collective-permute-start.10 = (bf16[8,2,192,192]{3,2,1,0:T(8,128)(2,1)}, bf16[8,2,192,192]{3,2,1,0:T(8,128)(2,1)}, u32[]{:S(2)}, u32[]{:S(2)}) collective-permute-start(bf16[8,2,192,192]{3,2,1,0:T(8,128)(2,1)} %get-tuple-element.37), channel_id=1, source_target_pairs={{1,0},{2,1},{3,2},{4,3},{5,4},{6,5},{7,6},{8,7},{9,8},{10,9},{11,1... | collective-permute-start | bytes 3538952 | tf_op jit(solution)/shard_map/ppermute | solution.py:147
  115.9 1.9 copy-start.2
  131.4 948.4 %collective-permute-start.5 = (bf16[8,2,192,192]{3,2,1,0:T(8,128)(2,1)}, bf16[8,2,192,192]{3,2,1,0:T(8,128)(2,1)}, u32[]{:S(2)}, u32[]{:S(2)}) collective-permute-start(bf16[8,2,192,192]{3,2,1,0:T(8,128)(2,1)} %get-tuple-element.33), channel_id=1, source_target_pairs={{0,1},{1,2},{2,3},{3,4},{4,5},{5,6},{6,7},{7,8},{8,9},{9,10},{10,1... | collective-permute-start | bytes 3538952 | tf_op jit(solution)/shard_map/ppermute | solution.py:147
  131.4 948.4 %collective-permute-start.6 = (bf16[8,2,192,192]{3,2,1,0:T(8,128)(2,1)}, bf16[8,2,192,192]{3,2,1,0:T(8,128)(2,1)}, u32[]{:S(2)}, u32[]{:S(2)}) collective-permute-start(bf16[8,2,192,192]{3,2,1,0:T(8,128)(2,1)} %get-tuple-element.34), channel_id=1, source_target_pairs={{1,0},{2,1},{3,2},{4,3},{5,4},{6,5},{7,6},{8,7},{9,8},{10,9},{11,1... | collective-permute-start | bytes 3538952 | tf_op jit(solution)/shard_map/ppermute | solution.py:147
  137.4 18.2 %copy-start = (f32[2,288,192]{2,1,0:T(8,128)S(1)}, f32[2,288,192]{2,1,0:T(8,128)}, u32[]{:S(2)}) copy-start(f32[2,288,192]{2,1,0:T(8,128)} %t_ref.11) | copy-start | bytes 1327108
  149.6 941.2 %collective-permute-start.11 = (bf16[8,2,192,192]{3,2,1,0:T(8,128)(2,1)}, bf16[8,2,192,192]{3,2,1,0:T(8,128)(2,1)}, u32[]{:S(2)}, u32[]{:S(2)}) collective-permute-start(bf16[8,2,192,192]{3,2,1,0:T(8,128)(2,1)} %get-tuple-element.39), channel_id=1, source_target_pairs={{0,1},{1,2},{2,3},{3,4},{4,5},{5,6},{6,7},{7,8},{8,9},{9,10},{10,1... | collective-permute-start | bytes 3538952 | tf_op jit(solution)/shard_map/ppermute | solution.py:147
  149.6 941.2 %collective-permute-start.12 = (bf16[8,2,192,192]{3,2,1,0:T(8,128)(2,1)}, bf16[8,2,192,192]{3,2,1,0:T(8,128)(2,1)}, u32[]{:S(2)}, u32[]{:S(2)}) collective-permute-start(bf16[8,2,192,192]{3,2,1,0:T(8,128)(2,1)} %get-tuple-element.40), channel_id=1, source_target_pairs={{1,0},{2,1},{3,2},{4,3},{5,4},{6,5},{7,6},{8,7},{9,8},{10,9},{11,1... | collective-permute-start | bytes 3538952 | tf_op jit(solution)/shard_map/ppermute | solution.py:147
  1090.8 11.2 %copy-start.3 = (f32[2,288,192]{2,1,0:T(8,128)S(1)}, f32[2,288,192]{2,1,0:T(8,128)}, u32[]{:S(2)}) copy-start(f32[2,288,192]{2,1,0:T(8,128)} %shard_map.48) | copy-start | bytes 1327108
  1090.8 11.2 %copy-start.4 = (f32[288,192]{1,0:T(8,128)S(1)}, f32[288,192]{1,0:T(8,128)}, u32[]{:S(2)}) copy-start(f32[288,192]{1,0:T(8,128)} %get-tuple-element.49) | copy-start | bytes 663556
  1090.8 11.2 %copy-start.5 = (f32[288,192]{1,0:T(8,128)S(1)}, f32[288,192]{1,0:T(8,128)}, u32[]{:S(2)}) copy-start(f32[288,192]{1,0:T(8,128)} %get-tuple-element.50) | copy-start | bytes 663556
  1090.8 11.2 %copy-start.6 = (f32[288,192]{1,0:T(8,128)S(1)}, f32[288,192]{1,0:T(8,128)}, u32[]{:S(2)}) copy-start(f32[288,192]{1,0:T(8,128)} %get-tuple-element.51) | copy-start | bytes 663556
  1090.8 11.2 %copy-start.7 = (f32[288,192]{1,0:T(8,128)S(1)}, f32[288,192]{1,0:T(8,128)}, u32[]{:S(2)}) copy-start(f32[288,192]{1,0:T(8,128)} %get-tuple-element.52) | copy-start | bytes 663556
  1090.8 11.2 %copy-start.8 = (f32[288,192]{1,0:T(8,128)S(1)}, f32[288,192]{1,0:T(8,128)}, u32[]{:S(2)}) copy-start(f32[288,192]{1,0:T(8,128)} %get-tuple-element.53) | copy-start | bytes 663556
  1090.8 11.2 %copy-start.9 = (f32[288,192]{1,0:T(8,128)S(1)}, f32[288,192]{1,0:T(8,128)}, u32[]{:S(2)}) copy-start(f32[288,192]{1,0:T(8,128)} %get-tuple-element.54) | copy-start | bytes 663556
Sparse Core Ops, SparseCore 0:
  159.3 919.0 all-reduce.2

commit v2 on v1

--- a/solution.py
+++ b/solution.py
@@ -17,7 +17,6 @@
 
 
 coupling = 4.0 * math.pi
-OFFLOAD_WIDTH = 16384
 
 
 def circulant(width):
@@ -167,6 +166,35 @@
     return sweep_call(True, potential, False, lo, hi, partner, targets, tmat, scalars)
 
 
+def butterfly_sum(x, axis):
+    count = lax.axis_size(axis)
+    step = 1
+    while step < count:
+        pairs = [(k, k ^ step) for k in range(count)]
+        x = x + lax.ppermute(x, axis, pairs)
+        step *= 2
+    return x
+
+
+def swap_over_y(block, mesh_shape):
+    bands, domains = mesh_shape
+    lanes = domains // 2
+    def index(y, rest):
+        return (y // 2) * domains + (y % 2) * lanes + rest
+    ring = 2 * bands
+    def shift(direction):
+        return [
+            (index(y, rest), index((y + direction) % ring, rest))
+            for y in range(ring)
+            for rest in range(lanes)
+        ]
+    half = block.shape[0] // 2
+    axes = ("band", "domain")
+    plus = lax.ppermute(lax.ppermute(block[:half], axes, shift(1)), axes, shift(1))
+    minus = lax.ppermute(lax.ppermute(block[half:], axes, shift(-1)), axes, shift(-1))
+    return jnp.concatenate([plus, minus], axis=0)
+
+
 def pair_sums(block, targets):
     part = block.astype(jnp.float32)
     return jnp.sum(part[:, None] * targets[None], axis=(2, 3))
@@ -190,14 +218,12 @@
     s_own = jnp.where(owners[0] == band, 0, 1).astype(jnp.int32)
     s_rem = 1 - s_own
     own_block = lax.dynamic_slice_in_dim(partner_pool, s_own * ORB, ORB, 0)
-    rem_block = lax.ppermute(own_block, "band", [(0, 1), (1, 0)])
+    rem_block = swap_over_y(own_block, (lax.axis_size("band"), lax.axis_size("domain")))
     tmat = circulant(targets.shape[2])
     zero = jnp.zeros((), jnp.int32)
 
     sums = jnp.stack([pair_sums(own_block, targets), pair_sums(rem_block, targets)])
-    padded = jnp.zeros((OFFLOAD_WIDTH,), jnp.float32).at[: sums.size].set(sums.reshape(-1))
-    totals = lax.psum(padded, "domain")[: sums.size].reshape(sums.shape)
-    means = totals / cell_count
+    means = butterfly_sum(sums, "domain") / cell_count
 
     own_acc = solve_stream(warm_start, s_own, partner_pool, s_own * ORB, targets, tmat, y0)
     rem_acc = solve_stream(warm_start, s_rem, rem_block, zero, targets, tmat, y0)

time: 1110 us -> 218 us (0.20)
  waiting for transfers between devices: 962 us -> 52.5 us
  starting transfers between devices: 39.6 us -> 66.7 us
  between operations: 14.2 us -> 0.94 us
    psum x1 -> x0, waiting for transfers between devices: 916 us -> none  [body(): totals = lax.psum(padded, 'domain')[:sums.size].reshape(sums.shape)]
    ppermute x6, starting transfers between devices: 39 us -> 61.8 us  [exchange_halos(): lax.ppermute(bwd, 'domain', backward)]
    ppermute x1 -> x11, waiting for transfers between devices: 40.2 us -> 52.5 us  [the longest x7 31.3 us: butterfly_sum(): x = x + lax.ppermute(x, axis, pairs)]
  transfers between devices with their start and end apart: 14 -> 23, of which waited for: 3 -> 8; matrix products, arithmetic and copies ran while one was open for 2% -> 8% of each run, Pallas kernels for 5% -> 27%
where the time goes in v2:
time: 218 us; the launch traced here: 215 us
  Pallas kernels  69.5 us (32%)
  starting transfers between devices  66.7 us (31%)
  waiting for transfers between devices  52.5 us (24%)
  local copies, waits for them, and re-layouts  16.9 us (8%)
  other arithmetic  8.38 us (4%)
    pallas_call x6, Pallas kernels, sweep_call(): pl.pallas_call(functools.partial(sweep_kernel, final), grid_spec=grid_spe...  69.5 us
    ppermute x6, starting transfers between devices, exchange_halos(): lax.ppermute(bwd, 'domain', backward)  61.8 us
    ppermute x7, waiting for transfers between devices, butterfly_sum(): x = x + lax.ppermute(x, axis, pairs)  31.3 us
    ppermute x1, waiting for transfers between devices, swap_over_y(): lax.ppermute(block[half:], axes, shift(-1))  10.6 us
    ppermute x1, waiting for transfers between devices, swap_over_y(): lax.ppermute(lax.ppermute(block[:half], axes, shift(1)), axes, shift(1))  10.6 us
    unnamed x31, local copies, waits for them, and re-layouts  4.41 us
  transfers between devices with their start and end apart: 23, of which 8 were waited for; matrix products, arithmetic and copies ran while one was open for 8% of the time, Pallas kernels for 27%

profile of v2, /device:TPU:16, one launch (start us, length us, event | category | flops | bytes accessed | tf_op | source)
XLA Modules:
  0.0 214.9 jit_solution(12533685025725731899)
XLA Ops:
  4.1 2.7 %dynamic-slice_bitcast_fusion = (bf16[8,2,288,192]{3,2,1,0:T(8,128)(2,1)S(1)}, bf16[8,2,288,192]{3,2,1,0:T(8,128)(2,1)S(1)}) fusion(bf16[2,8,2,288,192]{4,3,2,1,0:T(8,128)(2,1)} %v_ref.3, s32[]{:T(128)S(6)} %select_n.39, s32[]{:T(128)} %select_n.35), kind=kLoop, calls=%fused_computation.2 | loop fusion | bytes 7077896 | tf_op jit(solution)/shard_map/jit(dynamic_index_in_dim)/squeeze | solution.py:152
  6.8 1.9 fusion.9
  8.7 7.6 %collective-permute-start.12 = (bf16[8,2,192,192]{3,2,1,0:T(8,128)(2,1)}, bf16[8,2,192,192]{3,2,1,0:T(8,128)(2,1)}, u32[]{:S(2)}, u32[]{:S(2)}) collective-permute-start(bf16[8,2,192,192]{3,2,1,0:T(8,128)(2,1)} %get-tuple-element.69), channel_id=1, source_target_pairs={{1,0},{2,1},{3,2},{4,3},{5,4},{6,5},{7,6},{8,7},{9,8},{10,9},{11,1... | collective-permute-start | bytes 3538952 | tf_op jit(solution)/shard_map/ppermute | solution.py:146
  16.3 1.9 fusion.8
  18.3 23.1 %collective-permute-start.18 = (bf16[8,2,192,192]{3,2,1,0:T(8,128)(2,1)}, bf16[8,2,192,192]{3,2,1,0:T(8,128)(2,1)}, u32[]{:S(2)}, u32[]{:S(2)}) collective-permute-start(bf16[8,2,192,192]{3,2,1,0:T(8,128)(2,1)} %get-tuple-element.67), channel_id=1, source_target_pairs={{1,0},{2,1},{3,2},{4,3},{5,4},{6,5},{7,6},{8,7},{9,8},{10,9},{11,1... | collective-permute-start | bytes 3538952 | tf_op jit(solution)/shard_map/ppermute | solution.py:146
  41.3 10.6 %collective-permute-done.2 = bf16[4,288,192]{2,1,0:T(8,128)(2,1)} collective-permute-done((bf16[4,288,192]{2,1,0:T(8,128)(2,1)S(1)}, bf16[4,288,192]{2,1,0:T(8,128)(2,1)}, u32[]{:S(2)}, u32[]{:S(2)}) %collective-permute-start.2) | collective-permute-done | bytes 442400 | tf_op jit(solution)/shard_map/ppermute | solution.py:194
  51.9 10.6 %collective-permute-done.1 = bf16[4,288,192]{2,1,0:T(8,128)(2,1)S(1)} collective-permute-done((bf16[4,288,192]{2,1,0:T(8,128)(2,1)}, bf16[4,288,192]{2,1,0:T(8,128)(2,1)S(1)}, u32[]{:S(2)}, u32[]{:S(2)}) %collective-permute-start.1) | collective-permute-done | bytes 442400 | tf_op jit(solution)/shard_map/ppermute | solution.py:193
  62.5 2.6 %collective-permute-start.3 = (bf16[4,288,192]{2,1,0:T(8,128)(2,1)}, bf16[4,288,192]{2,1,0:T(8,128)(2,1)}, u32[]{:S(2)}, u32[]{:S(2)}) collective-permute-start(bf16[4,288,192]{2,1,0:T(8,128)(2,1)} %collective-permute-done.2), channel_id=1, source_target_pairs={{0,192},{1,193},{2,194},{3,195},{4,196},{5,197},{6,198},{7,199},{8... | collective-permute-start | bytes 1327112 | tf_op jit(solution)/shard_map/ppermute | solution.py:194
  67.1 11.7 %shard_map.46 = (f32[8,2,288,192]{3,2,1,0:T(8,128)}, bf16[8,2,192,192]{3,2,1,0:T(8,128)(2,1)}, bf16[8,2,192,192]{3,2,1,0:T(8,128)(2,1)}) custom-call(s32[3]{0:T(128)} %pad_add_fusion.sc_ref, bf16[2,8,2,288,192]{4,3,2,1,0:T(8,128)(2,1)} %v_ref.3, bf16[8,2,192,192]{3,2,1,0:T(8,128)(2,1)} %collective-permute-done.11.lo_ref, ...), custom_call_target="tpu_custom_call" | custom-call | flops 700710912 | bytes 11354112 | tf_op jit(solution)/shard_map/pallas_call | solution.py:129
  78.8 13.4 %collective-permute-start.14 = (bf16[8,2,192,192]{3,2,1,0:T(8,128)(2,1)}, bf16[8,2,192,192]{3,2,1,0:T(8,128)(2,1)}, u32[]{:S(2)}, u32[]{:S(2)}) collective-permute-start(bf16[8,2,192,192]{3,2,1,0:T(8,128)(2,1)} %get-tuple-element.19), channel_id=1, source_target_pairs={{1,0},{2,1},{3,2},{4,3},{5,4},{6,5},{7,6},{8,7},{9,8},{10,9},{11,1... | collective-permute-start | bytes 3538952 | tf_op jit(solution)/shard_map/ppermute | solution.py:146
  94.8 11.5 %shard_map.49 = (f32[8,2,288,192]{3,2,1,0:T(8,128)}, bf16[8,2,192,192]{3,2,1,0:T(8,128)(2,1)}, bf16[8,2,192,192]{3,2,1,0:T(8,128)(2,1)}) custom-call(s32[3]{0:T(128)} %pad_add_fusion.1.sc_ref, bf16[2,8,2,288,192]{4,3,2,1,0:T(8,128)(2,1)} %v_ref.3, bf16[8,2,192,192]{3,2,1,0:T(8,128)(2,1)} %copy-done.8, ...), custom_call_target="tpu_custom_call" | custom-call | flops 700710912 | bytes 11354112 | tf_op jit(solution)/shard_map/pallas_call | solution.py:129
  106.3 6.0 %collective-permute-start.20 = (bf16[8,2,192,192]{3,2,1,0:T(8,128)(2,1)}, bf16[8,2,192,192]{3,2,1,0:T(8,128)(2,1)}, u32[]{:S(2)}, u32[]{:S(2)}) collective-permute-start(bf16[8,2,192,192]{3,2,1,0:T(8,128)(2,1)} %get-tuple-element.25), channel_id=1, source_target_pairs={{1,0},{2,1},{3,2},{4,3},{5,4},{6,5},{7,6},{8,7},{9,8},{10,9},{11,1... | collective-permute-start | bytes 3538952 | tf_op jit(solution)/shard_map/ppermute | solution.py:146
  118.1 12.0 %shard_map.47 = (f32[8,2,288,192]{3,2,1,0:T(8,128)}, bf16[8,2,192,192]{3,2,1,0:T(8,128)(2,1)}, bf16[8,2,192,192]{3,2,1,0:T(8,128)(2,1)}) custom-call(s32[3]{0:T(128)} %pad_add_fusion.sc_ref, f32[8,2,288,192]{3,2,1,0:T(8,128)} %get-tuple-element.17.v_ref, bf16[8,2,192,192]{3,2,1,0:T(8,128)(2,1)} %collective-permute-done.13.lo_ref, ...), custom_call_target="tpu_custom_call" | custom-call | flops 700710912 | bytes 13123584 | tf_op jit(solution)/shard_map/pallas_call | solution.py:129
  130.2 5.8 %collective-permute-start.16 = (bf16[8,2,192,192]{3,2,1,0:T(8,128)(2,1)}, bf16[8,2,192,192]{3,2,1,0:T(8,128)(2,1)}, u32[]{:S(2)}, u32[]{:S(2)}) collective-permute-start(bf16[8,2,192,192]{3,2,1,0:T(8,128)(2,1)} %get-tuple-element.22), channel_id=1, source_target_pairs={{1,0},{2,1},{3,2},{4,3},{5,4},{6,5},{7,6},{8,7},{9,8},{10,9},{11,1... | collective-permute-start | bytes 3538952 | tf_op jit(solution)/shard_map/ppermute | solution.py:146
  137.2 12.2 %shard_map.50 = (f32[8,2,288,192]{3,2,1,0:T(8,128)}, bf16[8,2,192,192]{3,2,1,0:T(8,128)(2,1)}, bf16[8,2,192,192]{3,2,1,0:T(8,128)(2,1)}) custom-call(s32[3]{0:T(128)} %pad_add_fusion.1.sc_ref, f32[8,2,288,192]{3,2,1,0:T(8,128)} %get-tuple-element.23.v_ref, bf16[8,2,192,192]{3,2,1,0:T(8,128)(2,1)} %copy-done.9, ...), custom_call_target="tpu_custom_call" | custom-call | flops 700710912 | bytes 13123584 | tf_op jit(solution)/shard_map/pallas_call | solution.py:129
  149.4 6.0 %collective-permute-start.22 = (bf16[8,2,192,192]{3,2,1,0:T(8,128)(2,1)}, bf16[8,2,192,192]{3,2,1,0:T(8,128)(2,1)}, u32[]{:S(2)}, u32[]{:S(2)}) collective-permute-start(bf16[8,2,192,192]{3,2,1,0:T(8,128)(2,1)} %get-tuple-element.28), channel_id=1, source_target_pairs={{1,0},{2,1},{3,2},{4,3},{5,4},{6,5},{7,6},{8,7},{9,8},{10,9},{11,1... | collective-permute-start | bytes 3538952 | tf_op jit(solution)/shard_map/ppermute | solution.py:146
  156.0 12.8 %collective-permute-done.6 = f32[2,8,2]{1,2,0:T(2,128)S(1)} collective-permute-done((f32[2,8,2]{1,2,0:T(2,128)S(1)}, f32[2,8,2]{1,2,0:T(2,128)S(1)}, u32[]{:S(2)}, u32[]{:S(2)}) %collective-permute-start.6) | collective-permute-done | bytes 160 | tf_op jit(solution)/shard_map/ppermute | solution.py:174
  168.8 7.5 %collective-permute-done.7 = f32[2,8,2]{1,2,0:T(2,128)S(1)} collective-permute-done((f32[2,8,2]{1,2,0:T(2,128)S(1)}, f32[2,8,2]{1,2,0:T(2,128)S(1)}, u32[]{:S(2)}, u32[]{:S(2)}) %collective-permute-start.7) | collective-permute-done | bytes 160 | tf_op jit(solution)/shard_map/ppermute | solution.py:174
  176.3 3.6 %collective-permute-done.8 = f32[2,8,2]{1,2,0:T(2,128)S(1)} collective-permute-done((f32[2,8,2]{1,2,0:T(2,128)S(1)}, f32[2,8,2]{1,2,0:T(2,128)S(1)}, u32[]{:S(2)}, u32[]{:S(2)}) %collective-permute-start.8) | collective-permute-done | bytes 160 | tf_op jit(solution)/shard_map/ppermute | solution.py:174
  181.0 3.9 %collective-permute-done.9 = f32[2,8,2]{1,2,0:T(2,128)S(1)} collective-permute-done((f32[2,8,2]{1,2,0:T(2,128)S(1)}, f32[2,8,2]{1,2,0:T(2,128)S(1)}, u32[]{:S(2)}, u32[]{:S(2)}) %collective-permute-start.9) | collective-permute-done | bytes 160 | tf_op jit(solution)/shard_map/ppermute | solution.py:174
  186.3 2.3 %collective-permute-done.10 = f32[2,8,2]{1,2,0:T(2,128)S(1)} collective-permute-done((f32[2,8,2]{1,2,0:T(2,128)S(1)}, f32[2,8,2]{1,2,0:T(2,128)S(1)}, u32[]{:S(2)}, u32[]{:S(2)}) %collective-permute-start.10) | collective-permute-done | bytes 160 | tf_op jit(solution)/shard_map/ppermute | solution.py:174
  189.6 11.0 %shard_map.48 = f32[2,288,192]{2,1,0:T(8,128)} custom-call(s32[3]{0:T(128)} %pad_add_fusion.sc_ref, f32[8,2,288,192]{3,2,1,0:T(8,128)} %get-tuple-element.20.v_ref, bf16[8,2,192,192]{3,2,1,0:T(8,128)(2,1)} %collective-permute-done.15.lo_ref, bf16[8,2,192,192]{3,2,1,0:T(8,128)(2,1)} %collective-permute-done.16.hi_ref, bf16[32,288,192]{2,1,0:T(8,128)(2,1)} %p_ref.5, ...), custom_call_target="tpu_custom_call" | custom-call | flops 700710912 | bytes 7667712 | tf_op jit(solution)/shard_map/pallas_call | solution.py:129
  200.6 11.1 %shard_map.51 = f32[2,288,192]{2,1,0:T(8,128)} custom-call(s32[3]{0:T(128)} %pad_add_fusion.1.sc_ref, f32[8,2,288,192]{3,2,1,0:T(8,128)} %get-tuple-element.26.v_ref, bf16[8,2,192,192]{3,2,1,0:T(8,128)(2,1)} %collective-permute-done.21.lo_ref, bf16[8,2,192,192]{3,2,1,0:T(8,128)(2,1)} %collective-permute-done.22.hi_ref, bf16[8,288,192]{2,1,0:T(8,128)(2,1)} %copy-done.1, ...), custom_call_target="tpu_custom_call" | custom-call | flops 700710912 | bytes 7667712 | tf_op jit(solution)/shard_map/pallas_call | solution.py:129
  211.7 3.2 %add_subtract_fusion = f32[2,288,192]{2,1,0:T(8,128)} fusion(f32[2,288,192]{2,1,0:T(8,128)S(1)} %copy-done.7, f32[2,288,192]{2,1,0:T(8,128)} %shard_map.51, f32[288,192]{1,0:T(8,128)S(1)} %get-tuple-element.60, f32[2]{0:T(128)S(1)} %get-tuple-element.32, f32[288,192]{1,0:T(8,128)} %get-tuple-element.61, f32[2]{0:T(128)S(1)} %get-tuple-element.33, ...), kind=kLoop, calls=%fused_computation.5 | loop fusion | flops 3760128 | bytes 4866176 | tf_op jit(solution)/shard_map/sub | solution.py:231
  (84 shorter events, 19.1 us)
Async XLA Ops:
  2.0 16.3 %collective-permute-start = (bf16[4,288,192]{2,1,0:T(8,128)(2,1)S(1)}, bf16[4,288,192]{2,1,0:T(8,128)(2,1)S(1)}, u32[]{:S(2)}, u32[]{:S(2)}) collective-permute-start(bf16[4,288,192]{2,1,0:T(8,128)(2,1)S(1)} %get-tuple-element.48), channel_id=1, source_target_pairs={{0,64},{1,65},{2,66},{3,67},{4,68},{5,69},{6,70},{7,71},{8,72},{9,... | collective-permute-start | bytes 1327112 | tf_op jit(solution)/shard_map/ppermute | solution.py:193
  3.3 48.6 %collective-permute-start.2 = (bf16[4,288,192]{2,1,0:T(8,128)(2,1)S(1)}, bf16[4,288,192]{2,1,0:T(8,128)(2,1)}, u32[]{:S(2)}, u32[]{:S(2)}) collective-permute-start(bf16[4,288,192]{2,1,0:T(8,128)(2,1)S(1)} %get-tuple-element.47), channel_id=1, source_target_pairs={{0,192},{1,193},{2,194},{3,195},{4,196},{5,197},{6,198},{7,199},{8... | collective-permute-start | bytes 1327112 | tf_op jit(solution)/shard_map/ppermute | solution.py:194
  8.7 58.4 %collective-permute-start.11 = (bf16[8,2,192,192]{3,2,1,0:T(8,128)(2,1)}, bf16[8,2,192,192]{3,2,1,0:T(8,128)(2,1)}, u32[]{:S(2)}, u32[]{:S(2)}) collective-permute-start(bf16[8,2,192,192]{3,2,1,0:T(8,128)(2,1)} %get-tuple-element.70), channel_id=1, source_target_pairs={{0,1},{1,2},{2,3},{3,4},{4,5},{5,6},{6,7},{7,8},{8,9},{9,10},{10,1... | collective-permute-start | bytes 3538952 | tf_op jit(solution)/shard_map/ppermute | solution.py:146
  8.7 58.4 %collective-permute-start.12 = (bf16[8,2,192,192]{3,2,1,0:T(8,128)(2,1)}, bf16[8,2,192,192]{3,2,1,0:T(8,128)(2,1)}, u32[]{:S(2)}, u32[]{:S(2)}) collective-permute-start(bf16[8,2,192,192]{3,2,1,0:T(8,128)(2,1)} %get-tuple-element.69), channel_id=1, source_target_pairs={{1,0},{2,1},{3,2},{4,3},{5,4},{6,5},{7,6},{8,7},{9,8},{10,9},{11,1... | collective-permute-start | bytes 3538952 | tf_op jit(solution)/shard_map/ppermute | solution.py:146
  18.3 75.1 %collective-permute-start.17 = (bf16[8,2,192,192]{3,2,1,0:T(8,128)(2,1)}, bf16[8,2,192,192]{3,2,1,0:T(8,128)(2,1)S(1)}, u32[]{:S(2)}, u32[]{:S(2)}) collective-permute-start(bf16[8,2,192,192]{3,2,1,0:T(8,128)(2,1)} %get-tuple-element.68), channel_id=1, source_target_pairs={{0,1},{1,2},{2,3},{3,4},{4,5},{5,6},{6,7},{7,8},{8,9},{9,10},{10,1... | collective-permute-start | bytes 3538952 | tf_op jit(solution)/shard_map/ppermute | solution.py:146
  18.3 75.1 %collective-permute-start.18 = (bf16[8,2,192,192]{3,2,1,0:T(8,128)(2,1)}, bf16[8,2,192,192]{3,2,1,0:T(8,128)(2,1)}, u32[]{:S(2)}, u32[]{:S(2)}) collective-permute-start(bf16[8,2,192,192]{3,2,1,0:T(8,128)(2,1)} %get-tuple-element.67), channel_id=1, source_target_pairs={{1,0},{2,1},{3,2},{4,3},{5,4},{6,5},{7,6},{8,7},{9,8},{10,9},{11,1... | collective-permute-start | bytes 3538952 | tf_op jit(solution)/shard_map/ppermute | solution.py:146
  51.9 10.6 %collective-permute-start.1 = (bf16[4,288,192]{2,1,0:T(8,128)(2,1)}, bf16[4,288,192]{2,1,0:T(8,128)(2,1)S(1)}, u32[]{:S(2)}, u32[]{:S(2)}) collective-permute-start(bf16[4,288,192]{2,1,0:T(8,128)(2,1)} %copy-done.14), channel_id=1, source_target_pairs={{0,64},{1,65},{2,66},{3,67},{4,68},{5,69},{6,70},{7,71},{8,72},{9,... | collective-permute-start | bytes 1327112 | tf_op jit(solution)/shard_map/ppermute | solution.py:193
  62.5 29.7 %collective-permute-start.3 = (bf16[4,288,192]{2,1,0:T(8,128)(2,1)}, bf16[4,288,192]{2,1,0:T(8,128)(2,1)}, u32[]{:S(2)}, u32[]{:S(2)}) collective-permute-start(bf16[4,288,192]{2,1,0:T(8,128)(2,1)} %collective-permute-done.2), channel_id=1, source_target_pairs={{0,192},{1,193},{2,194},{3,195},{4,196},{5,197},{6,198},{7,199},{8... | collective-permute-start | bytes 1327112 | tf_op jit(solution)/shard_map/ppermute | solution.py:194
  78.8 39.3 %collective-permute-start.13 = (bf16[8,2,192,192]{3,2,1,0:T(8,128)(2,1)}, bf16[8,2,192,192]{3,2,1,0:T(8,128)(2,1)}, u32[]{:S(2)}, u32[]{:S(2)}) collective-permute-start(bf16[8,2,192,192]{3,2,1,0:T(8,128)(2,1)} %get-tuple-element.18), channel_id=1, source_target_pairs={{0,1},{1,2},{2,3},{3,4},{4,5},{5,6},{6,7},{7,8},{8,9},{9,10},{10,1... | collective-permute-start | bytes 3538952 | tf_op jit(solution)/shard_map/ppermute | solution.py:146
  78.8 39.3 %collective-permute-start.14 = (bf16[8,2,192,192]{3,2,1,0:T(8,128)(2,1)}, bf16[8,2,192,192]{3,2,1,0:T(8,128)(2,1)}, u32[]{:S(2)}, u32[]{:S(2)}) collective-permute-start(bf16[8,2,192,192]{3,2,1,0:T(8,128)(2,1)} %get-tuple-element.19), channel_id=1, source_target_pairs={{1,0},{2,1},{3,2},{4,3},{5,4},{6,5},{7,6},{8,7},{9,8},{10,9},{11,1... | collective-permute-start | bytes 3538952 | tf_op jit(solution)/shard_map/ppermute | solution.py:146
  106.3 29.7 %collective-permute-start.19 = (bf16[8,2,192,192]{3,2,1,0:T(8,128)(2,1)}, bf16[8,2,192,192]{3,2,1,0:T(8,128)(2,1)S(1)}, u32[]{:S(2)}, u32[]{:S(2)}) collective-permute-start(bf16[8,2,192,192]{3,2,1,0:T(8,128)(2,1)} %get-tuple-element.24), channel_id=1, source_target_pairs={{0,1},{1,2},{2,3},{3,4},{4,5},{5,6},{6,7},{7,8},{8,9},{9,10},{10,1... | collective-permute-start | bytes 3538952 | tf_op jit(solution)/shard_map/ppermute | solution.py:146
  106.3 29.7 %collective-permute-start.20 = (bf16[8,2,192,192]{3,2,1,0:T(8,128)(2,1)}, bf16[8,2,192,192]{3,2,1,0:T(8,128)(2,1)}, u32[]{:S(2)}, u32[]{:S(2)}) collective-permute-start(bf16[8,2,192,192]{3,2,1,0:T(8,128)(2,1)} %get-tuple-element.25), channel_id=1, source_target_pairs={{1,0},{2,1},{3,2},{4,3},{5,4},{6,5},{7,6},{8,7},{9,8},{10,9},{11,1... | collective-permute-start | bytes 3538952 | tf_op jit(solution)/shard_map/ppermute | solution.py:146
  116.9 1.2 collective-permute-start.4
  118.0 37.3 %collective-permute-start.5 = (f32[2,8,2]{1,2,0:T(2,128)S(1)}, f32[2,8,2]{1,2,0:T(2,128)}, u32[]{:S(2)}, u32[]{:S(2)}) collective-permute-start(f32[2,8,2]{1,2,0:T(2,128)S(1)} %fusion.7), channel_id=1, source_target_pairs={{0,2},{1,3},{2,0},{3,1},{4,6},{5,7},{6,4},{7,5},{8,10},{9,11},{10,... | collective-permute-start | bytes 392 | tf_op jit(solution)/shard_map/ppermute | solution.py:174
  130.1 59.5 %collective-permute-start.15 = (bf16[8,2,192,192]{3,2,1,0:T(8,128)(2,1)}, bf16[8,2,192,192]{3,2,1,0:T(8,128)(2,1)}, u32[]{:S(2)}, u32[]{:S(2)}) collective-permute-start(bf16[8,2,192,192]{3,2,1,0:T(8,128)(2,1)} %get-tuple-element.21), channel_id=1, source_target_pairs={{0,1},{1,2},{2,3},{3,4},{4,5},{5,6},{6,7},{7,8},{8,9},{9,10},{10,1... | collective-permute-start | bytes 3538952 | tf_op jit(solution)/shard_map/ppermute | solution.py:146
  130.2 59.3 %collective-permute-start.16 = (bf16[8,2,192,192]{3,2,1,0:T(8,128)(2,1)}, bf16[8,2,192,192]{3,2,1,0:T(8,128)(2,1)}, u32[]{:S(2)}, u32[]{:S(2)}) collective-permute-start(bf16[8,2,192,192]{3,2,1,0:T(8,128)(2,1)} %get-tuple-element.22), channel_id=1, source_target_pairs={{1,0},{2,1},{3,2},{4,3},{5,4},{6,5},{7,6},{8,7},{9,8},{10,9},{11,1... | collective-permute-start | bytes 3538952 | tf_op jit(solution)/shard_map/ppermute | solution.py:146
  137.2 42.7 %copy-start.6 = (f32[8,288,192]{2,1,0:T(8,128)S(1)}, f32[8,288,192]{2,1,0:T(8,128)}, u32[]{:S(2)}) copy-start(f32[8,288,192]{2,1,0:T(8,128)} %copy-done.5) | copy-start | bytes 5308420
  149.4 51.2 %collective-permute-start.21 = (bf16[8,2,192,192]{3,2,1,0:T(8,128)(2,1)}, bf16[8,2,192,192]{3,2,1,0:T(8,128)(2,1)}, u32[]{:S(2)}, u32[]{:S(2)}) collective-permute-start(bf16[8,2,192,192]{3,2,1,0:T(8,128)(2,1)} %get-tuple-element.27), channel_id=1, source_target_pairs={{0,1},{1,2},{2,3},{3,4},{4,5},{5,6},{6,7},{7,8},{8,9},{9,10},{10,1... | collective-permute-start | bytes 3538952 | tf_op jit(solution)/shard_map/ppermute | solution.py:146
  149.4 51.1 %collective-permute-start.22 = (bf16[8,2,192,192]{3,2,1,0:T(8,128)(2,1)}, bf16[8,2,192,192]{3,2,1,0:T(8,128)(2,1)}, u32[]{:S(2)}, u32[]{:S(2)}) collective-permute-start(bf16[8,2,192,192]{3,2,1,0:T(8,128)(2,1)} %get-tuple-element.28), channel_id=1, source_target_pairs={{1,0},{2,1},{3,2},{4,3},{5,4},{6,5},{7,6},{8,7},{9,8},{10,9},{11,1... | collective-permute-start | bytes 3538952 | tf_op jit(solution)/shard_map/ppermute | solution.py:146
  156.0 12.8 %collective-permute-start.6 = (f32[2,8,2]{1,2,0:T(2,128)S(1)}, f32[2,8,2]{1,2,0:T(2,128)S(1)}, u32[]{:S(2)}, u32[]{:S(2)}) collective-permute-start(f32[2,8,2]{1,2,0:T(2,128)S(1)} %fusion.10), channel_id=1, source_target_pairs={{0,4},{1,5},{2,6},{3,7},{4,0},{5,1},{6,2},{7,3},{8,12},{9,13},{10,... | collective-permute-start | bytes 392 | tf_op jit(solution)/shard_map/ppermute | solution.py:174
  168.8 7.5 %collective-permute-start.7 = (f32[2,8,2]{1,2,0:T(2,128)S(1)}, f32[2,8,2]{1,2,0:T(2,128)S(1)}, u32[]{:S(2)}, u32[]{:S(2)}) collective-permute-start(f32[2,8,2]{1,2,0:T(2,128)S(1)} %add.117), channel_id=1, source_target_pairs={{0,8},{1,9},{2,10},{3,11},{4,12},{5,13},{6,14},{7,15},{8,0},{9,1},... | collective-permute-start | bytes 392 | tf_op jit(solution)/shard_map/ppermute | solution.py:174
  176.3 3.6 %collective-permute-start.8 = (f32[2,8,2]{1,2,0:T(2,128)S(1)}, f32[2,8,2]{1,2,0:T(2,128)S(1)}, u32[]{:S(2)}, u32[]{:S(2)}) collective-permute-start(f32[2,8,2]{1,2,0:T(2,128)S(1)} %add.118), channel_id=1, source_target_pairs={{0,16},{1,17},{2,18},{3,19},{4,20},{5,21},{6,22},{7,23},{8,24},{9,... | collective-permute-start | bytes 392 | tf_op jit(solution)/shard_map/ppermute | solution.py:174
  179.9 5.1 %collective-permute-start.9 = (f32[2,8,2]{1,2,0:T(2,128)S(1)}, f32[2,8,2]{1,2,0:T(2,128)S(1)}, u32[]{:S(2)}, u32[]{:S(2)}) collective-permute-start(f32[2,8,2]{1,2,0:T(2,128)S(1)} %add.119), channel_id=1, source_target_pairs={{0,32},{1,33},{2,34},{3,35},{4,36},{5,37},{6,38},{7,39},{8,40},{9,... | collective-permute-start | bytes 392 | tf_op jit(solution)/shard_map/ppermute | solution.py:174
  185.0 3.6 %collective-permute-start.10 = (f32[2,8,2]{1,2,0:T(2,128)S(1)}, f32[2,8,2]{1,2,0:T(2,128)S(1)}, u32[]{:S(2)}, u32[]{:S(2)}) collective-permute-start(f32[2,8,2]{1,2,0:T(2,128)S(1)} %add.120), channel_id=1, source_target_pairs={{0,64},{1,65},{2,66},{3,67},{4,68},{5,69},{6,70},{7,71},{8,72},{9,... | collective-permute-start | bytes 392 | tf_op jit(solution)/shard_map/ppermute | solution.py:174
  (14 other events, 99.3 us)

commit v3 on v2

--- a/solution.py
+++ b/solution.py
@@ -146,17 +146,12 @@
     return lax.ppermute(fwd, "domain", forward), lax.ppermute(bwd, "domain", backward)
 
 
-def solve_stream(warm_start, s, partner, pbase, targets, tmat, y0):
-    row_count = targets.shape[1]
-    halo = GY
+def warm_halos(warm_start, s, row_count):
     warm_block = lax.dynamic_index_in_dim(warm_start, s, 0, keepdims=False)
-    lo, hi = exchange_halos(
-        warm_block[:, :, row_count - halo :], warm_block[:, :, :halo]
-    )
-    scalars = jnp.stack([y0, s, pbase]).astype(jnp.int32)
-    potential, fwd, bwd = sweep_call(
-        False, warm_start, True, lo, hi, partner, targets, tmat, scalars
-    )
+    return warm_block[:, :, row_count - GY :], warm_block[:, :, :GY]
+
+
+def finish_stream(potential, fwd, bwd, partner, targets, tmat, scalars):
     for sweep_index in range(1, SWEEPS - 1):
         lo, hi = exchange_halos(fwd, bwd)
         potential, fwd, bwd = sweep_call(
@@ -170,9 +165,16 @@
     count = lax.axis_size(axis)
     step = 1
     while step < count:
-        pairs = [(k, k ^ step) for k in range(count)]
-        x = x + lax.ppermute(x, axis, pairs)
-        step *= 2
+        radix = 2
+        total = x
+        for part in range(1, radix):
+            pairs = [
+                (k, (k // (step * radix)) * step * radix + ((k // step) % radix ^ part) * step + k % step)
+                for k in range(count)
+            ]
+            total = total + lax.ppermute(x, axis, pairs)
+        x = total
+        step *= radix
     return x
 
 
@@ -190,9 +192,11 @@
         ]
     half = block.shape[0] // 2
     axes = ("band", "domain")
-    plus = lax.ppermute(lax.ppermute(block[:half], axes, shift(1)), axes, shift(1))
-    minus = lax.ppermute(lax.ppermute(block[half:], axes, shift(-1)), axes, shift(-1))
-    return jnp.concatenate([plus, minus], axis=0)
+    plus = lax.ppermute(block[:half], axes, shift(1))
+    minus = lax.ppermute(block[half:], axes, shift(-1))
+    return plus, minus, lambda plus, minus: jnp.concatenate(
+        [lax.ppermute(plus, axes, shift(1)), lax.ppermute(minus, axes, shift(-1))], axis=0
+    )
 
 
 def pair_sums(block, targets):
@@ -218,15 +222,32 @@
     s_own = jnp.where(owners[0] == band, 0, 1).astype(jnp.int32)
     s_rem = 1 - s_own
     own_block = lax.dynamic_slice_in_dim(partner_pool, s_own * ORB, ORB, 0)
-    rem_block = swap_over_y(own_block, (lax.axis_size("band"), lax.axis_size("domain")))
     tmat = circulant(targets.shape[2])
-    zero = jnp.zeros((), jnp.int32)
+    own_scalars = jnp.stack([y0, s_own, s_own * ORB]).astype(jnp.int32)
+    rem_scalars = jnp.stack([y0, s_rem, jnp.zeros((), jnp.int32)]).astype(jnp.int32)
+
+    own_halos = exchange_halos(*warm_halos(warm_start, s_own, row_count))
+    rem_sends, own_halos = lax.optimization_barrier(
+        (warm_halos(warm_start, s_rem, row_count), own_halos)
+    )
+    rem_halos = exchange_halos(*rem_sends)
+    plus, minus, finish_swap = swap_over_y(
+        own_block, (lax.axis_size("band"), lax.axis_size("domain"))
+    )
+    potential, fwd, bwd = sweep_call(
+        False, warm_start, True, *own_halos, partner_pool, targets, tmat, own_scalars
+    )
+    (plus, minus), potential = lax.optimization_barrier(((plus, minus), potential))
+    rem_block = finish_swap(plus, minus)
+    rem_state = sweep_call(
+        False, warm_start, True, *rem_halos, rem_block, targets, tmat, rem_scalars
+    )
 
     sums = jnp.stack([pair_sums(own_block, targets), pair_sums(rem_block, targets)])
     means = butterfly_sum(sums, "domain") / cell_count
 
-    own_acc = solve_stream(warm_start, s_own, partner_pool, s_own * ORB, targets, tmat, y0)
-    rem_acc = solve_stream(warm_start, s_rem, rem_block, zero, targets, tmat, y0)
+    own_acc = finish_stream(potential, fwd, bwd, partner_pool, targets, tmat, own_scalars)
+    rem_acc = finish_stream(*rem_state, rem_block, targets, tmat, rem_scalars)
     correction = mean_term(own_block, means[0]) + mean_term(rem_block, means[1])
     return (0.5 * coupling) * correction - (own_acc + rem_acc)
 

time: 218 us -> 220 us (level)
  waiting for transfers between devices: 52.5 us -> 87.3 us
  starting transfers between devices: 66.7 us -> 36.3 us
    ppermute x6, starting transfers between devices: 61.8 us -> 31.9 us  [exchange_halos(): lax.ppermute(bwd, 'domain', backward)]
    ppermute x11, waiting for transfers between devices: 52.5 us -> 70.8 us  [the longest x7 31.2 us: butterfly_sum(): total = total + lax.ppermute(x, axis, pairs)]
    ppermute x6, waiting for transfers between devices: 0.02 us -> 16.5 us  [exchange_halos(): lax.ppermute(fwd, 'domain', forward)]
    unnamed x31 -> x29, local copies, waits for them, and re-layouts: 4.41 us -> 4.45 us
  transfers between devices with their start and end apart: 23 -> 23, of which waited for: 8 -> 11; matrix products, arithmetic and copies ran while one was open for 8% -> 6% of each run, Pallas kernels for 27% -> 27%
where the time goes in v3:
time: 220 us; the launch traced here: 218 us
  waiting for transfers between devices  87.3 us (40%)
  Pallas kernels  69.4 us (32%)
  starting transfers between devices  36.3 us (16%)
  local copies, waits for them, and re-layouts  15.9 us (7%)
  other arithmetic  8.38 us (4%)
    pallas_call x6, Pallas kernels, sweep_call(): pl.pallas_call(functools.partial(sweep_kernel, final), grid_spec=grid_spe...  69.4 us
    ppermute x6, starting transfers between devices, exchange_halos(): lax.ppermute(bwd, 'domain', backward)  31.9 us
    ppermute x7, waiting for transfers between devices, butterfly_sum(): total = total + lax.ppermute(x, axis, pairs)  31.2 us
    ppermute x1, waiting for transfers between devices, swap_over_y(): lax.ppermute(plus, axes, shift(1))  25.1 us
    ppermute x6, waiting for transfers between devices, exchange_halos(): lax.ppermute(fwd, 'domain', forward)  16.5 us
    ppermute x1, waiting for transfers between devices, swap_over_y(): plus = lax.ppermute(block[:half], axes, shift(1))  9.92 us
    unnamed x29, local copies, waits for them, and re-layouts  4.45 us
  transfers between devices with their start and end apart: 23, of which 11 were waited for; matrix products, arithmetic and copies ran while one was open for 6% of the time, Pallas kernels for 27%

profile of v3, /device:TPU:16, one launch (start us, length us, event | category | flops | bytes accessed | tf_op | source)
XLA Modules:
  0.0 218.2 jit_solution(9588314768666226916)
XLA Ops:
  0.7 2.7 %dynamic-slice_bitcast_fusion = (bf16[8,2,288,192]{3,2,1,0:T(8,128)(2,1)S(1)}, bf16[8,2,288,192]{3,2,1,0:T(8,128)(2,1)S(1)}) fusion(bf16[2,8,2,288,192]{4,3,2,1,0:T(8,128)(2,1)} %v_ref.3, s32[]{:T(128)} %select_n.35, s32[]{:T(128)S(6)} %select_n.38), kind=kLoop, calls=%fused_computation.2 | loop fusion | bytes 7077896 | tf_op jit(solution)/shard_map/jit(dynamic_index_in_dim)/squeeze | solution.py:150
  5.3 8.2 %collective-permute-start.3 = (bf16[8,2,192,192]{3,2,1,0:T(8,128)(2,1)}, bf16[8,2,192,192]{3,2,1,0:T(8,128)(2,1)}, u32[]{:S(2)}, u32[]{:S(2)}) collective-permute-start(bf16[8,2,192,192]{3,2,1,0:T(8,128)(2,1)} %get-tuple-element.81), channel_id=1, source_target_pairs={{1,0},{2,1},{3,2},{4,3},{5,4},{6,5},{7,6},{8,7},{9,8},{10,9},{11,1... | collective-permute-start | bytes 3538952 | tf_op jit(solution)/shard_map/ppermute | solution.py:146
  13.5 2.0 fusion.9
  15.4 16.5 %collective-permute-done.2.lo_ref = bf16[8,2,192,192]{3,2,1,0:T(8,128)(2,1)} collective-permute-done((bf16[8,2,192,192]{3,2,1,0:T(8,128)(2,1)}, bf16[8,2,192,192]{3,2,1,0:T(8,128)(2,1)}, u32[]{:S(2)}, u32[]{:S(2)}) %collective-permute-start.2) | collective-permute-done | bytes 1179680 | tf_op jit(solution)/shard_map/ppermute | solution.py:146
  31.9 6.0 %collective-permute-start.18 = (bf16[8,2,192,192]{3,2,1,0:T(8,128)(2,1)}, bf16[8,2,192,192]{3,2,1,0:T(8,128)(2,1)}, u32[]{:S(2)}, u32[]{:S(2)}) collective-permute-start(bf16[8,2,192,192]{3,2,1,0:T(8,128)(2,1)} %get-tuple-element.36), channel_id=1, source_target_pairs={{1,0},{2,1},{3,2},{4,3},{5,4},{6,5},{7,6},{8,7},{9,8},{10,9},{11,1... | collective-permute-start | bytes 3538952 | tf_op jit(solution)/shard_map/ppermute | solution.py:146
  42.6 11.6 %shard_map.46 = (f32[8,2,288,192]{3,2,1,0:T(8,128)}, bf16[8,2,192,192]{3,2,1,0:T(8,128)(2,1)}, bf16[8,2,192,192]{3,2,1,0:T(8,128)(2,1)}) custom-call(s32[3]{0:T(128)} %pad_add_fusion.sc_ref, bf16[2,8,2,288,192]{4,3,2,1,0:T(8,128)(2,1)} %v_ref.3, bf16[8,2,192,192]{3,2,1,0:T(8,128)(2,1)} %collective-permute-done.2.lo_ref, ...), custom_call_target="tpu_custom_call" | custom-call | flops 700710912 | bytes 11354112 | tf_op jit(solution)/shard_map/pallas_call | solution.py:129
  54.2 9.9 %collective-permute-done = bf16[4,288,192]{2,1,0:T(8,128)(2,1)} collective-permute-done((bf16[4,288,192]{2,1,0:T(8,128)(2,1)S(1)}, bf16[4,288,192]{2,1,0:T(8,128)(2,1)}, u32[]{:S(2)}, u32[]{:S(2)}) %collective-permute-start) | collective-permute-done | bytes 442400 | tf_op jit(solution)/shard_map/ppermute | solution.py:195
  64.2 2.2 %collective-permute-done.1 = bf16[4,288,192]{2,1,0:T(8,128)(2,1)S(1)} collective-permute-done((bf16[4,288,192]{2,1,0:T(8,128)(2,1)S(1)}, bf16[4,288,192]{2,1,0:T(8,128)(2,1)S(1)}, u32[]{:S(2)}, u32[]{:S(2)}) %collective-permute-start.1) | collective-permute-done | bytes 442400 | tf_op jit(solution)/shard_map/ppermute | solution.py:196
  69.0 25.1 %collective-permute-done.4 = bf16[4,288,192]{2,1,0:T(8,128)(2,1)S(1)} collective-permute-done((bf16[4,288,192]{2,1,0:T(8,128)(2,1)}, bf16[4,288,192]{2,1,0:T(8,128)(2,1)S(1)}, u32[]{:S(2)}, u32[]{:S(2)}) %collective-permute-start.4) | collective-permute-done | bytes 442400 | tf_op jit(solution)/shard_map/ppermute | solution.py:198
  94.1 2.4 %collective-permute-done.5 = bf16[4,288,192]{2,1,0:T(8,128)(2,1)S(1)} collective-permute-done((bf16[4,288,192]{2,1,0:T(8,128)(2,1)S(1)}, bf16[4,288,192]{2,1,0:T(8,128)(2,1)S(1)}, u32[]{:S(2)}, u32[]{:S(2)}) %collective-permute-start.5) | collective-permute-done | bytes 442400 | tf_op jit(solution)/shard_map/ppermute | solution.py:198
  98.1 11.5 %shard_map.49 = (f32[8,2,288,192]{3,2,1,0:T(8,128)}, bf16[8,2,192,192]{3,2,1,0:T(8,128)(2,1)}, bf16[8,2,192,192]{3,2,1,0:T(8,128)(2,1)}) custom-call(s32[3]{0:T(128)} %pad_add_fusion.1.sc_ref, bf16[2,8,2,288,192]{4,3,2,1,0:T(8,128)(2,1)} %v_ref.3, bf16[8,2,192,192]{3,2,1,0:T(8,128)(2,1)} %copy-done.8, ...), custom_call_target="tpu_custom_call" | custom-call | flops 700710912 | bytes 11354112 | tf_op jit(solution)/shard_map/pallas_call | solution.py:129
  109.6 6.0 %collective-permute-start.20 = (bf16[8,2,192,192]{3,2,1,0:T(8,128)(2,1)}, bf16[8,2,192,192]{3,2,1,0:T(8,128)(2,1)}, u32[]{:S(2)}, u32[]{:S(2)}) collective-permute-start(bf16[8,2,192,192]{3,2,1,0:T(8,128)(2,1)} %get-tuple-element.39), channel_id=1, source_target_pairs={{1,0},{2,1},{3,2},{4,3},{5,4},{6,5},{7,6},{8,7},{9,8},{10,9},{11,1... | collective-permute-start | bytes 3538952 | tf_op jit(solution)/shard_map/ppermute | solution.py:146
  121.3 12.0 %shard_map.47 = (f32[8,2,288,192]{3,2,1,0:T(8,128)}, bf16[8,2,192,192]{3,2,1,0:T(8,128)(2,1)}, bf16[8,2,192,192]{3,2,1,0:T(8,128)(2,1)}) custom-call(s32[3]{0:T(128)} %pad_add_fusion.sc_ref, f32[8,2,288,192]{3,2,1,0:T(8,128)} %get-tuple-element.29.v_ref, bf16[8,2,192,192]{3,2,1,0:T(8,128)(2,1)} %collective-permute-done.13.lo_ref, ...), custom_call_target="tpu_custom_call" | custom-call | flops 700710912 | bytes 13123584 | tf_op jit(solution)/shard_map/pallas_call | solution.py:129
  133.5 5.8 %collective-permute-start.16 = (bf16[8,2,192,192]{3,2,1,0:T(8,128)(2,1)}, bf16[8,2,192,192]{3,2,1,0:T(8,128)(2,1)}, u32[]{:S(2)}, u32[]{:S(2)}) collective-permute-start(bf16[8,2,192,192]{3,2,1,0:T(8,128)(2,1)} %get-tuple-element.34), channel_id=1, source_target_pairs={{1,0},{2,1},{3,2},{4,3},{5,4},{6,5},{7,6},{8,7},{9,8},{10,9},{11,1... | collective-permute-start | bytes 3538952 | tf_op jit(solution)/shard_map/ppermute | solution.py:146
  140.5 12.2 %shard_map.50 = (f32[8,2,288,192]{3,2,1,0:T(8,128)}, bf16[8,2,192,192]{3,2,1,0:T(8,128)(2,1)}, bf16[8,2,192,192]{3,2,1,0:T(8,128)(2,1)}) custom-call(s32[3]{0:T(128)} %pad_add_fusion.1.sc_ref, f32[8,2,288,192]{3,2,1,0:T(8,128)} %get-tuple-element.37.v_ref, bf16[8,2,192,192]{3,2,1,0:T(8,128)(2,1)} %copy-done.9, ...), custom_call_target="tpu_custom_call" | custom-call | flops 700710912 | bytes 13123584 | tf_op jit(solution)/shard_map/pallas_call | solution.py:129
  152.7 6.0 %collective-permute-start.22 = (bf16[8,2,192,192]{3,2,1,0:T(8,128)(2,1)}, bf16[8,2,192,192]{3,2,1,0:T(8,128)(2,1)}, u32[]{:S(2)}, u32[]{:S(2)}) collective-permute-start(bf16[8,2,192,192]{3,2,1,0:T(8,128)(2,1)} %get-tuple-element.42), channel_id=1, source_target_pairs={{1,0},{2,1},{3,2},{4,3},{5,4},{6,5},{7,6},{8,7},{9,8},{10,9},{11,1... | collective-permute-start | bytes 3538952 | tf_op jit(solution)/shard_map/ppermute | solution.py:146
  159.2 12.8 %collective-permute-done.8 = f32[2,8,2]{1,2,0:T(2,128)S(1)} collective-permute-done((f32[2,8,2]{1,2,0:T(2,128)S(1)}, f32[2,8,2]{1,2,0:T(2,128)S(1)}, u32[]{:S(2)}, u32[]{:S(2)}) %collective-permute-start.8) | collective-permute-done | bytes 160 | tf_op jit(solution)/shard_map/ppermute | solution.py:175
  172.1 7.5 %collective-permute-done.9 = f32[2,8,2]{1,2,0:T(2,128)S(1)} collective-permute-done((f32[2,8,2]{1,2,0:T(2,128)S(1)}, f32[2,8,2]{1,2,0:T(2,128)S(1)}, u32[]{:S(2)}, u32[]{:S(2)}) %collective-permute-start.9) | collective-permute-done | bytes 160 | tf_op jit(solution)/shard_map/ppermute | solution.py:175
  179.6 3.6 %collective-permute-done.10 = f32[2,8,2]{1,2,0:T(2,128)S(1)} collective-permute-done((f32[2,8,2]{1,2,0:T(2,128)S(1)}, f32[2,8,2]{1,2,0:T(2,128)S(1)}, u32[]{:S(2)}, u32[]{:S(2)}) %collective-permute-start.10) | collective-permute-done | bytes 160 | tf_op jit(solution)/shard_map/ppermute | solution.py:175
  184.3 3.9 %collective-permute-done.11 = f32[2,8,2]{1,2,0:T(2,128)S(1)} collective-permute-done((f32[2,8,2]{1,2,0:T(2,128)S(1)}, f32[2,8,2]{1,2,0:T(2,128)S(1)}, u32[]{:S(2)}, u32[]{:S(2)}) %collective-permute-start.11) | collective-permute-done | bytes 160 | tf_op jit(solution)/shard_map/ppermute | solution.py:175
  189.6 2.3 %collective-permute-done.12 = f32[2,8,2]{1,2,0:T(2,128)S(1)} collective-permute-done((f32[2,8,2]{1,2,0:T(2,128)S(1)}, f32[2,8,2]{1,2,0:T(2,128)S(1)}, u32[]{:S(2)}, u32[]{:S(2)}) %collective-permute-start.12) | collective-permute-done | bytes 160 | tf_op jit(solution)/shard_map/ppermute | solution.py:175
  192.8 11.0 %shard_map.48 = f32[2,288,192]{2,1,0:T(8,128)} custom-call(s32[3]{0:T(128)} %pad_add_fusion.sc_ref, f32[8,2,288,192]{3,2,1,0:T(8,128)} %get-tuple-element.32.v_ref, bf16[8,2,192,192]{3,2,1,0:T(8,128)(2,1)} %collective-permute-done.15.lo_ref, bf16[8,2,192,192]{3,2,1,0:T(8,128)(2,1)} %collective-permute-done.16.hi_ref, bf16[32,288,192]{2,1,0:T(8,128)(2,1)} %p_ref.5, ...), custom_call_target="tpu_custom_call" | custom-call | flops 700710912 | bytes 7667712 | tf_op jit(solution)/shard_map/pallas_call | solution.py:129
  203.9 11.1 %shard_map.51 = f32[2,288,192]{2,1,0:T(8,128)} custom-call(s32[3]{0:T(128)} %pad_add_fusion.1.sc_ref, f32[8,2,288,192]{3,2,1,0:T(8,128)} %get-tuple-element.40.v_ref, bf16[8,2,192,192]{3,2,1,0:T(8,128)(2,1)} %collective-permute-done.21.lo_ref, bf16[8,2,192,192]{3,2,1,0:T(8,128)(2,1)} %collective-permute-done.22.hi_ref, bf16[8,288,192]{2,1,0:T(8,128)(2,1)} %copy-done.1, ...), custom_call_target="tpu_custom_call" | custom-call | flops 700710912 | bytes 7667712 | tf_op jit(solution)/shard_map/pallas_call | solution.py:129
  215.0 3.2 %add_subtract_fusion = f32[2,288,192]{2,1,0:T(8,128)} fusion(f32[2,288,192]{2,1,0:T(8,128)S(1)} %copy-done.7, f32[2,288,192]{2,1,0:T(8,128)} %shard_map.51, f32[288,192]{1,0:T(8,128)S(1)} %get-tuple-element.74, f32[2]{0:T(128)S(1)} %get-tuple-element.46, f32[288,192]{1,0:T(8,128)} %get-tuple-element.75, f32[2]{0:T(128)S(1)} %get-tuple-element.47, ...), kind=kLoop, calls=%fused_computation.5 | loop fusion | flops 3760128 | bytes 4866176 | tf_op jit(solution)/shard_map/sub | solution.py:252
  (82 shorter events, 22.0 us)
Async XLA Ops:
  5.3 26.6 %collective-permute-start.2 = (bf16[8,2,192,192]{3,2,1,0:T(8,128)(2,1)}, bf16[8,2,192,192]{3,2,1,0:T(8,128)(2,1)}, u32[]{:S(2)}, u32[]{:S(2)}) collective-permute-start(bf16[8,2,192,192]{3,2,1,0:T(8,128)(2,1)} %get-tuple-element.82), channel_id=1, source_target_pairs={{0,1},{1,2},{2,3},{3,4},{4,5},{5,6},{6,7},{7,8},{8,9},{9,10},{10,1... | collective-permute-start | bytes 3538952 | tf_op jit(solution)/shard_map/ppermute | solution.py:146
  5.3 26.6 %collective-permute-start.3 = (bf16[8,2,192,192]{3,2,1,0:T(8,128)(2,1)}, bf16[8,2,192,192]{3,2,1,0:T(8,128)(2,1)}, u32[]{:S(2)}, u32[]{:S(2)}) collective-permute-start(bf16[8,2,192,192]{3,2,1,0:T(8,128)(2,1)} %get-tuple-element.81), channel_id=1, source_target_pairs={{1,0},{2,1},{3,2},{4,3},{5,4},{6,5},{7,6},{8,7},{9,8},{10,9},{11,1... | collective-permute-start | bytes 3538952 | tf_op jit(solution)/shard_map/ppermute | solution.py:146
  31.9 64.6 %collective-permute-start.17 = (bf16[8,2,192,192]{3,2,1,0:T(8,128)(2,1)}, bf16[8,2,192,192]{3,2,1,0:T(8,128)(2,1)S(1)}, u32[]{:S(2)}, u32[]{:S(2)}) collective-permute-start(bf16[8,2,192,192]{3,2,1,0:T(8,128)(2,1)} %get-tuple-element.35), channel_id=1, source_target_pairs={{0,1},{1,2},{2,3},{3,4},{4,5},{5,6},{6,7},{7,8},{8,9},{9,10},{10,1... | collective-permute-start | bytes 3538952 | tf_op jit(solution)/shard_map/ppermute | solution.py:146
  31.9 64.6 %collective-permute-start.18 = (bf16[8,2,192,192]{3,2,1,0:T(8,128)(2,1)}, bf16[8,2,192,192]{3,2,1,0:T(8,128)(2,1)}, u32[]{:S(2)}, u32[]{:S(2)}) collective-permute-start(bf16[8,2,192,192]{3,2,1,0:T(8,128)(2,1)} %get-tuple-element.36), channel_id=1, source_target_pairs={{1,0},{2,1},{3,2},{4,3},{5,4},{6,5},{7,6},{8,7},{9,8},{10,9},{11,1... | collective-permute-start | bytes 3538952 | tf_op jit(solution)/shard_map/ppermute | solution.py:146
  39.2 25.0 %collective-permute-start = (bf16[4,288,192]{2,1,0:T(8,128)(2,1)S(1)}, bf16[4,288,192]{2,1,0:T(8,128)(2,1)}, u32[]{:S(2)}, u32[]{:S(2)}) collective-permute-start(bf16[4,288,192]{2,1,0:T(8,128)(2,1)S(1)} %get-tuple-element.64), channel_id=1, source_target_pairs={{0,64},{1,65},{2,66},{3,67},{4,68},{5,69},{6,70},{7,71},{8,72},{9,... | collective-permute-start | bytes 1327112 | tf_op jit(solution)/shard_map/ppermute | solution.py:195
  40.0 26.4 %collective-permute-start.1 = (bf16[4,288,192]{2,1,0:T(8,128)(2,1)S(1)}, bf16[4,288,192]{2,1,0:T(8,128)(2,1)S(1)}, u32[]{:S(2)}, u32[]{:S(2)}) collective-permute-start(bf16[4,288,192]{2,1,0:T(8,128)(2,1)S(1)} %get-tuple-element.63), channel_id=1, source_target_pairs={{0,192},{1,193},{2,194},{3,195},{4,196},{5,197},{6,198},{7,199},{8... | collective-permute-start | bytes 1327112 | tf_op jit(solution)/shard_map/ppermute | solution.py:196
  66.4 27.7 %collective-permute-start.4 = (bf16[4,288,192]{2,1,0:T(8,128)(2,1)}, bf16[4,288,192]{2,1,0:T(8,128)(2,1)S(1)}, u32[]{:S(2)}, u32[]{:S(2)}) collective-permute-start(bf16[4,288,192]{2,1,0:T(8,128)(2,1)} %collective-permute-done), channel_id=1, source_target_pairs={{0,64},{1,65},{2,66},{3,67},{4,68},{5,69},{6,70},{7,71},{8,72},{9,... | collective-permute-start | bytes 1327112 | tf_op jit(solution)/shard_map/ppermute | solution.py:198
  66.8 29.7 %collective-permute-start.5 = (bf16[4,288,192]{2,1,0:T(8,128)(2,1)S(1)}, bf16[4,288,192]{2,1,0:T(8,128)(2,1)S(1)}, u32[]{:S(2)}, u32[]{:S(2)}) collective-permute-start(bf16[4,288,192]{2,1,0:T(8,128)(2,1)S(1)} %collective-permute-done.1), channel_id=1, source_target_pairs={{0,192},{1,193},{2,194},{3,195},{4,196},{5,197},{6,198},{7,199},{8... | collective-permute-start | bytes 1327112 | tf_op jit(solution)/shard_map/ppermute | solution.py:198
  69.0 52.4 %collective-permute-start.13 = (bf16[8,2,192,192]{3,2,1,0:T(8,128)(2,1)}, bf16[8,2,192,192]{3,2,1,0:T(8,128)(2,1)}, u32[]{:S(2)}, u32[]{:S(2)}) collective-permute-start(bf16[8,2,192,192]{3,2,1,0:T(8,128)(2,1)} %get-tuple-element.30), channel_id=1, source_target_pairs={{0,1},{1,2},{2,3},{3,4},{4,5},{5,6},{6,7},{7,8},{8,9},{9,10},{10,1... | collective-permute-start | bytes 3538952 | tf_op jit(solution)/shard_map/ppermute | solution.py:146
  94.1 27.3 %collective-permute-start.14 = (bf16[8,2,192,192]{3,2,1,0:T(8,128)(2,1)}, bf16[8,2,192,192]{3,2,1,0:T(8,128)(2,1)}, u32[]{:S(2)}, u32[]{:S(2)}) collective-permute-start(bf16[8,2,192,192]{3,2,1,0:T(8,128)(2,1)} %get-tuple-element.31), channel_id=1, source_target_pairs={{1,0},{2,1},{3,2},{4,3},{5,4},{6,5},{7,6},{8,7},{9,8},{10,9},{11,1... | collective-permute-start | bytes 3538952 | tf_op jit(solution)/shard_map/ppermute | solution.py:146
  109.6 29.7 %collective-permute-start.19 = (bf16[8,2,192,192]{3,2,1,0:T(8,128)(2,1)}, bf16[8,2,192,192]{3,2,1,0:T(8,128)(2,1)S(1)}, u32[]{:S(2)}, u32[]{:S(2)}) collective-permute-start(bf16[8,2,192,192]{3,2,1,0:T(8,128)(2,1)} %get-tuple-element.38), channel_id=1, source_target_pairs={{0,1},{1,2},{2,3},{3,4},{4,5},{5,6},{6,7},{7,8},{8,9},{9,10},{10,1... | collective-permute-start | bytes 3538952 | tf_op jit(solution)/shard_map/ppermute | solution.py:146
  109.6 29.7 %collective-permute-start.20 = (bf16[8,2,192,192]{3,2,1,0:T(8,128)(2,1)}, bf16[8,2,192,192]{3,2,1,0:T(8,128)(2,1)}, u32[]{:S(2)}, u32[]{:S(2)}) collective-permute-start(bf16[8,2,192,192]{3,2,1,0:T(8,128)(2,1)} %get-tuple-element.39), channel_id=1, source_target_pairs={{1,0},{2,1},{3,2},{4,3},{5,4},{6,5},{7,6},{8,7},{9,8},{10,9},{11,1... | collective-permute-start | bytes 3538952 | tf_op jit(solution)/shard_map/ppermute | solution.py:146
  120.1 1.2 collective-permute-start.6
  121.3 37.3 %collective-permute-start.7 = (f32[2,8,2]{1,2,0:T(2,128)S(1)}, f32[2,8,2]{1,2,0:T(2,128)}, u32[]{:S(2)}, u32[]{:S(2)}) collective-permute-start(f32[2,8,2]{1,2,0:T(2,128)S(1)} %fusion.7), channel_id=1, source_target_pairs={{0,2},{1,3},{2,0},{3,1},{4,6},{5,7},{6,4},{7,5},{8,10},{9,11},{10,... | collective-permute-start | bytes 392 | tf_op jit(solution)/shard_map/ppermute | solution.py:175
  133.3 59.5 %collective-permute-start.15 = (bf16[8,2,192,192]{3,2,1,0:T(8,128)(2,1)}, bf16[8,2,192,192]{3,2,1,0:T(8,128)(2,1)}, u32[]{:S(2)}, u32[]{:S(2)}) collective-permute-start(bf16[8,2,192,192]{3,2,1,0:T(8,128)(2,1)} %get-tuple-element.33), channel_id=1, source_target_pairs={{0,1},{1,2},{2,3},{3,4},{4,5},{5,6},{6,7},{7,8},{8,9},{9,10},{10,1... | collective-permute-start | bytes 3538952 | tf_op jit(solution)/shard_map/ppermute | solution.py:146
  133.5 59.3 %collective-permute-start.16 = (bf16[8,2,192,192]{3,2,1,0:T(8,128)(2,1)}, bf16[8,2,192,192]{3,2,1,0:T(8,128)(2,1)}, u32[]{:S(2)}, u32[]{:S(2)}) collective-permute-start(bf16[8,2,192,192]{3,2,1,0:T(8,128)(2,1)} %get-tuple-element.34), channel_id=1, source_target_pairs={{1,0},{2,1},{3,2},{4,3},{5,4},{6,5},{7,6},{8,7},{9,8},{10,9},{11,1... | collective-permute-start | bytes 3538952 | tf_op jit(solution)/shard_map/ppermute | solution.py:146
  140.5 42.7 %copy-start.6 = (f32[8,288,192]{2,1,0:T(8,128)S(1)}, f32[8,288,192]{2,1,0:T(8,128)}, u32[]{:S(2)}) copy-start(f32[8,288,192]{2,1,0:T(8,128)} %copy-done.5) | copy-start | bytes 5308420
  152.6 51.2 %collective-permute-start.21 = (bf16[8,2,192,192]{3,2,1,0:T(8,128)(2,1)}, bf16[8,2,192,192]{3,2,1,0:T(8,128)(2,1)}, u32[]{:S(2)}, u32[]{:S(2)}) collective-permute-start(bf16[8,2,192,192]{3,2,1,0:T(8,128)(2,1)} %get-tuple-element.41), channel_id=1, source_target_pairs={{0,1},{1,2},{2,3},{3,4},{4,5},{5,6},{6,7},{7,8},{8,9},{9,10},{10,1... | collective-permute-start | bytes 3538952 | tf_op jit(solution)/shard_map/ppermute | solution.py:146
  152.7 51.1 %collective-permute-start.22 = (bf16[8,2,192,192]{3,2,1,0:T(8,128)(2,1)}, bf16[8,2,192,192]{3,2,1,0:T(8,128)(2,1)}, u32[]{:S(2)}, u32[]{:S(2)}) collective-permute-start(bf16[8,2,192,192]{3,2,1,0:T(8,128)(2,1)} %get-tuple-element.42), channel_id=1, source_target_pairs={{1,0},{2,1},{3,2},{4,3},{5,4},{6,5},{7,6},{8,7},{9,8},{10,9},{11,1... | collective-permute-start | bytes 3538952 | tf_op jit(solution)/shard_map/ppermute | solution.py:146
  159.2 12.8 %collective-permute-start.8 = (f32[2,8,2]{1,2,0:T(2,128)S(1)}, f32[2,8,2]{1,2,0:T(2,128)S(1)}, u32[]{:S(2)}, u32[]{:S(2)}) collective-permute-start(f32[2,8,2]{1,2,0:T(2,128)S(1)} %fusion.10), channel_id=1, source_target_pairs={{0,4},{1,5},{2,6},{3,7},{4,0},{5,1},{6,2},{7,3},{8,12},{9,13},{10,... | collective-permute-start | bytes 392 | tf_op jit(solution)/shard_map/ppermute | solution.py:175
  172.1 7.5 %collective-permute-start.9 = (f32[2,8,2]{1,2,0:T(2,128)S(1)}, f32[2,8,2]{1,2,0:T(2,128)S(1)}, u32[]{:S(2)}, u32[]{:S(2)}) collective-permute-start(f32[2,8,2]{1,2,0:T(2,128)S(1)} %add.122), channel_id=1, source_target_pairs={{0,8},{1,9},{2,10},{3,11},{4,12},{5,13},{6,14},{7,15},{8,0},{9,1},... | collective-permute-start | bytes 392 | tf_op jit(solution)/shard_map/ppermute | solution.py:175
  179.6 3.6 %collective-permute-start.10 = (f32[2,8,2]{1,2,0:T(2,128)S(1)}, f32[2,8,2]{1,2,0:T(2,128)S(1)}, u32[]{:S(2)}, u32[]{:S(2)}) collective-permute-start(f32[2,8,2]{1,2,0:T(2,128)S(1)} %add.123), channel_id=1, source_target_pairs={{0,16},{1,17},{2,18},{3,19},{4,20},{5,21},{6,22},{7,23},{8,24},{9,... | collective-permute-start | bytes 392 | tf_op jit(solution)/shard_map/ppermute | solution.py:175
  183.2 5.1 %collective-permute-start.11 = (f32[2,8,2]{1,2,0:T(2,128)S(1)}, f32[2,8,2]{1,2,0:T(2,128)S(1)}, u32[]{:S(2)}, u32[]{:S(2)}) collective-permute-start(f32[2,8,2]{1,2,0:T(2,128)S(1)} %add.124), channel_id=1, source_target_pairs={{0,32},{1,33},{2,34},{3,35},{4,36},{5,37},{6,38},{7,39},{8,40},{9,... | collective-permute-start | bytes 392 | tf_op jit(solution)/shard_map/ppermute | solution.py:175
  188.3 3.6 %collective-permute-start.12 = (f32[2,8,2]{1,2,0:T(2,128)S(1)}, f32[2,8,2]{1,2,0:T(2,128)S(1)}, u32[]{:S(2)}, u32[]{:S(2)}) collective-permute-start(f32[2,8,2]{1,2,0:T(2,128)S(1)} %add.125), channel_id=1, source_target_pairs={{0,64},{1,65},{2,66},{3,67},{4,68},{5,69},{6,70},{7,71},{8,72},{9,... | collective-permute-start | bytes 392 | tf_op jit(solution)/shard_map/ppermute | solution.py:175
  (13 other events, 76.3 us)

commit v4 on v3

--- a/solution.py
+++ b/solution.py
@@ -227,18 +227,17 @@
     rem_scalars = jnp.stack([y0, s_rem, jnp.zeros((), jnp.int32)]).astype(jnp.int32)
 
     own_halos = exchange_halos(*warm_halos(warm_start, s_own, row_count))
-    rem_sends, own_halos = lax.optimization_barrier(
-        (warm_halos(warm_start, s_rem, row_count), own_halos)
-    )
-    rem_halos = exchange_halos(*rem_sends)
     plus, minus, finish_swap = swap_over_y(
         own_block, (lax.axis_size("band"), lax.axis_size("domain"))
     )
+    rem_sends, own_halos, plus, minus = lax.optimization_barrier(
+        (warm_halos(warm_start, s_rem, row_count), own_halos, plus, minus)
+    )
+    rem_halos = exchange_halos(*rem_sends)
+    rem_block = finish_swap(plus, minus)
     potential, fwd, bwd = sweep_call(
         False, warm_start, True, *own_halos, partner_pool, targets, tmat, own_scalars
     )
-    (plus, minus), potential = lax.optimization_barrier(((plus, minus), potential))
-    rem_block = finish_swap(plus, minus)
     rem_state = sweep_call(
         False, warm_start, True, *rem_halos, rem_block, targets, tmat, rem_scalars
     )

time: 220 us -> 217 us (0.986)
  waiting for transfers between devices: 87.3 us -> 83 us
    ppermute x6, waiting for transfers between devices: 16.5 us -> 0.02 us  [exchange_halos(): lax.ppermute(fwd, 'domain', forward)]
    ppermute x1, waiting for transfers between devices: 9.92 us -> 20.7 us  [swap_over_y(): plus = lax.ppermute(block[:half], axes, shift(1))]
    unnamed x29 -> x31, local copies, waits for them, and re-layouts: 4.45 us -> 5.12 us
  transfers between devices with their start and end apart: 23 -> 23, of which waited for: 11 -> 10; matrix products, arithmetic and copies ran while one was open for 6% -> 6% of each run, Pallas kernels for 27% -> 27%
where the time goes in v4:
time: 217 us; the launch traced here: 215 us
  waiting for transfers between devices  83 us (38%)
  Pallas kernels  69.5 us (32%)
  starting transfers between devices  35.8 us (16%)
  local copies, waits for them, and re-layouts  17.7 us (8%)
  other arithmetic  8.38 us (4%)
    pallas_call x6, Pallas kernels, sweep_call(): pl.pallas_call(functools.partial(sweep_kernel, final), grid_spec=grid_spe...  69.5 us
    ppermute x6, starting transfers between devices, exchange_halos(): lax.ppermute(bwd, 'domain', backward)  31.2 us
    ppermute x7, waiting for transfers between devices, butterfly_sum(): total = total + lax.ppermute(x, axis, pairs)  31.1 us
    ppermute x1, waiting for transfers between devices, swap_over_y(): lax.ppermute(plus, axes, shift(1))  26.8 us
    ppermute x1, waiting for transfers between devices, swap_over_y(): plus = lax.ppermute(block[:half], axes, shift(1))  20.7 us
    unnamed x31, local copies, waits for them, and re-layouts  5.12 us
  transfers between devices with their start and end apart: 23, of which 10 were waited for; matrix products, arithmetic and copies ran while one was open for 6% of the time, Pallas kernels for 27%

profile of v4, /device:TPU:16, one launch (start us, length us, event | category | flops | bytes accessed | tf_op | source)
XLA Modules:
  0.0 215.2 jit_solution(11941812280827773525)
XLA Ops:
  0.7 2.7 %dynamic-slice_bitcast_fusion = (bf16[8,2,288,192]{3,2,1,0:T(8,128)(2,1)S(1)}, bf16[8,2,288,192]{3,2,1,0:T(8,128)(2,1)S(1)}) fusion(bf16[2,8,2,288,192]{4,3,2,1,0:T(8,128)(2,1)} %v_ref.3, s32[]{:T(128)} %select_n.35, s32[]{:T(128)S(6)} %select_n.37), kind=kLoop, calls=%fused_computation.2 | loop fusion | bytes 7077896 | tf_op jit(solution)/shard_map/jit(dynamic_index_in_dim)/squeeze | solution.py:150
  3.4 1.9 fusion.8
  5.3 8.2 %collective-permute-start.1 = (bf16[8,2,192,192]{3,2,1,0:T(8,128)(2,1)}, bf16[8,2,192,192]{3,2,1,0:T(8,128)(2,1)}, u32[]{:S(2)}, u32[]{:S(2)}) collective-permute-start(bf16[8,2,192,192]{3,2,1,0:T(8,128)(2,1)} %get-tuple-element.79), channel_id=1, source_target_pairs={{1,0},{2,1},{3,2},{4,3},{5,4},{6,5},{7,6},{8,7},{9,8},{10,9},{11,1... | collective-permute-start | bytes 3538952 | tf_op jit(solution)/shard_map/ppermute | solution.py:146
  16.9 2.0 fusion.9
  18.9 20.7 %collective-permute-done.2 = bf16[4,288,192]{2,1,0:T(8,128)(2,1)} collective-permute-done((bf16[4,288,192]{2,1,0:T(8,128)(2,1)S(1)}, bf16[4,288,192]{2,1,0:T(8,128)(2,1)}, u32[]{:S(2)}, u32[]{:S(2)}) %collective-permute-start.2) | collective-permute-done | bytes 442400 | tf_op jit(solution)/shard_map/ppermute | solution.py:195
  39.6 2.2 %collective-permute-done.3 = bf16[4,288,192]{2,1,0:T(8,128)(2,1)S(1)} collective-permute-done((bf16[4,288,192]{2,1,0:T(8,128)(2,1)S(1)}, bf16[4,288,192]{2,1,0:T(8,128)(2,1)S(1)}, u32[]{:S(2)}, u32[]{:S(2)}) %collective-permute-start.3) | collective-permute-done | bytes 442400 | tf_op jit(solution)/shard_map/ppermute | solution.py:196
  42.6 5.2 %collective-permute-start.18 = (bf16[8,2,192,192]{3,2,1,0:T(8,128)(2,1)}, bf16[8,2,192,192]{3,2,1,0:T(8,128)(2,1)}, u32[]{:S(2)}, u32[]{:S(2)}) collective-permute-start(bf16[8,2,192,192]{3,2,1,0:T(8,128)(2,1)} %get-tuple-element.34), channel_id=1, source_target_pairs={{1,0},{2,1},{3,2},{4,3},{5,4},{6,5},{7,6},{8,7},{9,8},{10,9},{11,1... | collective-permute-start | bytes 3538952 | tf_op jit(solution)/shard_map/ppermute | solution.py:146
  51.8 11.7 %shard_map.46 = (f32[8,2,288,192]{3,2,1,0:T(8,128)}, bf16[8,2,192,192]{3,2,1,0:T(8,128)(2,1)}, bf16[8,2,192,192]{3,2,1,0:T(8,128)(2,1)}) custom-call(s32[3]{0:T(128)} %pad_add_fusion.sc_ref, bf16[2,8,2,288,192]{4,3,2,1,0:T(8,128)(2,1)} %v_ref.3, bf16[8,2,192,192]{3,2,1,0:T(8,128)(2,1)} %collective-permute-done.lo_ref, ...), custom_call_target="tpu_custom_call" | custom-call | flops 700710912 | bytes 11354112 | tf_op jit(solution)/shard_map/pallas_call | solution.py:129
  63.5 26.8 %collective-permute-done.4 = bf16[4,288,192]{2,1,0:T(8,128)(2,1)S(1)} collective-permute-done((bf16[4,288,192]{2,1,0:T(8,128)(2,1)}, bf16[4,288,192]{2,1,0:T(8,128)(2,1)S(1)}, u32[]{:S(2)}, u32[]{:S(2)}) %collective-permute-start.4) | collective-permute-done | bytes 442400 | tf_op jit(solution)/shard_map/ppermute | solution.py:198
  90.3 2.2 %collective-permute-done.5 = bf16[4,288,192]{2,1,0:T(8,128)(2,1)} collective-permute-done((bf16[4,288,192]{2,1,0:T(8,128)(2,1)}, bf16[4,288,192]{2,1,0:T(8,128)(2,1)}, u32[]{:S(2)}, u32[]{:S(2)}) %collective-permute-start.5) | collective-permute-done | bytes 442400 | tf_op jit(solution)/shard_map/ppermute | solution.py:198
  95.1 11.5 %shard_map.49 = (f32[8,2,288,192]{3,2,1,0:T(8,128)}, bf16[8,2,192,192]{3,2,1,0:T(8,128)(2,1)}, bf16[8,2,192,192]{3,2,1,0:T(8,128)(2,1)}) custom-call(s32[3]{0:T(128)} %pad_add_fusion.1.sc_ref, bf16[2,8,2,288,192]{4,3,2,1,0:T(8,128)(2,1)} %v_ref.3, bf16[8,2,192,192]{3,2,1,0:T(8,128)(2,1)} %copy-done.8, ...), custom_call_target="tpu_custom_call" | custom-call | flops 700710912 | bytes 11354112 | tf_op jit(solution)/shard_map/pallas_call | solution.py:129
  106.7 6.0 %collective-permute-start.20 = (bf16[8,2,192,192]{3,2,1,0:T(8,128)(2,1)}, bf16[8,2,192,192]{3,2,1,0:T(8,128)(2,1)}, u32[]{:S(2)}, u32[]{:S(2)}) collective-permute-start(bf16[8,2,192,192]{3,2,1,0:T(8,128)(2,1)} %get-tuple-element.37), channel_id=1, source_target_pairs={{1,0},{2,1},{3,2},{4,3},{5,4},{6,5},{7,6},{8,7},{9,8},{10,9},{11,1... | collective-permute-start | bytes 3538952 | tf_op jit(solution)/shard_map/ppermute | solution.py:146
  118.4 12.0 %shard_map.47 = (f32[8,2,288,192]{3,2,1,0:T(8,128)}, bf16[8,2,192,192]{3,2,1,0:T(8,128)(2,1)}, bf16[8,2,192,192]{3,2,1,0:T(8,128)(2,1)}) custom-call(s32[3]{0:T(128)} %pad_add_fusion.sc_ref, f32[8,2,288,192]{3,2,1,0:T(8,128)} %get-tuple-element.27.v_ref, bf16[8,2,192,192]{3,2,1,0:T(8,128)(2,1)} %collective-permute-done.13.lo_ref, ...), custom_call_target="tpu_custom_call" | custom-call | flops 700710912 | bytes 13123584 | tf_op jit(solution)/shard_map/pallas_call | solution.py:129
  130.6 5.8 %collective-permute-start.16 = (bf16[8,2,192,192]{3,2,1,0:T(8,128)(2,1)}, bf16[8,2,192,192]{3,2,1,0:T(8,128)(2,1)}, u32[]{:S(2)}, u32[]{:S(2)}) collective-permute-start(bf16[8,2,192,192]{3,2,1,0:T(8,128)(2,1)} %get-tuple-element.32), channel_id=1, source_target_pairs={{1,0},{2,1},{3,2},{4,3},{5,4},{6,5},{7,6},{8,7},{9,8},{10,9},{11,1... | collective-permute-start | bytes 3538952 | tf_op jit(solution)/shard_map/ppermute | solution.py:146
  137.5 12.2 %shard_map.50 = (f32[8,2,288,192]{3,2,1,0:T(8,128)}, bf16[8,2,192,192]{3,2,1,0:T(8,128)(2,1)}, bf16[8,2,192,192]{3,2,1,0:T(8,128)(2,1)}) custom-call(s32[3]{0:T(128)} %pad_add_fusion.1.sc_ref, f32[8,2,288,192]{3,2,1,0:T(8,128)} %get-tuple-element.35.v_ref, bf16[8,2,192,192]{3,2,1,0:T(8,128)(2,1)} %copy-done.9, ...), custom_call_target="tpu_custom_call" | custom-call | flops 700710912 | bytes 13123584 | tf_op jit(solution)/shard_map/pallas_call | solution.py:129
  149.7 6.0 %collective-permute-start.22 = (bf16[8,2,192,192]{3,2,1,0:T(8,128)(2,1)}, bf16[8,2,192,192]{3,2,1,0:T(8,128)(2,1)}, u32[]{:S(2)}, u32[]{:S(2)}) collective-permute-start(bf16[8,2,192,192]{3,2,1,0:T(8,128)(2,1)} %get-tuple-element.40), channel_id=1, source_target_pairs={{1,0},{2,1},{3,2},{4,3},{5,4},{6,5},{7,6},{8,7},{9,8},{10,9},{11,1... | collective-permute-start | bytes 3538952 | tf_op jit(solution)/shard_map/ppermute | solution.py:146
  156.3 12.8 %collective-permute-done.8 = f32[2,8,2]{1,2,0:T(2,128)S(1)} collective-permute-done((f32[2,8,2]{1,2,0:T(2,128)S(1)}, f32[2,8,2]{1,2,0:T(2,128)S(1)}, u32[]{:S(2)}, u32[]{:S(2)}) %collective-permute-start.8) | collective-permute-done | bytes 160 | tf_op jit(solution)/shard_map/ppermute | solution.py:175
  169.1 7.5 %collective-permute-done.9 = f32[2,8,2]{1,2,0:T(2,128)S(1)} collective-permute-done((f32[2,8,2]{1,2,0:T(2,128)S(1)}, f32[2,8,2]{1,2,0:T(2,128)S(1)}, u32[]{:S(2)}, u32[]{:S(2)}) %collective-permute-start.9) | collective-permute-done | bytes 160 | tf_op jit(solution)/shard_map/ppermute | solution.py:175
  176.6 3.6 %collective-permute-done.10 = f32[2,8,2]{1,2,0:T(2,128)S(1)} collective-permute-done((f32[2,8,2]{1,2,0:T(2,128)S(1)}, f32[2,8,2]{1,2,0:T(2,128)S(1)}, u32[]{:S(2)}, u32[]{:S(2)}) %collective-permute-start.10) | collective-permute-done | bytes 160 | tf_op jit(solution)/shard_map/ppermute | solution.py:175
  181.4 3.9 %collective-permute-done.11 = f32[2,8,2]{1,2,0:T(2,128)S(1)} collective-permute-done((f32[2,8,2]{1,2,0:T(2,128)S(1)}, f32[2,8,2]{1,2,0:T(2,128)S(1)}, u32[]{:S(2)}, u32[]{:S(2)}) %collective-permute-start.11) | collective-permute-done | bytes 160 | tf_op jit(solution)/shard_map/ppermute | solution.py:175
  186.8 2.1 collective-permute-done.12
  189.9 11.0 %shard_map.48 = f32[2,288,192]{2,1,0:T(8,128)} custom-call(s32[3]{0:T(128)} %pad_add_fusion.sc_ref, f32[8,2,288,192]{3,2,1,0:T(8,128)} %get-tuple-element.30.v_ref, bf16[8,2,192,192]{3,2,1,0:T(8,128)(2,1)} %collective-permute-done.15.lo_ref, bf16[8,2,192,192]{3,2,1,0:T(8,128)(2,1)} %collective-permute-done.16.hi_ref, bf16[32,288,192]{2,1,0:T(8,128)(2,1)} %p_ref.5, ...), custom_call_target="tpu_custom_call" | custom-call | flops 700710912 | bytes 7667712 | tf_op jit(solution)/shard_map/pallas_call | solution.py:129
  200.9 11.1 %shard_map.51 = f32[2,288,192]{2,1,0:T(8,128)} custom-call(s32[3]{0:T(128)} %pad_add_fusion.1.sc_ref, f32[8,2,288,192]{3,2,1,0:T(8,128)} %get-tuple-element.38.v_ref, bf16[8,2,192,192]{3,2,1,0:T(8,128)(2,1)} %collective-permute-done.21.lo_ref, bf16[8,2,192,192]{3,2,1,0:T(8,128)(2,1)} %collective-permute-done.22.hi_ref, bf16[8,288,192]{2,1,0:T(8,128)(2,1)} %copy-done.1, ...), custom_call_target="tpu_custom_call" | custom-call | flops 700710912 | bytes 7667712 | tf_op jit(solution)/shard_map/pallas_call | solution.py:129
  212.0 3.2 %add_subtract_fusion = f32[2,288,192]{2,1,0:T(8,128)} fusion(f32[2,288,192]{2,1,0:T(8,128)S(1)} %copy-done.7, f32[2,288,192]{2,1,0:T(8,128)} %shard_map.51, f32[288,192]{1,0:T(8,128)S(1)} %get-tuple-element.72, f32[2]{0:T(128)S(1)} %get-tuple-element.44, f32[288,192]{1,0:T(8,128)} %get-tuple-element.73, f32[2]{0:T(128)S(1)} %get-tuple-element.45, ...), kind=kLoop, calls=%fused_computation.5 | loop fusion | flops 3760128 | bytes 4866176 | tf_op jit(solution)/shard_map/sub | solution.py:251
  (84 shorter events, 22.1 us)
Async XLA Ops:
  5.3 36.5 %collective-permute-start = (bf16[8,2,192,192]{3,2,1,0:T(8,128)(2,1)}, bf16[8,2,192,192]{3,2,1,0:T(8,128)(2,1)}, u32[]{:S(2)}, u32[]{:S(2)}) collective-permute-start(bf16[8,2,192,192]{3,2,1,0:T(8,128)(2,1)} %get-tuple-element.80), channel_id=1, source_target_pairs={{0,1},{1,2},{2,3},{3,4},{4,5},{5,6},{6,7},{7,8},{8,9},{9,10},{10,1... | collective-permute-start | bytes 3538952 | tf_op jit(solution)/shard_map/ppermute | solution.py:146
  5.3 36.5 %collective-permute-start.1 = (bf16[8,2,192,192]{3,2,1,0:T(8,128)(2,1)}, bf16[8,2,192,192]{3,2,1,0:T(8,128)(2,1)}, u32[]{:S(2)}, u32[]{:S(2)}) collective-permute-start(bf16[8,2,192,192]{3,2,1,0:T(8,128)(2,1)} %get-tuple-element.79), channel_id=1, source_target_pairs={{1,0},{2,1},{3,2},{4,3},{5,4},{6,5},{7,6},{8,7},{9,8},{10,9},{11,1... | collective-permute-start | bytes 3538952 | tf_op jit(solution)/shard_map/ppermute | solution.py:146
  14.8 24.8 %collective-permute-start.2 = (bf16[4,288,192]{2,1,0:T(8,128)(2,1)S(1)}, bf16[4,288,192]{2,1,0:T(8,128)(2,1)}, u32[]{:S(2)}, u32[]{:S(2)}) collective-permute-start(bf16[4,288,192]{2,1,0:T(8,128)(2,1)S(1)} %get-tuple-element.60), channel_id=1, source_target_pairs={{0,64},{1,65},{2,66},{3,67},{4,68},{5,69},{6,70},{7,71},{8,72},{9,... | collective-permute-start | bytes 1327112 | tf_op jit(solution)/shard_map/ppermute | solution.py:195
  15.6 26.2 %collective-permute-start.3 = (bf16[4,288,192]{2,1,0:T(8,128)(2,1)S(1)}, bf16[4,288,192]{2,1,0:T(8,128)(2,1)S(1)}, u32[]{:S(2)}, u32[]{:S(2)}) collective-permute-start(bf16[4,288,192]{2,1,0:T(8,128)(2,1)S(1)} %get-tuple-element.59), channel_id=1, source_target_pairs={{0,192},{1,193},{2,194},{3,195},{4,196},{5,197},{6,198},{7,199},{8... | collective-permute-start | bytes 1327112 | tf_op jit(solution)/shard_map/ppermute | solution.py:196
  41.8 51.8 %collective-permute-start.17 = (bf16[8,2,192,192]{3,2,1,0:T(8,128)(2,1)}, bf16[8,2,192,192]{3,2,1,0:T(8,128)(2,1)S(1)}, u32[]{:S(2)}, u32[]{:S(2)}) collective-permute-start(bf16[8,2,192,192]{3,2,1,0:T(8,128)(2,1)} %get-tuple-element.33), channel_id=1, source_target_pairs={{0,1},{1,2},{2,3},{3,4},{4,5},{5,6},{6,7},{7,8},{8,9},{9,10},{10,1... | collective-permute-start | bytes 3538952 | tf_op jit(solution)/shard_map/ppermute | solution.py:146
  42.6 51.0 %collective-permute-start.18 = (bf16[8,2,192,192]{3,2,1,0:T(8,128)(2,1)}, bf16[8,2,192,192]{3,2,1,0:T(8,128)(2,1)}, u32[]{:S(2)}, u32[]{:S(2)}) collective-permute-start(bf16[8,2,192,192]{3,2,1,0:T(8,128)(2,1)} %get-tuple-element.34), channel_id=1, source_target_pairs={{1,0},{2,1},{3,2},{4,3},{5,4},{6,5},{7,6},{8,7},{9,8},{10,9},{11,1... | collective-permute-start | bytes 3538952 | tf_op jit(solution)/shard_map/ppermute | solution.py:146
  47.9 42.4 %collective-permute-start.4 = (bf16[4,288,192]{2,1,0:T(8,128)(2,1)}, bf16[4,288,192]{2,1,0:T(8,128)(2,1)S(1)}, u32[]{:S(2)}, u32[]{:S(2)}) collective-permute-start(bf16[4,288,192]{2,1,0:T(8,128)(2,1)} %collective-permute-done.2), channel_id=1, source_target_pairs={{0,64},{1,65},{2,66},{3,67},{4,68},{5,69},{6,70},{7,71},{8,72},{9,... | collective-permute-start | bytes 1327112 | tf_op jit(solution)/shard_map/ppermute | solution.py:198
  48.3 44.2 %collective-permute-start.5 = (bf16[4,288,192]{2,1,0:T(8,128)(2,1)}, bf16[4,288,192]{2,1,0:T(8,128)(2,1)}, u32[]{:S(2)}, u32[]{:S(2)}) collective-permute-start(bf16[4,288,192]{2,1,0:T(8,128)(2,1)} %copy-done.14), channel_id=1, source_target_pairs={{0,192},{1,193},{2,194},{3,195},{4,196},{5,197},{6,198},{7,199},{8... | collective-permute-start | bytes 1327112 | tf_op jit(solution)/shard_map/ppermute | solution.py:198
  63.5 54.9 %collective-permute-start.13 = (bf16[8,2,192,192]{3,2,1,0:T(8,128)(2,1)}, bf16[8,2,192,192]{3,2,1,0:T(8,128)(2,1)}, u32[]{:S(2)}, u32[]{:S(2)}) collective-permute-start(bf16[8,2,192,192]{3,2,1,0:T(8,128)(2,1)} %get-tuple-element.28), channel_id=1, source_target_pairs={{0,1},{1,2},{2,3},{3,4},{4,5},{5,6},{6,7},{7,8},{8,9},{9,10},{10,1... | collective-permute-start | bytes 3538952 | tf_op jit(solution)/shard_map/ppermute | solution.py:146
  90.3 28.1 %collective-permute-start.14 = (bf16[8,2,192,192]{3,2,1,0:T(8,128)(2,1)}, bf16[8,2,192,192]{3,2,1,0:T(8,128)(2,1)}, u32[]{:S(2)}, u32[]{:S(2)}) collective-permute-start(bf16[8,2,192,192]{3,2,1,0:T(8,128)(2,1)} %get-tuple-element.29), channel_id=1, source_target_pairs={{1,0},{2,1},{3,2},{4,3},{5,4},{6,5},{7,6},{8,7},{9,8},{10,9},{11,1... | collective-permute-start | bytes 3538952 | tf_op jit(solution)/shard_map/ppermute | solution.py:146
  106.6 29.7 %collective-permute-start.19 = (bf16[8,2,192,192]{3,2,1,0:T(8,128)(2,1)}, bf16[8,2,192,192]{3,2,1,0:T(8,128)(2,1)S(1)}, u32[]{:S(2)}, u32[]{:S(2)}) collective-permute-start(bf16[8,2,192,192]{3,2,1,0:T(8,128)(2,1)} %get-tuple-element.36), channel_id=1, source_target_pairs={{0,1},{1,2},{2,3},{3,4},{4,5},{5,6},{6,7},{7,8},{8,9},{9,10},{10,1... | collective-permute-start | bytes 3538952 | tf_op jit(solution)/shard_map/ppermute | solution.py:146
  106.7 29.7 %collective-permute-start.20 = (bf16[8,2,192,192]{3,2,1,0:T(8,128)(2,1)}, bf16[8,2,192,192]{3,2,1,0:T(8,128)(2,1)}, u32[]{:S(2)}, u32[]{:S(2)}) collective-permute-start(bf16[8,2,192,192]{3,2,1,0:T(8,128)(2,1)} %get-tuple-element.37), channel_id=1, source_target_pairs={{1,0},{2,1},{3,2},{4,3},{5,4},{6,5},{7,6},{8,7},{9,8},{10,9},{11,1... | collective-permute-start | bytes 3538952 | tf_op jit(solution)/shard_map/ppermute | solution.py:146
  117.2 1.2 collective-permute-start.6
  118.4 37.3 %collective-permute-start.7 = (f32[2,8,2]{1,2,0:T(2,128)S(1)}, f32[2,8,2]{1,2,0:T(2,128)}, u32[]{:S(2)}, u32[]{:S(2)}) collective-permute-start(f32[2,8,2]{1,2,0:T(2,128)S(1)} %fusion.7), channel_id=1, source_target_pairs={{0,2},{1,3},{2,0},{3,1},{4,6},{5,7},{6,4},{7,5},{8,10},{9,11},{10,... | collective-permute-start | bytes 392 | tf_op jit(solution)/shard_map/ppermute | solution.py:175
  130.4 59.5 %collective-permute-start.15 = (bf16[8,2,192,192]{3,2,1,0:T(8,128)(2,1)}, bf16[8,2,192,192]{3,2,1,0:T(8,128)(2,1)}, u32[]{:S(2)}, u32[]{:S(2)}) collective-permute-start(bf16[8,2,192,192]{3,2,1,0:T(8,128)(2,1)} %get-tuple-element.31), channel_id=1, source_target_pairs={{0,1},{1,2},{2,3},{3,4},{4,5},{5,6},{6,7},{7,8},{8,9},{9,10},{10,1... | collective-permute-start | bytes 3538952 | tf_op jit(solution)/shard_map/ppermute | solution.py:146
  130.6 59.3 %collective-permute-start.16 = (bf16[8,2,192,192]{3,2,1,0:T(8,128)(2,1)}, bf16[8,2,192,192]{3,2,1,0:T(8,128)(2,1)}, u32[]{:S(2)}, u32[]{:S(2)}) collective-permute-start(bf16[8,2,192,192]{3,2,1,0:T(8,128)(2,1)} %get-tuple-element.32), channel_id=1, source_target_pairs={{1,0},{2,1},{3,2},{4,3},{5,4},{6,5},{7,6},{8,7},{9,8},{10,9},{11,1... | collective-permute-start | bytes 3538952 | tf_op jit(solution)/shard_map/ppermute | solution.py:146
  137.5 42.7 %copy-start.6 = (f32[8,288,192]{2,1,0:T(8,128)S(1)}, f32[8,288,192]{2,1,0:T(8,128)}, u32[]{:S(2)}) copy-start(f32[8,288,192]{2,1,0:T(8,128)} %copy-done.5) | copy-start | bytes 5308420
  149.7 51.2 %collective-permute-start.21 = (bf16[8,2,192,192]{3,2,1,0:T(8,128)(2,1)}, bf16[8,2,192,192]{3,2,1,0:T(8,128)(2,1)}, u32[]{:S(2)}, u32[]{:S(2)}) collective-permute-start(bf16[8,2,192,192]{3,2,1,0:T(8,128)(2,1)} %get-tuple-element.39), channel_id=1, source_target_pairs={{0,1},{1,2},{2,3},{3,4},{4,5},{5,6},{6,7},{7,8},{8,9},{9,10},{10,1... | collective-permute-start | bytes 3538952 | tf_op jit(solution)/shard_map/ppermute | solution.py:146
  149.7 51.1 %collective-permute-start.22 = (bf16[8,2,192,192]{3,2,1,0:T(8,128)(2,1)}, bf16[8,2,192,192]{3,2,1,0:T(8,128)(2,1)}, u32[]{:S(2)}, u32[]{:S(2)}) collective-permute-start(bf16[8,2,192,192]{3,2,1,0:T(8,128)(2,1)} %get-tuple-element.40), channel_id=1, source_target_pairs={{1,0},{2,1},{3,2},{4,3},{5,4},{6,5},{7,6},{8,7},{9,8},{10,9},{11,1... | collective-permute-start | bytes 3538952 | tf_op jit(solution)/shard_map/ppermute | solution.py:146
  156.3 12.8 %collective-permute-start.8 = (f32[2,8,2]{1,2,0:T(2,128)S(1)}, f32[2,8,2]{1,2,0:T(2,128)S(1)}, u32[]{:S(2)}, u32[]{:S(2)}) collective-permute-start(f32[2,8,2]{1,2,0:T(2,128)S(1)} %fusion.10), channel_id=1, source_target_pairs={{0,4},{1,5},{2,6},{3,7},{4,0},{5,1},{6,2},{7,3},{8,12},{9,13},{10,... | collective-permute-start | bytes 392 | tf_op jit(solution)/shard_map/ppermute | solution.py:175
  169.1 7.5 %collective-permute-start.9 = (f32[2,8,2]{1,2,0:T(2,128)S(1)}, f32[2,8,2]{1,2,0:T(2,128)S(1)}, u32[]{:S(2)}, u32[]{:S(2)}) collective-permute-start(f32[2,8,2]{1,2,0:T(2,128)S(1)} %add.118), channel_id=1, source_target_pairs={{0,8},{1,9},{2,10},{3,11},{4,12},{5,13},{6,14},{7,15},{8,0},{9,1},... | collective-permute-start | bytes 392 | tf_op jit(solution)/shard_map/ppermute | solution.py:175
  176.6 3.6 %collective-permute-start.10 = (f32[2,8,2]{1,2,0:T(2,128)S(1)}, f32[2,8,2]{1,2,0:T(2,128)S(1)}, u32[]{:S(2)}, u32[]{:S(2)}) collective-permute-start(f32[2,8,2]{1,2,0:T(2,128)S(1)} %add.119), channel_id=1, source_target_pairs={{0,16},{1,17},{2,18},{3,19},{4,20},{5,21},{6,22},{7,23},{8,24},{9,... | collective-permute-start | bytes 392 | tf_op jit(solution)/shard_map/ppermute | solution.py:175
  180.2 5.1 %collective-permute-start.11 = (f32[2,8,2]{1,2,0:T(2,128)S(1)}, f32[2,8,2]{1,2,0:T(2,128)S(1)}, u32[]{:S(2)}, u32[]{:S(2)}) collective-permute-start(f32[2,8,2]{1,2,0:T(2,128)S(1)} %add.120), channel_id=1, source_target_pairs={{0,32},{1,33},{2,34},{3,35},{4,36},{5,37},{6,38},{7,39},{8,40},{9,... | collective-permute-start | bytes 392 | tf_op jit(solution)/shard_map/ppermute | solution.py:175
  185.3 3.6 %collective-permute-start.12 = (f32[2,8,2]{1,2,0:T(2,128)S(1)}, f32[2,8,2]{1,2,0:T(2,128)S(1)}, u32[]{:S(2)}, u32[]{:S(2)}) collective-permute-start(f32[2,8,2]{1,2,0:T(2,128)S(1)} %add.121), channel_id=1, source_target_pairs={{0,64},{1,65},{2,66},{3,67},{4,68},{5,69},{6,70},{7,71},{8,72},{9,... | collective-permute-start | bytes 392 | tf_op jit(solution)/shard_map/ppermute | solution.py:175
  (14 other events, 77.2 us)

commit v5 on v4

--- a/solution.py
+++ b/solution.py
@@ -26,44 +26,51 @@
     return ((gap == 1) | (gap == width - 1)).astype(jnp.bfloat16)
 
 
-def stencil(y0, v, lo, hi, q, t_ref, wide):
+def split_dot(lhs, rhs, left):
+    high = lhs.astype(jnp.bfloat16)
+    low = (lhs - high.astype(jnp.float32)).astype(jnp.bfloat16)
+    if left:
+        return jnp.dot(rhs, high, preferred_element_type=jnp.float32) + jnp.dot(
+            rhs, low, preferred_element_type=jnp.float32
+        )
+    return jnp.dot(high, rhs, preferred_element_type=jnp.float32) + jnp.dot(
+        low, rhs, preferred_element_type=jnp.float32
+    )
+
+
+def stencil(y0, v, lo, hi, q, ty_ref, tz_ref, wide, inner):
     row_count = v.shape[0]
     halo = lo.shape[0]
     wide[0:halo, :] = lo
     wide[halo : halo + row_count, :] = v
     wide[halo + row_count : 2 * halo + row_count, :] = hi
+    ty = ty_ref[...]
+    tz = tz_ref[...]
+    first = pl.multiple_of(GY - y0, 8)
+    for plane in range(inner.shape[0] // GY):
+        block = wide[pl.ds(first + plane * GY, GY), :]
+        inner[plane * GY : (plane + 1) * GY, :] = split_dot(block, ty, True) + split_dot(
+            block, tz, False
+        )
     beside = wide[0:row_count, :] + wide[2 * halo : 2 * halo + row_count, :]
-    down = wide[halo - 1 : halo - 1 + row_count, :]
-    up = wide[halo + 1 : halo + 1 + row_count, :]
-    down_wrap = wide[2 * halo - 1 : 2 * halo - 1 + row_count, :]
-    up_wrap = wide[1 : 1 + row_count, :]
-    y = lax.broadcasted_iota(jnp.int32, v.shape, 0) + y0
-    for _ in range((row_count + GY - 2) // GY):
-        y = jnp.where(y >= GY, y - GY, y)
-    beside = beside + jnp.where(y == 0, down_wrap, down)
-    beside = beside + jnp.where(y == GY - 1, up_wrap, up)
-    high = v.astype(jnp.bfloat16)
-    low = (v - high.astype(jnp.float32)).astype(jnp.bfloat16)
-    tmat = t_ref[...]
-    beside = beside + jnp.dot(high, tmat, preferred_element_type=jnp.float32)
-    beside = beside + jnp.dot(low, tmat, preferred_element_type=jnp.float32)
+    beside = beside + inner[pl.ds(pl.multiple_of(y0, 8), row_count), :]
     return (beside + coupling * q) * (1.0 / 6.0)
 
 
-def sweep_kernel(final, sc_ref, v_ref, lo_ref, hi_ref, p_ref, t_ref, c_ref, *rest):
+def sweep_kernel(final, sc_ref, v_ref, lo_ref, hi_ref, p_ref, t_ref, cy_ref, cz_ref, *rest):
     y0 = sc_ref[0]
     part = p_ref[...].astype(jnp.float32)
     row_count = part.shape[0]
     halo = lo_ref.shape[-2]
     if final:
-        acc_ref, wide = rest
+        acc_ref, wide, inner = rest
 
         @pl.when(pl.program_id(0) == 0)
         def _():
             acc_ref[...] = jnp.zeros_like(acc_ref)
 
     else:
-        out_ref, fwd_ref, bwd_ref, wide = rest
+        out_ref, fwd_ref, bwd_ref, wide, inner = rest
     for j in range(v_ref.shape[0]):
         q = part * t_ref[j]
         new = stencil(
@@ -72,8 +79,10 @@
             lo_ref[j].astype(jnp.float32),
             hi_ref[j].astype(jnp.float32),
             q,
-            c_ref,
+            cy_ref,
+            cz_ref,
             wide,
+            inner,
         )
         if final:
             acc_ref[j] = acc_ref[j] + new * part
@@ -83,7 +92,7 @@
             bwd_ref[j] = new[0:halo].astype(jnp.bfloat16)
 
 
-def sweep_call(final, v, from_warm, lo, hi, partner, targets, tmat, scalars):
+def sweep_call(final, v, from_warm, lo, hi, partner, targets, tmats, scalars):
     orb, tgt, halo, width = lo.shape
     row_count = targets.shape[1]
     if from_warm:
@@ -95,7 +104,9 @@
     h_spec = pl.BlockSpec((None, tgt, halo, width), lambda i, sc: (i, 0, 0, 0))
     p_spec = pl.BlockSpec((None, row_count, width), lambda i, sc: (sc[2] + i, 0, 0))
     t_spec = pl.BlockSpec((tgt, row_count, width), lambda i, sc: (0, 0, 0))
-    c_spec = pl.BlockSpec((width, width), lambda i, sc: (0, 0))
+    cy_spec = pl.BlockSpec((GY, GY), lambda i, sc: (0, 0))
+    cz_spec = pl.BlockSpec((width, width), lambda i, sc: (0, 0))
+    planes = -(-(row_count + GY - math.gcd(row_count, GY)) // GY)
     cells = orb * tgt * row_count * width
     if final:
         out_shape = jax.ShapeDtypeStruct((tgt, row_count, width), jnp.float32)
@@ -122,9 +133,12 @@
     grid_spec = pltpu.PrefetchScalarGridSpec(
         num_scalar_prefetch=1,
         grid=(orb,),
-        in_specs=[v_spec, h_spec, h_spec, p_spec, t_spec, c_spec],
+        in_specs=[v_spec, h_spec, h_spec, p_spec, t_spec, cy_spec, cz_spec],
         out_specs=out_specs,
-        scratch_shapes=[pltpu.VMEM((row_count + 2 * halo, width), jnp.float32)],
+        scratch_shapes=[
+            pltpu.VMEM((row_count + 2 * halo, width), jnp.float32),
+            pltpu.VMEM((planes * GY, width), jnp.float32),
+        ],
     )
     return pl.pallas_call(
         functools.partial(sweep_kernel, final),
@@ -132,11 +146,11 @@
         out_shape=out_shape,
         compiler_params=pltpu.CompilerParams(dimension_semantics=("arbitrary",)),
         cost_estimate=pl.CostEstimate(
-            flops=cells * (4 * width + 24),
+            flops=cells * (8 * width + 16),
             transcendentals=0,
             bytes_accessed=in_bytes + out_bytes,
         ),
-    )(scalars, v, lo, hi, partner, targets, tmat)
+    )(scalars, v, lo, hi, partner, targets, *tmats)
 
 
 def exchange_halos(fwd, bwd):
@@ -222,7 +236,7 @@
     s_own = jnp.where(owners[0] == band, 0, 1).astype(jnp.int32)
     s_rem = 1 - s_own
     own_block = lax.dynamic_slice_in_dim(partner_pool, s_own * ORB, ORB, 0)
-    tmat = circulant(targets.shape[2])
+    tmat = (circulant(GY), circulant(targets.shape[2]))
     own_scalars = jnp.stack([y0, s_own, s_own * ORB]).astype(jnp.int32)
     rem_scalars = jnp.stack([y0, s_rem, jnp.zeros((), jnp.int32)]).astype(jnp.int32)
 

time: 217 us -> 220 us (1.014)
  Pallas kernels: 69.5 us -> 72.6 us
    pallas_call x6, Pallas kernels: 69.5 us -> 72.6 us  [sweep_call(): pl.pallas_call(functools.partial(sweep_kernel, final), grid_spec=grid_spe...]
    unnamed x31 -> x33, local copies, waits for them, and re-layouts: 5.12 us -> 5.24 us
  transfers between devices with their start and end apart: 23 -> 23, of which waited for: 10 -> 10; matrix products, arithmetic and copies ran while one was open for 6% -> 6% of each run, Pallas kernels for 27% -> 28%
where the time goes in v5:
time: 220 us; the launch traced here: 218 us
  waiting for transfers between devices  82.3 us (37%)
  Pallas kernels  72.6 us (33%)
  starting transfers between devices  36.3 us (16%)
  local copies, waits for them, and re-layouts  17.8 us (8%)
  other arithmetic  8.38 us (4%)
    pallas_call x6, Pallas kernels, sweep_call(): pl.pallas_call(functools.partial(sweep_kernel, final), grid_spec=grid_spe...  72.6 us
    ppermute x6, starting transfers between devices, exchange_halos(): lax.ppermute(bwd, 'domain', backward)  31.8 us
    ppermute x7, waiting for transfers between devices, butterfly_sum(): total = total + lax.ppermute(x, axis, pairs)  30.9 us
    ppermute x1, waiting for transfers between devices, swap_over_y(): lax.ppermute(plus, axes, shift(1))  25.7 us
    ppermute x1, waiting for transfers between devices, swap_over_y(): plus = lax.ppermute(block[:half], axes, shift(1))  20.7 us
    unnamed x33, local copies, waits for them, and re-layouts  5.24 us
  transfers between devices with their start and end apart: 23, of which 10 were waited for; matrix products, arithmetic and copies ran while one was open for 6% of the time, Pallas kernels for 28%

profile of v5, /device:TPU:16, one launch (start us, length us, event | category | flops | bytes accessed | tf_op | source)
XLA Modules:
  0.0 218.3 jit_solution(12320169617781725787)
XLA Ops:
  0.7 2.7 %dynamic-slice_bitcast_fusion = (bf16[8,2,288,192]{3,2,1,0:T(8,128)(2,1)S(1)}, bf16[8,2,288,192]{3,2,1,0:T(8,128)(2,1)S(1)}) fusion(bf16[2,8,2,288,192]{4,3,2,1,0:T(8,128)(2,1)} %v_ref.3, s32[]{:T(128)} %select_n.49, s32[]{:T(128)S(6)} %select_n.51), kind=kLoop, calls=%fused_computation.2 | loop fusion | bytes 7077896 | tf_op jit(solution)/shard_map/jit(dynamic_index_in_dim)/squeeze | solution.py:164
  3.4 1.9 fusion.8
  5.3 8.2 %collective-permute-start.1 = (bf16[8,2,192,192]{3,2,1,0:T(8,128)(2,1)}, bf16[8,2,192,192]{3,2,1,0:T(8,128)(2,1)}, u32[]{:S(2)}, u32[]{:S(2)}) collective-permute-start(bf16[8,2,192,192]{3,2,1,0:T(8,128)(2,1)} %get-tuple-element.79), channel_id=1, source_target_pairs={{1,0},{2,1},{3,2},{4,3},{5,4},{6,5},{7,6},{8,7},{9,8},{10,9},{11,1... | collective-permute-start | bytes 3538952 | tf_op jit(solution)/shard_map/ppermute | solution.py:160
  16.9 2.0 fusion.9
  18.9 20.7 %collective-permute-done.2 = bf16[4,288,192]{2,1,0:T(8,128)(2,1)S(1)} collective-permute-done((bf16[4,288,192]{2,1,0:T(8,128)(2,1)S(1)}, bf16[4,288,192]{2,1,0:T(8,128)(2,1)S(1)}, u32[]{:S(2)}, u32[]{:S(2)}) %collective-permute-start.2) | collective-permute-done | bytes 442400 | tf_op jit(solution)/shard_map/ppermute | solution.py:209
  39.6 2.2 %collective-permute-done.3 = bf16[4,288,192]{2,1,0:T(8,128)(2,1)S(1)} collective-permute-done((bf16[4,288,192]{2,1,0:T(8,128)(2,1)S(1)}, bf16[4,288,192]{2,1,0:T(8,128)(2,1)S(1)}, u32[]{:S(2)}, u32[]{:S(2)}) %collective-permute-start.3) | collective-permute-done | bytes 442400 | tf_op jit(solution)/shard_map/ppermute | solution.py:210
  42.7 6.0 %collective-permute-start.18 = (bf16[8,2,192,192]{3,2,1,0:T(8,128)(2,1)}, bf16[8,2,192,192]{3,2,1,0:T(8,128)(2,1)}, u32[]{:S(2)}, u32[]{:S(2)}) collective-permute-start(bf16[8,2,192,192]{3,2,1,0:T(8,128)(2,1)} %get-tuple-element.34), channel_id=1, source_target_pairs={{1,0},{2,1},{3,2},{4,3},{5,4},{6,5},{7,6},{8,7},{9,8},{10,9},{11,1... | collective-permute-start | bytes 3538952 | tf_op jit(solution)/shard_map/ppermute | solution.py:160
  52.5 12.1 %shard_map.46 = (f32[8,2,288,192]{3,2,1,0:T(8,128)}, bf16[8,2,192,192]{3,2,1,0:T(8,128)(2,1)}, bf16[8,2,192,192]{3,2,1,0:T(8,128)(2,1)}) custom-call(s32[3]{0:T(128)} %pad_add_fusion.sc_ref, bf16[2,8,2,288,192]{4,3,2,1,0:T(8,128)(2,1)} %v_ref.3, bf16[8,2,192,192]{3,2,1,0:T(8,128)(2,1)} %collective-permute-done.lo_ref, ...), custom_call_target="tpu_custom_call" | custom-call | flops 1373110272 | bytes 11354112 | tf_op jit(solution)/shard_map/pallas_call | solution.py:143
  64.7 25.7 %collective-permute-done.4 = bf16[4,288,192]{2,1,0:T(8,128)(2,1)S(1)} collective-permute-done((bf16[4,288,192]{2,1,0:T(8,128)(2,1)}, bf16[4,288,192]{2,1,0:T(8,128)(2,1)S(1)}, u32[]{:S(2)}, u32[]{:S(2)}) %collective-permute-start.4) | collective-permute-done | bytes 442400 | tf_op jit(solution)/shard_map/ppermute | solution.py:212
  90.4 2.7 %collective-permute-done.5 = bf16[4,288,192]{2,1,0:T(8,128)(2,1)} collective-permute-done((bf16[4,288,192]{2,1,0:T(8,128)(2,1)}, bf16[4,288,192]{2,1,0:T(8,128)(2,1)}, u32[]{:S(2)}, u32[]{:S(2)}) %collective-permute-start.5) | collective-permute-done | bytes 442400 | tf_op jit(solution)/shard_map/ppermute | solution.py:212
  95.8 12.0 %shard_map.49 = (f32[8,2,288,192]{3,2,1,0:T(8,128)}, bf16[8,2,192,192]{3,2,1,0:T(8,128)(2,1)}, bf16[8,2,192,192]{3,2,1,0:T(8,128)(2,1)}) custom-call(s32[3]{0:T(128)} %pad_add_fusion.1.sc_ref, bf16[2,8,2,288,192]{4,3,2,1,0:T(8,128)(2,1)} %v_ref.3, bf16[8,2,192,192]{3,2,1,0:T(8,128)(2,1)} %copy-done.8, ...), custom_call_target="tpu_custom_call" | custom-call | flops 1373110272 | bytes 11354112 | tf_op jit(solution)/shard_map/pallas_call | solution.py:143
  107.8 5.9 %collective-permute-start.20 = (bf16[8,2,192,192]{3,2,1,0:T(8,128)(2,1)}, bf16[8,2,192,192]{3,2,1,0:T(8,128)(2,1)}, u32[]{:S(2)}, u32[]{:S(2)}) collective-permute-start(bf16[8,2,192,192]{3,2,1,0:T(8,128)(2,1)} %get-tuple-element.37), channel_id=1, source_target_pairs={{1,0},{2,1},{3,2},{4,3},{5,4},{6,5},{7,6},{8,7},{9,8},{10,9},{11,1... | collective-permute-start | bytes 3538952 | tf_op jit(solution)/shard_map/ppermute | solution.py:160
  119.5 12.5 %shard_map.47 = (f32[8,2,288,192]{3,2,1,0:T(8,128)}, bf16[8,2,192,192]{3,2,1,0:T(8,128)(2,1)}, bf16[8,2,192,192]{3,2,1,0:T(8,128)(2,1)}) custom-call(s32[3]{0:T(128)} %pad_add_fusion.sc_ref, f32[8,2,288,192]{3,2,1,0:T(8,128)} %get-tuple-element.27.v_ref, bf16[8,2,192,192]{3,2,1,0:T(8,128)(2,1)} %collective-permute-done.13.lo_ref, ...), custom_call_target="tpu_custom_call" | custom-call | flops 1373110272 | bytes 13123584 | tf_op jit(solution)/shard_map/pallas_call | solution.py:143
  132.2 5.8 %collective-permute-start.16 = (bf16[8,2,192,192]{3,2,1,0:T(8,128)(2,1)}, bf16[8,2,192,192]{3,2,1,0:T(8,128)(2,1)}, u32[]{:S(2)}, u32[]{:S(2)}) collective-permute-start(bf16[8,2,192,192]{3,2,1,0:T(8,128)(2,1)} %get-tuple-element.32), channel_id=1, source_target_pairs={{1,0},{2,1},{3,2},{4,3},{5,4},{6,5},{7,6},{8,7},{9,8},{10,9},{11,1... | collective-permute-start | bytes 3538952 | tf_op jit(solution)/shard_map/ppermute | solution.py:160
  139.1 12.6 %shard_map.50 = (f32[8,2,288,192]{3,2,1,0:T(8,128)}, bf16[8,2,192,192]{3,2,1,0:T(8,128)(2,1)}, bf16[8,2,192,192]{3,2,1,0:T(8,128)(2,1)}) custom-call(s32[3]{0:T(128)} %pad_add_fusion.1.sc_ref, f32[8,2,288,192]{3,2,1,0:T(8,128)} %get-tuple-element.35.v_ref, bf16[8,2,192,192]{3,2,1,0:T(8,128)(2,1)} %copy-done.9, ...), custom_call_target="tpu_custom_call" | custom-call | flops 1373110272 | bytes 13123584 | tf_op jit(solution)/shard_map/pallas_call | solution.py:143
  151.7 6.0 %collective-permute-start.22 = (bf16[8,2,192,192]{3,2,1,0:T(8,128)(2,1)}, bf16[8,2,192,192]{3,2,1,0:T(8,128)(2,1)}, u32[]{:S(2)}, u32[]{:S(2)}) collective-permute-start(bf16[8,2,192,192]{3,2,1,0:T(8,128)(2,1)} %get-tuple-element.40), channel_id=1, source_target_pairs={{1,0},{2,1},{3,2},{4,3},{5,4},{6,5},{7,6},{8,7},{9,8},{10,9},{11,1... | collective-permute-start | bytes 3538952 | tf_op jit(solution)/shard_map/ppermute | solution.py:160
  158.3 12.4 %collective-permute-done.8 = f32[2,8,2]{1,2,0:T(2,128)S(1)} collective-permute-done((f32[2,8,2]{1,2,0:T(2,128)S(1)}, f32[2,8,2]{1,2,0:T(2,128)S(1)}, u32[]{:S(2)}, u32[]{:S(2)}) %collective-permute-start.8) | collective-permute-done | bytes 160 | tf_op jit(solution)/shard_map/ppermute | solution.py:189
  170.8 7.5 %collective-permute-done.9 = f32[2,8,2]{1,2,0:T(2,128)S(1)} collective-permute-done((f32[2,8,2]{1,2,0:T(2,128)S(1)}, f32[2,8,2]{1,2,0:T(2,128)S(1)}, u32[]{:S(2)}, u32[]{:S(2)}) %collective-permute-start.9) | collective-permute-done | bytes 160 | tf_op jit(solution)/shard_map/ppermute | solution.py:189
  178.3 3.6 %collective-permute-done.10 = f32[2,8,2]{1,2,0:T(2,128)S(1)} collective-permute-done((f32[2,8,2]{1,2,0:T(2,128)S(1)}, f32[2,8,2]{1,2,0:T(2,128)S(1)}, u32[]{:S(2)}, u32[]{:S(2)}) %collective-permute-start.10) | collective-permute-done | bytes 160 | tf_op jit(solution)/shard_map/ppermute | solution.py:189
  183.0 3.9 %collective-permute-done.11 = f32[2,8,2]{1,2,0:T(2,128)S(1)} collective-permute-done((f32[2,8,2]{1,2,0:T(2,128)S(1)}, f32[2,8,2]{1,2,0:T(2,128)S(1)}, u32[]{:S(2)}, u32[]{:S(2)}) %collective-permute-start.11) | collective-permute-done | bytes 160 | tf_op jit(solution)/shard_map/ppermute | solution.py:189
  188.3 2.3 %collective-permute-done.12 = f32[2,8,2]{1,2,0:T(2,128)S(1)} collective-permute-done((f32[2,8,2]{1,2,0:T(2,128)S(1)}, f32[2,8,2]{1,2,0:T(2,128)S(1)}, u32[]{:S(2)}, u32[]{:S(2)}) %collective-permute-start.12) | collective-permute-done | bytes 160 | tf_op jit(solution)/shard_map/ppermute | solution.py:189
  191.5 11.7 %shard_map.48 = f32[2,288,192]{2,1,0:T(8,128)} custom-call(s32[3]{0:T(128)} %pad_add_fusion.sc_ref, f32[8,2,288,192]{3,2,1,0:T(8,128)} %get-tuple-element.30.v_ref, bf16[8,2,192,192]{3,2,1,0:T(8,128)(2,1)} %collective-permute-done.15.lo_ref, bf16[8,2,192,192]{3,2,1,0:T(8,128)(2,1)} %collective-permute-done.16.hi_ref, bf16[32,288,192]{2,1,0:T(8,128)(2,1)} %p_ref.5, ...), custom_call_target="tpu_custom_call" | custom-call | flops 1373110272 | bytes 7667712 | tf_op jit(solution)/shard_map/pallas_call | solution.py:143
  203.3 11.8 %shard_map.51 = f32[2,288,192]{2,1,0:T(8,128)} custom-call(s32[3]{0:T(128)} %pad_add_fusion.1.sc_ref, f32[8,2,288,192]{3,2,1,0:T(8,128)} %get-tuple-element.38.v_ref, bf16[8,2,192,192]{3,2,1,0:T(8,128)(2,1)} %collective-permute-done.21.lo_ref, bf16[8,2,192,192]{3,2,1,0:T(8,128)(2,1)} %collective-permute-done.22.hi_ref, bf16[8,288,192]{2,1,0:T(8,128)(2,1)} %copy-done.1, ...), custom_call_target="tpu_custom_call" | custom-call | flops 1373110272 | bytes 7667712 | tf_op jit(solution)/shard_map/pallas_call | solution.py:143
  215.1 3.2 %add_subtract_fusion = f32[2,288,192]{2,1,0:T(8,128)} fusion(f32[2,288,192]{2,1,0:T(8,128)S(1)} %copy-done.7, f32[2,288,192]{2,1,0:T(8,128)} %shard_map.51, f32[288,192]{1,0:T(8,128)S(1)} %get-tuple-element.72, f32[2]{0:T(128)S(1)} %get-tuple-element.44, f32[288,192]{1,0:T(8,128)} %get-tuple-element.73, f32[2]{0:T(128)S(1)} %get-tuple-element.45, ...), kind=kLoop, calls=%fused_computation.5 | loop fusion | flops 3760128 | bytes 4866176 | tf_op jit(solution)/shard_map/sub | solution.py:265
  (86 shorter events, 22.0 us)
Async XLA Ops:
  5.3 36.5 %collective-permute-start = (bf16[8,2,192,192]{3,2,1,0:T(8,128)(2,1)}, bf16[8,2,192,192]{3,2,1,0:T(8,128)(2,1)}, u32[]{:S(2)}, u32[]{:S(2)}) collective-permute-start(bf16[8,2,192,192]{3,2,1,0:T(8,128)(2,1)} %get-tuple-element.80), channel_id=1, source_target_pairs={{0,1},{1,2},{2,3},{3,4},{4,5},{5,6},{6,7},{7,8},{8,9},{9,10},{10,1... | collective-permute-start | bytes 3538952 | tf_op jit(solution)/shard_map/ppermute | solution.py:160
  5.3 36.5 %collective-permute-start.1 = (bf16[8,2,192,192]{3,2,1,0:T(8,128)(2,1)}, bf16[8,2,192,192]{3,2,1,0:T(8,128)(2,1)}, u32[]{:S(2)}, u32[]{:S(2)}) collective-permute-start(bf16[8,2,192,192]{3,2,1,0:T(8,128)(2,1)} %get-tuple-element.79), channel_id=1, source_target_pairs={{1,0},{2,1},{3,2},{4,3},{5,4},{6,5},{7,6},{8,7},{9,8},{10,9},{11,1... | collective-permute-start | bytes 3538952 | tf_op jit(solution)/shard_map/ppermute | solution.py:160
  14.8 24.8 %collective-permute-start.2 = (bf16[4,288,192]{2,1,0:T(8,128)(2,1)S(1)}, bf16[4,288,192]{2,1,0:T(8,128)(2,1)S(1)}, u32[]{:S(2)}, u32[]{:S(2)}) collective-permute-start(bf16[4,288,192]{2,1,0:T(8,128)(2,1)S(1)} %get-tuple-element.60), channel_id=1, source_target_pairs={{0,64},{1,65},{2,66},{3,67},{4,68},{5,69},{6,70},{7,71},{8,72},{9,... | collective-permute-start | bytes 1327112 | tf_op jit(solution)/shard_map/ppermute | solution.py:209
  15.7 26.2 %collective-permute-start.3 = (bf16[4,288,192]{2,1,0:T(8,128)(2,1)S(1)}, bf16[4,288,192]{2,1,0:T(8,128)(2,1)S(1)}, u32[]{:S(2)}, u32[]{:S(2)}) collective-permute-start(bf16[4,288,192]{2,1,0:T(8,128)(2,1)S(1)} %get-tuple-element.59), channel_id=1, source_target_pairs={{0,192},{1,193},{2,194},{3,195},{4,196},{5,197},{6,198},{7,199},{8... | collective-permute-start | bytes 1327112 | tf_op jit(solution)/shard_map/ppermute | solution.py:210
  42.7 51.6 %collective-permute-start.17 = (bf16[8,2,192,192]{3,2,1,0:T(8,128)(2,1)}, bf16[8,2,192,192]{3,2,1,0:T(8,128)(2,1)S(1)}, u32[]{:S(2)}, u32[]{:S(2)}) collective-permute-start(bf16[8,2,192,192]{3,2,1,0:T(8,128)(2,1)} %get-tuple-element.33), channel_id=1, source_target_pairs={{0,1},{1,2},{2,3},{3,4},{4,5},{5,6},{6,7},{7,8},{8,9},{9,10},{10,1... | collective-permute-start | bytes 3538952 | tf_op jit(solution)/shard_map/ppermute | solution.py:160
  42.7 51.6 %collective-permute-start.18 = (bf16[8,2,192,192]{3,2,1,0:T(8,128)(2,1)}, bf16[8,2,192,192]{3,2,1,0:T(8,128)(2,1)}, u32[]{:S(2)}, u32[]{:S(2)}) collective-permute-start(bf16[8,2,192,192]{3,2,1,0:T(8,128)(2,1)} %get-tuple-element.34), channel_id=1, source_target_pairs={{1,0},{2,1},{3,2},{4,3},{5,4},{6,5},{7,6},{8,7},{9,8},{10,9},{11,1... | collective-permute-start | bytes 3538952 | tf_op jit(solution)/shard_map/ppermute | solution.py:160
  48.6 41.8 %collective-permute-start.4 = (bf16[4,288,192]{2,1,0:T(8,128)(2,1)}, bf16[4,288,192]{2,1,0:T(8,128)(2,1)S(1)}, u32[]{:S(2)}, u32[]{:S(2)}) collective-permute-start(bf16[4,288,192]{2,1,0:T(8,128)(2,1)} %copy-done.15), channel_id=1, source_target_pairs={{0,64},{1,65},{2,66},{3,67},{4,68},{5,69},{6,70},{7,71},{8,72},{9,... | collective-permute-start | bytes 1327112 | tf_op jit(solution)/shard_map/ppermute | solution.py:212
  49.7 43.5 %collective-permute-start.5 = (bf16[4,288,192]{2,1,0:T(8,128)(2,1)}, bf16[4,288,192]{2,1,0:T(8,128)(2,1)}, u32[]{:S(2)}, u32[]{:S(2)}) collective-permute-start(bf16[4,288,192]{2,1,0:T(8,128)(2,1)} %copy-done.14), channel_id=1, source_target_pairs={{0,192},{1,193},{2,194},{3,195},{4,196},{5,197},{6,198},{7,199},{8... | collective-permute-start | bytes 1327112 | tf_op jit(solution)/shard_map/ppermute | solution.py:212
  64.7 54.8 %collective-permute-start.13 = (bf16[8,2,192,192]{3,2,1,0:T(8,128)(2,1)}, bf16[8,2,192,192]{3,2,1,0:T(8,128)(2,1)}, u32[]{:S(2)}, u32[]{:S(2)}) collective-permute-start(bf16[8,2,192,192]{3,2,1,0:T(8,128)(2,1)} %get-tuple-element.28), channel_id=1, source_target_pairs={{0,1},{1,2},{2,3},{3,4},{4,5},{5,6},{6,7},{7,8},{8,9},{9,10},{10,1... | collective-permute-start | bytes 3538952 | tf_op jit(solution)/shard_map/ppermute | solution.py:160
  90.4 29.1 %collective-permute-start.14 = (bf16[8,2,192,192]{3,2,1,0:T(8,128)(2,1)}, bf16[8,2,192,192]{3,2,1,0:T(8,128)(2,1)}, u32[]{:S(2)}, u32[]{:S(2)}) collective-permute-start(bf16[8,2,192,192]{3,2,1,0:T(8,128)(2,1)} %get-tuple-element.29), channel_id=1, source_target_pairs={{1,0},{2,1},{3,2},{4,3},{5,4},{6,5},{7,6},{8,7},{9,8},{10,9},{11,1... | collective-permute-start | bytes 3538952 | tf_op jit(solution)/shard_map/ppermute | solution.py:160
  107.7 30.2 %collective-permute-start.19 = (bf16[8,2,192,192]{3,2,1,0:T(8,128)(2,1)}, bf16[8,2,192,192]{3,2,1,0:T(8,128)(2,1)S(1)}, u32[]{:S(2)}, u32[]{:S(2)}) collective-permute-start(bf16[8,2,192,192]{3,2,1,0:T(8,128)(2,1)} %get-tuple-element.36), channel_id=1, source_target_pairs={{0,1},{1,2},{2,3},{3,4},{4,5},{5,6},{6,7},{7,8},{8,9},{9,10},{10,1... | collective-permute-start | bytes 3538952 | tf_op jit(solution)/shard_map/ppermute | solution.py:160
  107.8 30.2 %collective-permute-start.20 = (bf16[8,2,192,192]{3,2,1,0:T(8,128)(2,1)}, bf16[8,2,192,192]{3,2,1,0:T(8,128)(2,1)}, u32[]{:S(2)}, u32[]{:S(2)}) collective-permute-start(bf16[8,2,192,192]{3,2,1,0:T(8,128)(2,1)} %get-tuple-element.37), channel_id=1, source_target_pairs={{1,0},{2,1},{3,2},{4,3},{5,4},{6,5},{7,6},{8,7},{9,8},{10,9},{11,1... | collective-permute-start | bytes 3538952 | tf_op jit(solution)/shard_map/ppermute | solution.py:160
  118.3 1.2 collective-permute-start.6
  119.5 38.2 %collective-permute-start.7 = (f32[2,8,2]{1,2,0:T(2,128)S(1)}, f32[2,8,2]{1,2,0:T(2,128)}, u32[]{:S(2)}, u32[]{:S(2)}) collective-permute-start(f32[2,8,2]{1,2,0:T(2,128)S(1)} %fusion.7), channel_id=1, source_target_pairs={{0,2},{1,3},{2,0},{3,1},{4,6},{5,7},{6,4},{7,5},{8,10},{9,11},{10,... | collective-permute-start | bytes 392 | tf_op jit(solution)/shard_map/ppermute | solution.py:189
  132.0 59.5 %collective-permute-start.15 = (bf16[8,2,192,192]{3,2,1,0:T(8,128)(2,1)}, bf16[8,2,192,192]{3,2,1,0:T(8,128)(2,1)}, u32[]{:S(2)}, u32[]{:S(2)}) collective-permute-start(bf16[8,2,192,192]{3,2,1,0:T(8,128)(2,1)} %get-tuple-element.31), channel_id=1, source_target_pairs={{0,1},{1,2},{2,3},{3,4},{4,5},{5,6},{6,7},{7,8},{8,9},{9,10},{10,1... | collective-permute-start | bytes 3538952 | tf_op jit(solution)/shard_map/ppermute | solution.py:160
  132.2 59.3 %collective-permute-start.16 = (bf16[8,2,192,192]{3,2,1,0:T(8,128)(2,1)}, bf16[8,2,192,192]{3,2,1,0:T(8,128)(2,1)}, u32[]{:S(2)}, u32[]{:S(2)}) collective-permute-start(bf16[8,2,192,192]{3,2,1,0:T(8,128)(2,1)} %get-tuple-element.32), channel_id=1, source_target_pairs={{1,0},{2,1},{3,2},{4,3},{5,4},{6,5},{7,6},{8,7},{9,8},{10,9},{11,1... | collective-permute-start | bytes 3538952 | tf_op jit(solution)/shard_map/ppermute | solution.py:160
  139.1 42.7 %copy-start.6 = (f32[8,288,192]{2,1,0:T(8,128)S(1)}, f32[8,288,192]{2,1,0:T(8,128)}, u32[]{:S(2)}) copy-start(f32[8,288,192]{2,1,0:T(8,128)} %copy-done.5) | copy-start | bytes 5308420
  151.7 51.5 %collective-permute-start.21 = (bf16[8,2,192,192]{3,2,1,0:T(8,128)(2,1)}, bf16[8,2,192,192]{3,2,1,0:T(8,128)(2,1)}, u32[]{:S(2)}, u32[]{:S(2)}) collective-permute-start(bf16[8,2,192,192]{3,2,1,0:T(8,128)(2,1)} %get-tuple-element.39), channel_id=1, source_target_pairs={{0,1},{1,2},{2,3},{3,4},{4,5},{5,6},{6,7},{7,8},{8,9},{9,10},{10,1... | collective-permute-start | bytes 3538952 | tf_op jit(solution)/shard_map/ppermute | solution.py:160
  151.7 51.5 %collective-permute-start.22 = (bf16[8,2,192,192]{3,2,1,0:T(8,128)(2,1)}, bf16[8,2,192,192]{3,2,1,0:T(8,128)(2,1)}, u32[]{:S(2)}, u32[]{:S(2)}) collective-permute-start(bf16[8,2,192,192]{3,2,1,0:T(8,128)(2,1)} %get-tuple-element.40), channel_id=1, source_target_pairs={{1,0},{2,1},{3,2},{4,3},{5,4},{6,5},{7,6},{8,7},{9,8},{10,9},{11,1... | collective-permute-start | bytes 3538952 | tf_op jit(solution)/shard_map/ppermute | solution.py:160
  158.3 12.4 %collective-permute-start.8 = (f32[2,8,2]{1,2,0:T(2,128)S(1)}, f32[2,8,2]{1,2,0:T(2,128)S(1)}, u32[]{:S(2)}, u32[]{:S(2)}) collective-permute-start(f32[2,8,2]{1,2,0:T(2,128)S(1)} %fusion.10), channel_id=1, source_target_pairs={{0,4},{1,5},{2,6},{3,7},{4,0},{5,1},{6,2},{7,3},{8,12},{9,13},{10,... | collective-permute-start | bytes 392 | tf_op jit(solution)/shard_map/ppermute | solution.py:189
  170.8 7.5 %collective-permute-start.9 = (f32[2,8,2]{1,2,0:T(2,128)S(1)}, f32[2,8,2]{1,2,0:T(2,128)S(1)}, u32[]{:S(2)}, u32[]{:S(2)}) collective-permute-start(f32[2,8,2]{1,2,0:T(2,128)S(1)} %add.142), channel_id=1, source_target_pairs={{0,8},{1,9},{2,10},{3,11},{4,12},{5,13},{6,14},{7,15},{8,0},{9,1},... | collective-permute-start | bytes 392 | tf_op jit(solution)/shard_map/ppermute | solution.py:189
  178.3 3.6 %collective-permute-start.10 = (f32[2,8,2]{1,2,0:T(2,128)S(1)}, f32[2,8,2]{1,2,0:T(2,128)S(1)}, u32[]{:S(2)}, u32[]{:S(2)}) collective-permute-start(f32[2,8,2]{1,2,0:T(2,128)S(1)} %add.143), channel_id=1, source_target_pairs={{0,16},{1,17},{2,18},{3,19},{4,20},{5,21},{6,22},{7,23},{8,24},{9,... | collective-permute-start | bytes 392 | tf_op jit(solution)/shard_map/ppermute | solution.py:189
  181.9 5.1 %collective-permute-start.11 = (f32[2,8,2]{1,2,0:T(2,128)S(1)}, f32[2,8,2]{1,2,0:T(2,128)S(1)}, u32[]{:S(2)}, u32[]{:S(2)}) collective-permute-start(f32[2,8,2]{1,2,0:T(2,128)S(1)} %add.144), channel_id=1, source_target_pairs={{0,32},{1,33},{2,34},{3,35},{4,36},{5,37},{6,38},{7,39},{8,40},{9,... | collective-permute-start | bytes 392 | tf_op jit(solution)/shard_map/ppermute | solution.py:189
  187.0 3.6 %collective-permute-start.12 = (f32[2,8,2]{1,2,0:T(2,128)S(1)}, f32[2,8,2]{1,2,0:T(2,128)S(1)}, u32[]{:S(2)}, u32[]{:S(2)}) collective-permute-start(f32[2,8,2]{1,2,0:T(2,128)S(1)} %add.145), channel_id=1, source_target_pairs={{0,64},{1,65},{2,66},{3,67},{4,68},{5,69},{6,70},{7,71},{8,72},{9,... | collective-permute-start | bytes 392 | tf_op jit(solution)/shard_map/ppermute | solution.py:189
  (15 other events, 83.6 us)

commit v6 on v5

--- a/solution.py
+++ b/solution.py
@@ -87,9 +87,10 @@
         if final:
             acc_ref[j] = acc_ref[j] + new * part
         else:
-            out_ref[j] = new
-            fwd_ref[j] = new[row_count - halo : row_count].astype(jnp.bfloat16)
-            bwd_ref[j] = new[0:halo].astype(jnp.bfloat16)
+            rounded = new.astype(jnp.bfloat16)
+            out_ref[j] = rounded
+            fwd_ref[j] = rounded[row_count - halo : row_count]
+            bwd_ref[j] = rounded[0:halo]
 
 
 def sweep_call(final, v, from_warm, lo, hi, partner, targets, tmats, scalars):
@@ -114,7 +115,7 @@
         out_bytes = tgt * row_count * width * 4
     else:
         out_shape = (
-            jax.ShapeDtypeStruct((orb, tgt, row_count, width), jnp.float32),
+            jax.ShapeDtypeStruct((orb, tgt, row_count, width), jnp.bfloat16),
             jax.ShapeDtypeStruct((orb, tgt, halo, width), jnp.bfloat16),
             jax.ShapeDtypeStruct((orb, tgt, halo, width), jnp.bfloat16),
         )
@@ -123,7 +124,7 @@
             h_spec,
             h_spec,
         )
-        out_bytes = cells * 4 + 2 * orb * tgt * halo * width * 2
+        out_bytes = cells * 2 + 2 * orb * tgt * halo * width * 2
     in_bytes = (
         cells * v.dtype.itemsize
         + 2 * orb * tgt * halo * width * 2

time: 220 us -> 218 us (level)
  Pallas kernels: 72.6 us -> 69.5 us
    pallas_call x6, Pallas kernels: 72.6 us -> 69.5 us  [sweep_call(): pl.pallas_call(functools.partial(sweep_kernel, final), grid_spec=grid_spe...]
  transfers between devices with their start and end apart: 23 -> 23, of which waited for: 10 -> 10; matrix products, arithmetic and copies ran while one was open for 6% -> 6% of each run, Pallas kernels for 28% -> 27%
where the time goes in v6:
time: 218 us; the launch traced here: 217 us
  waiting for transfers between devices  83.5 us (38%)
  Pallas kernels  69.5 us (32%)
  starting transfers between devices  36.2 us (17%)
  local copies, waits for them, and re-layouts  17.9 us (8%)
  other arithmetic  8.6 us (4%)
    pallas_call x6, Pallas kernels, sweep_call(): pl.pallas_call(functools.partial(sweep_kernel, final), grid_spec=grid_spe...  69.5 us
    ppermute x6, starting transfers between devices, exchange_halos(): lax.ppermute(bwd, 'domain', backward)  31.9 us
    ppermute x7, waiting for transfers between devices, butterfly_sum(): total = total + lax.ppermute(x, axis, pairs)  31.7 us
    ppermute x1, waiting for transfers between devices, swap_over_y(): lax.ppermute(plus, axes, shift(1))  26.1 us
    ppermute x1, waiting for transfers between devices, swap_over_y(): plus = lax.ppermute(block[:half], axes, shift(1))  20.7 us
    unnamed x33, local copies, waits for them, and re-layouts  5.39 us
  transfers between devices with their start and end apart: 23, of which 10 were waited for; matrix products, arithmetic and copies ran while one was open for 6% of the time, Pallas kernels for 27%

profile of v6, /device:TPU:16, one launch (start us, length us, event | category | flops | bytes accessed | tf_op | source)
XLA Modules:
  0.0 216.7 jit_solution(2932743466085830044)
XLA Ops:
  0.7 2.7 %dynamic-slice_bitcast_fusion = (bf16[8,2,288,192]{3,2,1,0:T(8,128)(2,1)S(1)}, bf16[8,2,288,192]{3,2,1,0:T(8,128)(2,1)S(1)}) fusion(bf16[2,8,2,288,192]{4,3,2,1,0:T(8,128)(2,1)} %v_ref.3, s32[]{:T(128)} %select_n.49, s32[]{:T(128)S(6)} %select_n.51), kind=kLoop, calls=%fused_computation.2 | loop fusion | bytes 7077896 | tf_op jit(solution)/shard_map/jit(dynamic_index_in_dim)/squeeze | solution.py:165
  3.4 1.9 fusion.8
  5.3 8.2 %collective-permute-start.1 = (bf16[8,2,192,192]{3,2,1,0:T(8,128)(2,1)}, bf16[8,2,192,192]{3,2,1,0:T(8,128)(2,1)}, u32[]{:S(2)}, u32[]{:S(2)}) collective-permute-start(bf16[8,2,192,192]{3,2,1,0:T(8,128)(2,1)} %get-tuple-element.79), channel_id=1, source_target_pairs={{1,0},{2,1},{3,2},{4,3},{5,4},{6,5},{7,6},{8,7},{9,8},{10,9},{11,1... | collective-permute-start | bytes 3538952 | tf_op jit(solution)/shard_map/ppermute | solution.py:161
  16.9 2.0 fusion.9
  18.9 20.7 %collective-permute-done.2 = bf16[4,288,192]{2,1,0:T(8,128)(2,1)S(1)} collective-permute-done((bf16[4,288,192]{2,1,0:T(8,128)(2,1)S(1)}, bf16[4,288,192]{2,1,0:T(8,128)(2,1)S(1)}, u32[]{:S(2)}, u32[]{:S(2)}) %collective-permute-start.2) | collective-permute-done | bytes 442400 | tf_op jit(solution)/shard_map/ppermute | solution.py:210
  39.6 2.2 %collective-permute-done.3 = bf16[4,288,192]{2,1,0:T(8,128)(2,1)S(1)} collective-permute-done((bf16[4,288,192]{2,1,0:T(8,128)(2,1)S(1)}, bf16[4,288,192]{2,1,0:T(8,128)(2,1)S(1)}, u32[]{:S(2)}, u32[]{:S(2)}) %collective-permute-start.3) | collective-permute-done | bytes 442400 | tf_op jit(solution)/shard_map/ppermute | solution.py:211
  42.6 6.0 %collective-permute-start.18 = (bf16[8,2,192,192]{3,2,1,0:T(8,128)(2,1)}, bf16[8,2,192,192]{3,2,1,0:T(8,128)(2,1)}, u32[]{:S(2)}, u32[]{:S(2)}) collective-permute-start(bf16[8,2,192,192]{3,2,1,0:T(8,128)(2,1)} %get-tuple-element.34), channel_id=1, source_target_pairs={{1,0},{2,1},{3,2},{4,3},{5,4},{6,5},{7,6},{8,7},{9,8},{10,9},{11,1... | collective-permute-start | bytes 3538952 | tf_op jit(solution)/shard_map/ppermute | solution.py:161
  52.7 11.6 %shard_map.46 = (bf16[8,2,288,192]{3,2,1,0:T(8,128)(2,1)}, bf16[8,2,192,192]{3,2,1,0:T(8,128)(2,1)}, bf16[8,2,192,192]{3,2,1,0:T(8,128)(2,1)}) custom-call(s32[3]{0:T(128)} %pad_add_fusion.sc_ref, bf16[2,8,2,288,192]{4,3,2,1,0:T(8,128)(2,1)} %v_ref.3, bf16[8,2,192,192]{3,2,1,0:T(8,128)(2,1)} %collective-permute-done.lo_ref, ...), custom_call_target="tpu_custom_call" | custom-call | flops 1373110272 | bytes 9584640 | tf_op jit(solution)/shard_map/pallas_call | solution.py:144
  64.3 26.1 %collective-permute-done.4 = bf16[4,288,192]{2,1,0:T(8,128)(2,1)S(1)} collective-permute-done((bf16[4,288,192]{2,1,0:T(8,128)(2,1)}, bf16[4,288,192]{2,1,0:T(8,128)(2,1)S(1)}, u32[]{:S(2)}, u32[]{:S(2)}) %collective-permute-start.4) | collective-permute-done | bytes 442400 | tf_op jit(solution)/shard_map/ppermute | solution.py:213
  90.4 2.8 %collective-permute-done.5 = bf16[4,288,192]{2,1,0:T(8,128)(2,1)} collective-permute-done((bf16[4,288,192]{2,1,0:T(8,128)(2,1)}, bf16[4,288,192]{2,1,0:T(8,128)(2,1)}, u32[]{:S(2)}, u32[]{:S(2)}) %collective-permute-start.5) | collective-permute-done | bytes 442400 | tf_op jit(solution)/shard_map/ppermute | solution.py:213
  95.9 11.7 %shard_map.49 = (bf16[8,2,288,192]{3,2,1,0:T(8,128)(2,1)}, bf16[8,2,192,192]{3,2,1,0:T(8,128)(2,1)}, bf16[8,2,192,192]{3,2,1,0:T(8,128)(2,1)}) custom-call(s32[3]{0:T(128)} %pad_add_fusion.1.sc_ref, bf16[2,8,2,288,192]{4,3,2,1,0:T(8,128)(2,1)} %v_ref.3, bf16[8,2,192,192]{3,2,1,0:T(8,128)(2,1)} %copy-done.8, ...), custom_call_target="tpu_custom_call" | custom-call | flops 1373110272 | bytes 9584640 | tf_op jit(solution)/shard_map/pallas_call | solution.py:144
  107.6 6.0 %collective-permute-start.20 = (bf16[8,2,192,192]{3,2,1,0:T(8,128)(2,1)}, bf16[8,2,192,192]{3,2,1,0:T(8,128)(2,1)}, u32[]{:S(2)}, u32[]{:S(2)}) collective-permute-start(bf16[8,2,192,192]{3,2,1,0:T(8,128)(2,1)} %get-tuple-element.37), channel_id=1, source_target_pairs={{1,0},{2,1},{3,2},{4,3},{5,4},{6,5},{7,6},{8,7},{9,8},{10,9},{11,1... | collective-permute-start | bytes 3538952 | tf_op jit(solution)/shard_map/ppermute | solution.py:161
  119.4 11.7 %shard_map.47 = (bf16[8,2,288,192]{3,2,1,0:T(8,128)(2,1)}, bf16[8,2,192,192]{3,2,1,0:T(8,128)(2,1)}, bf16[8,2,192,192]{3,2,1,0:T(8,128)(2,1)}) custom-call(s32[3]{0:T(128)} %pad_add_fusion.sc_ref, bf16[8,2,288,192]{3,2,1,0:T(8,128)(2,1)} %get-tuple-element.27.v_ref, bf16[8,2,192,192]{3,2,1,0:T(8,128)(2,1)} %collective-permute-done.13.lo_ref, ...), custom_call_target="tpu_custom_call" | custom-call | flops 1373110272 | bytes 9584640 | tf_op jit(solution)/shard_map/pallas_call | solution.py:144
  131.2 5.8 %collective-permute-start.16 = (bf16[8,2,192,192]{3,2,1,0:T(8,128)(2,1)}, bf16[8,2,192,192]{3,2,1,0:T(8,128)(2,1)}, u32[]{:S(2)}, u32[]{:S(2)}) collective-permute-start(bf16[8,2,192,192]{3,2,1,0:T(8,128)(2,1)} %get-tuple-element.32), channel_id=1, source_target_pairs={{1,0},{2,1},{3,2},{4,3},{5,4},{6,5},{7,6},{8,7},{9,8},{10,9},{11,1... | collective-permute-start | bytes 3538952 | tf_op jit(solution)/shard_map/ppermute | solution.py:161
  138.2 11.7 %shard_map.50 = (bf16[8,2,288,192]{3,2,1,0:T(8,128)(2,1)}, bf16[8,2,192,192]{3,2,1,0:T(8,128)(2,1)}, bf16[8,2,192,192]{3,2,1,0:T(8,128)(2,1)}) custom-call(s32[3]{0:T(128)} %pad_add_fusion.1.sc_ref, bf16[8,2,288,192]{3,2,1,0:T(8,128)(2,1)} %get-tuple-element.35.v_ref, bf16[8,2,192,192]{3,2,1,0:T(8,128)(2,1)} %copy-done.9, ...), custom_call_target="tpu_custom_call" | custom-call | flops 1373110272 | bytes 9584640 | tf_op jit(solution)/shard_map/pallas_call | solution.py:144
  150.0 6.0 %collective-permute-start.22 = (bf16[8,2,192,192]{3,2,1,0:T(8,128)(2,1)}, bf16[8,2,192,192]{3,2,1,0:T(8,128)(2,1)}, u32[]{:S(2)}, u32[]{:S(2)}) collective-permute-start(bf16[8,2,192,192]{3,2,1,0:T(8,128)(2,1)} %get-tuple-element.40), channel_id=1, source_target_pairs={{1,0},{2,1},{3,2},{4,3},{5,4},{6,5},{7,6},{8,7},{9,8},{10,9},{11,1... | collective-permute-start | bytes 3538952 | tf_op jit(solution)/shard_map/ppermute | solution.py:161
  156.6 13.2 %collective-permute-done.8 = f32[2,8,2]{1,2,0:T(2,128)S(1)} collective-permute-done((f32[2,8,2]{1,2,0:T(2,128)S(1)}, f32[2,8,2]{1,2,0:T(2,128)S(1)}, u32[]{:S(2)}, u32[]{:S(2)}) %collective-permute-start.8) | collective-permute-done | bytes 160 | tf_op jit(solution)/shard_map/ppermute | solution.py:190
  169.8 7.5 %collective-permute-done.9 = f32[2,8,2]{1,2,0:T(2,128)S(1)} collective-permute-done((f32[2,8,2]{1,2,0:T(2,128)S(1)}, f32[2,8,2]{1,2,0:T(2,128)S(1)}, u32[]{:S(2)}, u32[]{:S(2)}) %collective-permute-start.9) | collective-permute-done | bytes 160 | tf_op jit(solution)/shard_map/ppermute | solution.py:190
  177.3 3.6 %collective-permute-done.10 = f32[2,8,2]{1,2,0:T(2,128)S(1)} collective-permute-done((f32[2,8,2]{1,2,0:T(2,128)S(1)}, f32[2,8,2]{1,2,0:T(2,128)S(1)}, u32[]{:S(2)}, u32[]{:S(2)}) %collective-permute-start.10) | collective-permute-done | bytes 160 | tf_op jit(solution)/shard_map/ppermute | solution.py:190
  182.0 4.0 %collective-permute-done.11 = f32[2,8,2]{1,2,0:T(2,128)S(1)} collective-permute-done((f32[2,8,2]{1,2,0:T(2,128)S(1)}, f32[2,8,2]{1,2,0:T(2,128)S(1)}, u32[]{:S(2)}, u32[]{:S(2)}) %collective-permute-start.11) | collective-permute-done | bytes 160 | tf_op jit(solution)/shard_map/ppermute | solution.py:190
  187.3 2.3 %collective-permute-done.12 = f32[2,8,2]{1,2,0:T(2,128)S(1)} collective-permute-done((f32[2,8,2]{1,2,0:T(2,128)S(1)}, f32[2,8,2]{1,2,0:T(2,128)S(1)}, u32[]{:S(2)}, u32[]{:S(2)}) %collective-permute-start.12) | collective-permute-done | bytes 160 | tf_op jit(solution)/shard_map/ppermute | solution.py:190
  190.6 11.3 %shard_map.48 = f32[2,288,192]{2,1,0:T(8,128)} custom-call(s32[3]{0:T(128)} %pad_add_fusion.sc_ref, bf16[8,2,288,192]{3,2,1,0:T(8,128)(2,1)} %get-tuple-element.30.v_ref, bf16[8,2,192,192]{3,2,1,0:T(8,128)(2,1)} %collective-permute-done.15.lo_ref, bf16[8,2,192,192]{3,2,1,0:T(8,128)(2,1)} %collective-permute-done.16.hi_ref, bf16[32,288,192]{2,1,0:T(8,128)(2,1)} %p_ref.5, ...), custom_call_target="tpu_custom_call" | custom-call | flops 1373110272 | bytes 5898240 | tf_op jit(solution)/shard_map/pallas_call | solution.py:144
  202.0 11.5 %shard_map.51 = f32[2,288,192]{2,1,0:T(8,128)} custom-call(s32[3]{0:T(128)} %pad_add_fusion.1.sc_ref, bf16[8,2,288,192]{3,2,1,0:T(8,128)(2,1)} %get-tuple-element.38.v_ref, bf16[8,2,192,192]{3,2,1,0:T(8,128)(2,1)} %collective-permute-done.21.lo_ref, bf16[8,2,192,192]{3,2,1,0:T(8,128)(2,1)} %collective-permute-done.22.hi_ref, bf16[8,288,192]{2,1,0:T(8,128)(2,1)} %copy-done.1, ...), custom_call_target="tpu_custom_call" | custom-call | flops 1373110272 | bytes 5898240 | tf_op jit(solution)/shard_map/pallas_call | solution.py:144
  213.5 3.2 %add_subtract_fusion = f32[2,288,192]{2,1,0:T(8,128)} fusion(f32[2,288,192]{2,1,0:T(8,128)S(1)} %copy-done.7, f32[2,288,192]{2,1,0:T(8,128)} %shard_map.51, f32[288,192]{1,0:T(8,128)S(1)} %get-tuple-element.72, f32[2]{0:T(128)S(1)} %get-tuple-element.44, f32[288,192]{1,0:T(8,128)} %get-tuple-element.73, f32[2]{0:T(128)S(1)} %get-tuple-element.45, ...), kind=kLoop, calls=%fused_computation.5 | loop fusion | flops 3760128 | bytes 4866176 | tf_op jit(solution)/shard_map/sub | solution.py:266
  (86 shorter events, 22.2 us)
Async XLA Ops:
  5.3 36.5 %collective-permute-start = (bf16[8,2,192,192]{3,2,1,0:T(8,128)(2,1)}, bf16[8,2,192,192]{3,2,1,0:T(8,128)(2,1)}, u32[]{:S(2)}, u32[]{:S(2)}) collective-permute-start(bf16[8,2,192,192]{3,2,1,0:T(8,128)(2,1)} %get-tuple-element.80), channel_id=1, source_target_pairs={{0,1},{1,2},{2,3},{3,4},{4,5},{5,6},{6,7},{7,8},{8,9},{9,10},{10,1... | collective-permute-start | bytes 3538952 | tf_op jit(solution)/shard_map/ppermute | solution.py:161
  5.3 36.5 %collective-permute-start.1 = (bf16[8,2,192,192]{3,2,1,0:T(8,128)(2,1)}, bf16[8,2,192,192]{3,2,1,0:T(8,128)(2,1)}, u32[]{:S(2)}, u32[]{:S(2)}) collective-permute-start(bf16[8,2,192,192]{3,2,1,0:T(8,128)(2,1)} %get-tuple-element.79), channel_id=1, source_target_pairs={{1,0},{2,1},{3,2},{4,3},{5,4},{6,5},{7,6},{8,7},{9,8},{10,9},{11,1... | collective-permute-start | bytes 3538952 | tf_op jit(solution)/shard_map/ppermute | solution.py:161
  14.8 24.8 %collective-permute-start.2 = (bf16[4,288,192]{2,1,0:T(8,128)(2,1)S(1)}, bf16[4,288,192]{2,1,0:T(8,128)(2,1)S(1)}, u32[]{:S(2)}, u32[]{:S(2)}) collective-permute-start(bf16[4,288,192]{2,1,0:T(8,128)(2,1)S(1)} %get-tuple-element.60), channel_id=1, source_target_pairs={{0,64},{1,65},{2,66},{3,67},{4,68},{5,69},{6,70},{7,71},{8,72},{9,... | collective-permute-start | bytes 1327112 | tf_op jit(solution)/shard_map/ppermute | solution.py:210
  15.6 26.2 %collective-permute-start.3 = (bf16[4,288,192]{2,1,0:T(8,128)(2,1)S(1)}, bf16[4,288,192]{2,1,0:T(8,128)(2,1)S(1)}, u32[]{:S(2)}, u32[]{:S(2)}) collective-permute-start(bf16[4,288,192]{2,1,0:T(8,128)(2,1)S(1)} %get-tuple-element.59), channel_id=1, source_target_pairs={{0,192},{1,193},{2,194},{3,195},{4,196},{5,197},{6,198},{7,199},{8... | collective-permute-start | bytes 1327112 | tf_op jit(solution)/shard_map/ppermute | solution.py:211
  42.6 51.7 %collective-permute-start.17 = (bf16[8,2,192,192]{3,2,1,0:T(8,128)(2,1)}, bf16[8,2,192,192]{3,2,1,0:T(8,128)(2,1)S(1)}, u32[]{:S(2)}, u32[]{:S(2)}) collective-permute-start(bf16[8,2,192,192]{3,2,1,0:T(8,128)(2,1)} %get-tuple-element.33), channel_id=1, source_target_pairs={{0,1},{1,2},{2,3},{3,4},{4,5},{5,6},{6,7},{7,8},{8,9},{9,10},{10,1... | collective-permute-start | bytes 3538952 | tf_op jit(solution)/shard_map/ppermute | solution.py:161
  42.6 51.7 %collective-permute-start.18 = (bf16[8,2,192,192]{3,2,1,0:T(8,128)(2,1)}, bf16[8,2,192,192]{3,2,1,0:T(8,128)(2,1)}, u32[]{:S(2)}, u32[]{:S(2)}) collective-permute-start(bf16[8,2,192,192]{3,2,1,0:T(8,128)(2,1)} %get-tuple-element.34), channel_id=1, source_target_pairs={{1,0},{2,1},{3,2},{4,3},{5,4},{6,5},{7,6},{8,7},{9,8},{10,9},{11,1... | collective-permute-start | bytes 3538952 | tf_op jit(solution)/shard_map/ppermute | solution.py:161
  48.6 41.8 %collective-permute-start.4 = (bf16[4,288,192]{2,1,0:T(8,128)(2,1)}, bf16[4,288,192]{2,1,0:T(8,128)(2,1)S(1)}, u32[]{:S(2)}, u32[]{:S(2)}) collective-permute-start(bf16[4,288,192]{2,1,0:T(8,128)(2,1)} %copy-done.15), channel_id=1, source_target_pairs={{0,64},{1,65},{2,66},{3,67},{4,68},{5,69},{6,70},{7,71},{8,72},{9,... | collective-permute-start | bytes 1327112 | tf_op jit(solution)/shard_map/ppermute | solution.py:213
  49.7 43.5 %collective-permute-start.5 = (bf16[4,288,192]{2,1,0:T(8,128)(2,1)}, bf16[4,288,192]{2,1,0:T(8,128)(2,1)}, u32[]{:S(2)}, u32[]{:S(2)}) collective-permute-start(bf16[4,288,192]{2,1,0:T(8,128)(2,1)} %copy-done.14), channel_id=1, source_target_pairs={{0,192},{1,193},{2,194},{3,195},{4,196},{5,197},{6,198},{7,199},{8... | collective-permute-start | bytes 1327112 | tf_op jit(solution)/shard_map/ppermute | solution.py:213
  64.3 55.1 %collective-permute-start.13 = (bf16[8,2,192,192]{3,2,1,0:T(8,128)(2,1)}, bf16[8,2,192,192]{3,2,1,0:T(8,128)(2,1)}, u32[]{:S(2)}, u32[]{:S(2)}) collective-permute-start(bf16[8,2,192,192]{3,2,1,0:T(8,128)(2,1)} %get-tuple-element.28), channel_id=1, source_target_pairs={{0,1},{1,2},{2,3},{3,4},{4,5},{5,6},{6,7},{7,8},{8,9},{9,10},{10,1... | collective-permute-start | bytes 3538952 | tf_op jit(solution)/shard_map/ppermute | solution.py:161
  90.4 29.0 %collective-permute-start.14 = (bf16[8,2,192,192]{3,2,1,0:T(8,128)(2,1)}, bf16[8,2,192,192]{3,2,1,0:T(8,128)(2,1)}, u32[]{:S(2)}, u32[]{:S(2)}) collective-permute-start(bf16[8,2,192,192]{3,2,1,0:T(8,128)(2,1)} %get-tuple-element.29), channel_id=1, source_target_pairs={{1,0},{2,1},{3,2},{4,3},{5,4},{6,5},{7,6},{8,7},{9,8},{10,9},{11,1... | collective-permute-start | bytes 3538952 | tf_op jit(solution)/shard_map/ppermute | solution.py:161
  107.6 29.5 %collective-permute-start.19 = (bf16[8,2,192,192]{3,2,1,0:T(8,128)(2,1)}, bf16[8,2,192,192]{3,2,1,0:T(8,128)(2,1)S(1)}, u32[]{:S(2)}, u32[]{:S(2)}) collective-permute-start(bf16[8,2,192,192]{3,2,1,0:T(8,128)(2,1)} %get-tuple-element.36), channel_id=1, source_target_pairs={{0,1},{1,2},{2,3},{3,4},{4,5},{5,6},{6,7},{7,8},{8,9},{9,10},{10,1... | collective-permute-start | bytes 3538952 | tf_op jit(solution)/shard_map/ppermute | solution.py:161
  107.6 29.4 %collective-permute-start.20 = (bf16[8,2,192,192]{3,2,1,0:T(8,128)(2,1)}, bf16[8,2,192,192]{3,2,1,0:T(8,128)(2,1)}, u32[]{:S(2)}, u32[]{:S(2)}) collective-permute-start(bf16[8,2,192,192]{3,2,1,0:T(8,128)(2,1)} %get-tuple-element.37), channel_id=1, source_target_pairs={{1,0},{2,1},{3,2},{4,3},{5,4},{6,5},{7,6},{8,7},{9,8},{10,9},{11,1... | collective-permute-start | bytes 3538952 | tf_op jit(solution)/shard_map/ppermute | solution.py:161
  118.2 1.2 collective-permute-start.6
  119.4 36.6 %collective-permute-start.7 = (f32[2,8,2]{1,2,0:T(2,128)S(1)}, f32[2,8,2]{1,2,0:T(2,128)}, u32[]{:S(2)}, u32[]{:S(2)}) collective-permute-start(f32[2,8,2]{1,2,0:T(2,128)S(1)} %fusion.7), channel_id=1, source_target_pairs={{0,2},{1,3},{2,0},{3,1},{4,6},{5,7},{6,4},{7,5},{8,10},{9,11},{10,... | collective-permute-start | bytes 392 | tf_op jit(solution)/shard_map/ppermute | solution.py:190
  131.1 59.5 %collective-permute-start.15 = (bf16[8,2,192,192]{3,2,1,0:T(8,128)(2,1)}, bf16[8,2,192,192]{3,2,1,0:T(8,128)(2,1)}, u32[]{:S(2)}, u32[]{:S(2)}) collective-permute-start(bf16[8,2,192,192]{3,2,1,0:T(8,128)(2,1)} %get-tuple-element.31), channel_id=1, source_target_pairs={{0,1},{1,2},{2,3},{3,4},{4,5},{5,6},{6,7},{7,8},{8,9},{9,10},{10,1... | collective-permute-start | bytes 3538952 | tf_op jit(solution)/shard_map/ppermute | solution.py:161
  131.2 59.3 %collective-permute-start.16 = (bf16[8,2,192,192]{3,2,1,0:T(8,128)(2,1)}, bf16[8,2,192,192]{3,2,1,0:T(8,128)(2,1)}, u32[]{:S(2)}, u32[]{:S(2)}) collective-permute-start(bf16[8,2,192,192]{3,2,1,0:T(8,128)(2,1)} %get-tuple-element.32), channel_id=1, source_target_pairs={{1,0},{2,1},{3,2},{4,3},{5,4},{6,5},{7,6},{8,7},{9,8},{10,9},{11,1... | collective-permute-start | bytes 3538952 | tf_op jit(solution)/shard_map/ppermute | solution.py:161
  138.2 42.7 %copy-start.6 = (f32[8,288,192]{2,1,0:T(8,128)S(1)}, f32[8,288,192]{2,1,0:T(8,128)}, u32[]{:S(2)}) copy-start(f32[8,288,192]{2,1,0:T(8,128)} %copy-done.5) | copy-start | bytes 5308420
  150.0 52.0 %collective-permute-start.21 = (bf16[8,2,192,192]{3,2,1,0:T(8,128)(2,1)}, bf16[8,2,192,192]{3,2,1,0:T(8,128)(2,1)}, u32[]{:S(2)}, u32[]{:S(2)}) collective-permute-start(bf16[8,2,192,192]{3,2,1,0:T(8,128)(2,1)} %get-tuple-element.39), channel_id=1, source_target_pairs={{0,1},{1,2},{2,3},{3,4},{4,5},{5,6},{6,7},{7,8},{8,9},{9,10},{10,1... | collective-permute-start | bytes 3538952 | tf_op jit(solution)/shard_map/ppermute | solution.py:161
  150.0 52.0 %collective-permute-start.22 = (bf16[8,2,192,192]{3,2,1,0:T(8,128)(2,1)}, bf16[8,2,192,192]{3,2,1,0:T(8,128)(2,1)}, u32[]{:S(2)}, u32[]{:S(2)}) collective-permute-start(bf16[8,2,192,192]{3,2,1,0:T(8,128)(2,1)} %get-tuple-element.40), channel_id=1, source_target_pairs={{1,0},{2,1},{3,2},{4,3},{5,4},{6,5},{7,6},{8,7},{9,8},{10,9},{11,1... | collective-permute-start | bytes 3538952 | tf_op jit(solution)/shard_map/ppermute | solution.py:161
  156.6 13.2 %collective-permute-start.8 = (f32[2,8,2]{1,2,0:T(2,128)S(1)}, f32[2,8,2]{1,2,0:T(2,128)S(1)}, u32[]{:S(2)}, u32[]{:S(2)}) collective-permute-start(f32[2,8,2]{1,2,0:T(2,128)S(1)} %fusion.10), channel_id=1, source_target_pairs={{0,4},{1,5},{2,6},{3,7},{4,0},{5,1},{6,2},{7,3},{8,12},{9,13},{10,... | collective-permute-start | bytes 392 | tf_op jit(solution)/shard_map/ppermute | solution.py:190
  169.8 7.5 %collective-permute-start.9 = (f32[2,8,2]{1,2,0:T(2,128)S(1)}, f32[2,8,2]{1,2,0:T(2,128)S(1)}, u32[]{:S(2)}, u32[]{:S(2)}) collective-permute-start(f32[2,8,2]{1,2,0:T(2,128)S(1)} %add.142), channel_id=1, source_target_pairs={{0,8},{1,9},{2,10},{3,11},{4,12},{5,13},{6,14},{7,15},{8,0},{9,1},... | collective-permute-start | bytes 392 | tf_op jit(solution)/shard_map/ppermute | solution.py:190
  177.3 3.6 %collective-permute-start.10 = (f32[2,8,2]{1,2,0:T(2,128)S(1)}, f32[2,8,2]{1,2,0:T(2,128)S(1)}, u32[]{:S(2)}, u32[]{:S(2)}) collective-permute-start(f32[2,8,2]{1,2,0:T(2,128)S(1)} %add.143), channel_id=1, source_target_pairs={{0,16},{1,17},{2,18},{3,19},{4,20},{5,21},{6,22},{7,23},{8,24},{9,... | collective-permute-start | bytes 392 | tf_op jit(solution)/shard_map/ppermute | solution.py:190
  180.9 5.1 %collective-permute-start.11 = (f32[2,8,2]{1,2,0:T(2,128)S(1)}, f32[2,8,2]{1,2,0:T(2,128)S(1)}, u32[]{:S(2)}, u32[]{:S(2)}) collective-permute-start(f32[2,8,2]{1,2,0:T(2,128)S(1)} %add.144), channel_id=1, source_target_pairs={{0,32},{1,33},{2,34},{3,35},{4,36},{5,37},{6,38},{7,39},{8,40},{9,... | collective-permute-start | bytes 392 | tf_op jit(solution)/shard_map/ppermute | solution.py:190
  186.0 3.6 %collective-permute-start.12 = (f32[2,8,2]{1,2,0:T(2,128)S(1)}, f32[2,8,2]{1,2,0:T(2,128)S(1)}, u32[]{:S(2)}, u32[]{:S(2)}) collective-permute-start(f32[2,8,2]{1,2,0:T(2,128)S(1)} %add.145), channel_id=1, source_target_pairs={{0,64},{1,65},{2,66},{3,67},{4,68},{5,69},{6,70},{7,71},{8,72},{9,... | collective-permute-start | bytes 392 | tf_op jit(solution)/shard_map/ppermute | solution.py:190
  (15 other events, 82.3 us)

commit v7 on v4

--- a/solution.py
+++ b/solution.py
@@ -190,13 +190,16 @@
             for y in range(ring)
             for rest in range(lanes)
         ]
-    half = block.shape[0] // 2
     axes = ("band", "domain")
-    plus = lax.ppermute(block[:half], axes, shift(1))
-    minus = lax.ppermute(block[half:], axes, shift(-1))
-    return plus, minus, lambda plus, minus: jnp.concatenate(
-        [lax.ppermute(plus, axes, shift(1)), lax.ppermute(minus, axes, shift(-1))], axis=0
-    )
+    directions = [1, -1, 1, -1]
+
+    def hop(pieces, offset):
+        return [
+            lax.ppermute(piece, axes, shift(directions[offset + k]))
+            for k, piece in enumerate(pieces)
+        ]
+
+    return jnp.split(block, len(directions), axis=0), hop
 
 
 def pair_sums(block, targets):
@@ -227,17 +230,19 @@
     rem_scalars = jnp.stack([y0, s_rem, jnp.zeros((), jnp.int32)]).astype(jnp.int32)
 
     own_halos = exchange_halos(*warm_halos(warm_start, s_own, row_count))
-    plus, minus, finish_swap = swap_over_y(
-        own_block, (lax.axis_size("band"), lax.axis_size("domain"))
-    )
-    rem_sends, own_halos, plus, minus = lax.optimization_barrier(
-        (warm_halos(warm_start, s_rem, row_count), own_halos, plus, minus)
+    pieces, hop = swap_over_y(own_block, (lax.axis_size("band"), lax.axis_size("domain")))
+    early = hop(pieces[:2], 0)
+    rem_sends, own_halos, early, late = lax.optimization_barrier(
+        (warm_halos(warm_start, s_rem, row_count), own_halos, early, pieces[2:])
     )
     rem_halos = exchange_halos(*rem_sends)
-    rem_block = finish_swap(plus, minus)
+    early = hop(early, 0)
+    late = hop(late, 2)
     potential, fwd, bwd = sweep_call(
         False, warm_start, True, *own_halos, partner_pool, targets, tmat, own_scalars
     )
+    late, potential = lax.optimization_barrier((late, potential))
+    rem_block = jnp.concatenate(early + hop(late, 2), axis=0)
     rem_state = sweep_call(
         False, warm_start, True, *rem_halos, rem_block, targets, tmat, rem_scalars
     )

time: 217 us -> 228 us (1.051)
  starting transfers between devices: 35.8 us -> 48 us
    ppermute x6, starting transfers between devices: 31.2 us -> 38.9 us  [exchange_halos(): lax.ppermute(bwd, 'domain', backward)]
    ppermute x4 -> x8, starting transfers between devices: 4.13 us -> 8.75 us  [hop(): lax.ppermute(piece, axes, shift(directions[offset + k]))]
    ppermute x4 -> x8, waiting for transfers between devices: 51.9 us -> 50.5 us  [hop(): lax.ppermute(piece, axes, shift(directions[offset + k]))]
    unnamed x31 -> x37, local copies, waits for them, and re-layouts: 5.12 us -> 5.78 us
  transfers between devices with their start and end apart: 23 -> 27, of which waited for: 10 -> 11; matrix products, arithmetic and copies ran while one was open for 6% -> 5% of each run, Pallas kernels for 27% -> 26%
where the time goes in v7:
time: 228 us; the launch traced here: 226 us
  waiting for transfers between devices  81.7 us (36%)
  Pallas kernels  69.5 us (30%)
  starting transfers between devices  48 us (21%)
  local copies, waits for them, and re-layouts  17.4 us (8%)
  other arithmetic  8.62 us (4%)
    pallas_call x6, Pallas kernels, sweep_call(): pl.pallas_call(functools.partial(sweep_kernel, final), grid_spec=grid_spe...  69.5 us
    ppermute x8, waiting for transfers between devices, hop(): lax.ppermute(piece, axes, shift(directions[offset + k]))  50.5 us
    ppermute x6, starting transfers between devices, exchange_halos(): lax.ppermute(bwd, 'domain', backward)  38.9 us
    ppermute x7, waiting for transfers between devices, butterfly_sum(): total = total + lax.ppermute(x, axis, pairs)  31.2 us
    ppermute x8, starting transfers between devices, hop(): lax.ppermute(piece, axes, shift(directions[offset + k]))  8.75 us
    unnamed x37, local copies, waits for them, and re-layouts  5.78 us
  transfers between devices with their start and end apart: 27, of which 11 were waited for; matrix products, arithmetic and copies ran while one was open for 5% of the time, Pallas kernels for 26%

profile of v7, /device:TPU:16, one launch (start us, length us, event | category | flops | bytes accessed | tf_op | source)
XLA Modules:
  0.0 226.1 jit_solution(5492030152384226999)
XLA Ops:
  0.7 2.7 %dynamic-slice_bitcast_fusion = (bf16[8,2,288,192]{3,2,1,0:T(8,128)(2,1)S(1)}, bf16[8,2,288,192]{3,2,1,0:T(8,128)(2,1)S(1)}) fusion(bf16[2,8,2,288,192]{4,3,2,1,0:T(8,128)(2,1)} %v_ref.3, s32[]{:T(128)} %select_n.35, s32[]{:T(128)S(6)} %select_n.37), kind=kLoop, calls=%fused_computation.2 | loop fusion | bytes 7077896 | tf_op jit(solution)/shard_map/jit(dynamic_index_in_dim)/squeeze | solution.py:150
  5.3 8.2 %collective-permute-start.1 = (bf16[8,2,192,192]{3,2,1,0:T(8,128)(2,1)}, bf16[8,2,192,192]{3,2,1,0:T(8,128)(2,1)}, u32[]{:S(2)}, u32[]{:S(2)}) collective-permute-start(bf16[8,2,192,192]{3,2,1,0:T(8,128)(2,1)} %get-tuple-element.91), channel_id=1, source_target_pairs={{1,0},{2,1},{3,2},{4,3},{5,4},{6,5},{7,6},{8,7},{9,8},{10,9},{11,1... | collective-permute-start | bytes 3538952 | tf_op jit(solution)/shard_map/ppermute | solution.py:146
  18.9 14.4 %collective-permute-done.2 = bf16[2,288,192]{2,1,0:T(8,128)(2,1)S(1)} collective-permute-done((bf16[2,288,192]{2,1,0:T(8,128)(2,1)S(1)}, bf16[2,288,192]{2,1,0:T(8,128)(2,1)S(1)}, u32[]{:S(2)}, u32[]{:S(2)}) %collective-permute-start.2) | collective-permute-done | bytes 221216 | tf_op jit(solution)/shard_map/ppermute | solution.py:198
  33.3 2.2 collective-permute-done.3
  36.2 6.0 %collective-permute-start.22 = (bf16[8,2,192,192]{3,2,1,0:T(8,128)(2,1)}, bf16[8,2,192,192]{3,2,1,0:T(8,128)(2,1)}, u32[]{:S(2)}, u32[]{:S(2)}) collective-permute-start(bf16[8,2,192,192]{3,2,1,0:T(8,128)(2,1)} %get-tuple-element.44), channel_id=1, source_target_pairs={{1,0},{2,1},{3,2},{4,3},{5,4},{6,5},{7,6},{8,7},{9,8},{10,9},{11,1... | collective-permute-start | bytes 3538952 | tf_op jit(solution)/shard_map/ppermute | solution.py:146
  46.0 17.5 %collective-permute-done.6 = bf16[2,288,192]{2,1,0:T(8,128)(2,1)} collective-permute-done((bf16[2,288,192]{2,1,0:T(8,128)(2,1)S(1)}, bf16[2,288,192]{2,1,0:T(8,128)(2,1)}, u32[]{:S(2)}, u32[]{:S(2)}) %collective-permute-start.6) | collective-permute-done | bytes 221216 | tf_op jit(solution)/shard_map/ppermute | solution.py:198
  66.4 11.7 %shard_map.46 = (f32[8,2,288,192]{3,2,1,0:T(8,128)}, bf16[8,2,192,192]{3,2,1,0:T(8,128)(2,1)}, bf16[8,2,192,192]{3,2,1,0:T(8,128)(2,1)}) custom-call(s32[3]{0:T(128)} %pad_add_fusion.sc_ref, bf16[2,8,2,288,192]{4,3,2,1,0:T(8,128)(2,1)} %v_ref.3, bf16[8,2,192,192]{3,2,1,0:T(8,128)(2,1)} %collective-permute-done.lo_ref, ...), custom_call_target="tpu_custom_call" | custom-call | flops 700710912 | bytes 11354112 | tf_op jit(solution)/shard_map/pallas_call | solution.py:129
  80.9 4.8 %collective-permute-done.8 = bf16[2,288,192]{2,1,0:T(8,128)(2,1)S(1)} collective-permute-done((bf16[2,288,192]{2,1,0:T(8,128)(2,1)}, bf16[2,288,192]{2,1,0:T(8,128)(2,1)S(1)}, u32[]{:S(2)}, u32[]{:S(2)}) %collective-permute-start.8) | collective-permute-done | bytes 221216 | tf_op jit(solution)/shard_map/ppermute | solution.py:198
  85.7 7.1 %collective-permute-start.18 = (bf16[8,2,192,192]{3,2,1,0:T(8,128)(2,1)}, bf16[8,2,192,192]{3,2,1,0:T(8,128)(2,1)}, u32[]{:S(2)}, u32[]{:S(2)}) collective-permute-start(bf16[8,2,192,192]{3,2,1,0:T(8,128)(2,1)} %get-tuple-element.39), channel_id=1, source_target_pairs={{1,0},{2,1},{3,2},{4,3},{5,4},{6,5},{7,6},{8,7},{9,8},{10,9},{11,1... | collective-permute-start | bytes 3538952 | tf_op jit(solution)/shard_map/ppermute | solution.py:146
  92.8 11.5 %collective-permute-done.9 = bf16[2,288,192]{2,1,0:T(8,128)(2,1)S(1)} collective-permute-done((bf16[2,288,192]{2,1,0:T(8,128)(2,1)}, bf16[2,288,192]{2,1,0:T(8,128)(2,1)S(1)}, u32[]{:S(2)}, u32[]{:S(2)}) %collective-permute-start.9) | collective-permute-done | bytes 221216 | tf_op jit(solution)/shard_map/ppermute | solution.py:198
  105.9 11.6 %shard_map.49 = (f32[8,2,288,192]{3,2,1,0:T(8,128)}, bf16[8,2,192,192]{3,2,1,0:T(8,128)(2,1)}, bf16[8,2,192,192]{3,2,1,0:T(8,128)(2,1)}) custom-call(s32[3]{0:T(128)} %pad_add_fusion.1.sc_ref, bf16[2,8,2,288,192]{4,3,2,1,0:T(8,128)(2,1)} %v_ref.3, bf16[8,2,192,192]{3,2,1,0:T(8,128)(2,1)} %copy-done.8, ...), custom_call_target="tpu_custom_call" | custom-call | flops 700710912 | bytes 11354112 | tf_op jit(solution)/shard_map/pallas_call | solution.py:129
  117.5 6.0 %collective-permute-start.24 = (bf16[8,2,192,192]{3,2,1,0:T(8,128)(2,1)}, bf16[8,2,192,192]{3,2,1,0:T(8,128)(2,1)}, u32[]{:S(2)}, u32[]{:S(2)}) collective-permute-start(bf16[8,2,192,192]{3,2,1,0:T(8,128)(2,1)} %get-tuple-element.47), channel_id=1, source_target_pairs={{1,0},{2,1},{3,2},{4,3},{5,4},{6,5},{7,6},{8,7},{9,8},{10,9},{11,1... | collective-permute-start | bytes 3538952 | tf_op jit(solution)/shard_map/ppermute | solution.py:146
  129.2 12.0 %shard_map.47 = (f32[8,2,288,192]{3,2,1,0:T(8,128)}, bf16[8,2,192,192]{3,2,1,0:T(8,128)(2,1)}, bf16[8,2,192,192]{3,2,1,0:T(8,128)(2,1)}) custom-call(s32[3]{0:T(128)} %pad_add_fusion.sc_ref, f32[8,2,288,192]{3,2,1,0:T(8,128)} %get-tuple-element.37.v_ref, bf16[8,2,192,192]{3,2,1,0:T(8,128)(2,1)} %collective-permute-done.17.lo_ref, ...), custom_call_target="tpu_custom_call" | custom-call | flops 700710912 | bytes 13123584 | tf_op jit(solution)/shard_map/pallas_call | solution.py:129
  141.4 5.8 %collective-permute-start.20 = (bf16[8,2,192,192]{3,2,1,0:T(8,128)(2,1)}, bf16[8,2,192,192]{3,2,1,0:T(8,128)(2,1)}, u32[]{:S(2)}, u32[]{:S(2)}) collective-permute-start(bf16[8,2,192,192]{3,2,1,0:T(8,128)(2,1)} %get-tuple-element.42), channel_id=1, source_target_pairs={{1,0},{2,1},{3,2},{4,3},{5,4},{6,5},{7,6},{8,7},{9,8},{10,9},{11,1... | collective-permute-start | bytes 3538952 | tf_op jit(solution)/shard_map/ppermute | solution.py:146
  148.3 12.2 %shard_map.50 = (f32[8,2,288,192]{3,2,1,0:T(8,128)}, bf16[8,2,192,192]{3,2,1,0:T(8,128)(2,1)}, bf16[8,2,192,192]{3,2,1,0:T(8,128)(2,1)}) custom-call(s32[3]{0:T(128)} %pad_add_fusion.1.sc_ref, f32[8,2,288,192]{3,2,1,0:T(8,128)} %get-tuple-element.45.v_ref, bf16[8,2,192,192]{3,2,1,0:T(8,128)(2,1)} %copy-done.9, ...), custom_call_target="tpu_custom_call" | custom-call | flops 700710912 | bytes 13123584 | tf_op jit(solution)/shard_map/pallas_call | solution.py:129
  160.5 6.0 %collective-permute-start.26 = (bf16[8,2,192,192]{3,2,1,0:T(8,128)(2,1)}, bf16[8,2,192,192]{3,2,1,0:T(8,128)(2,1)}, u32[]{:S(2)}, u32[]{:S(2)}) collective-permute-start(bf16[8,2,192,192]{3,2,1,0:T(8,128)(2,1)} %get-tuple-element.50), channel_id=1, source_target_pairs={{1,0},{2,1},{3,2},{4,3},{5,4},{6,5},{7,6},{8,7},{9,8},{10,9},{11,1... | collective-permute-start | bytes 3538952 | tf_op jit(solution)/shard_map/ppermute | solution.py:146
  167.1 12.8 %collective-permute-done.12 = f32[2,8,2]{1,2,0:T(2,128)S(1)} collective-permute-done((f32[2,8,2]{1,2,0:T(2,128)S(1)}, f32[2,8,2]{1,2,0:T(2,128)S(1)}, u32[]{:S(2)}, u32[]{:S(2)}) %collective-permute-start.12) | collective-permute-done | bytes 160 | tf_op jit(solution)/shard_map/ppermute | solution.py:175
  179.9 7.5 %collective-permute-done.13 = f32[2,8,2]{1,2,0:T(2,128)S(1)} collective-permute-done((f32[2,8,2]{1,2,0:T(2,128)S(1)}, f32[2,8,2]{1,2,0:T(2,128)S(1)}, u32[]{:S(2)}, u32[]{:S(2)}) %collective-permute-start.13) | collective-permute-done | bytes 160 | tf_op jit(solution)/shard_map/ppermute | solution.py:175
  187.4 3.6 %collective-permute-done.14 = f32[2,8,2]{1,2,0:T(2,128)S(1)} collective-permute-done((f32[2,8,2]{1,2,0:T(2,128)S(1)}, f32[2,8,2]{1,2,0:T(2,128)S(1)}, u32[]{:S(2)}, u32[]{:S(2)}) %collective-permute-start.14) | collective-permute-done | bytes 160 | tf_op jit(solution)/shard_map/ppermute | solution.py:175
  192.2 4.0 %collective-permute-done.15 = f32[2,8,2]{1,2,0:T(2,128)S(1)} collective-permute-done((f32[2,8,2]{1,2,0:T(2,128)S(1)}, f32[2,8,2]{1,2,0:T(2,128)S(1)}, u32[]{:S(2)}, u32[]{:S(2)}) %collective-permute-start.15) | collective-permute-done | bytes 160 | tf_op jit(solution)/shard_map/ppermute | solution.py:175
  197.5 2.2 collective-permute-done.16
  200.7 10.9 %shard_map.48 = f32[2,288,192]{2,1,0:T(8,128)} custom-call(s32[3]{0:T(128)} %pad_add_fusion.sc_ref, f32[8,2,288,192]{3,2,1,0:T(8,128)} %get-tuple-element.40.v_ref, bf16[8,2,192,192]{3,2,1,0:T(8,128)(2,1)} %collective-permute-done.19.lo_ref, bf16[8,2,192,192]{3,2,1,0:T(8,128)(2,1)} %collective-permute-done.20.hi_ref, bf16[32,288,192]{2,1,0:T(8,128)(2,1)} %p_ref.5, ...), custom_call_target="tpu_custom_call" | custom-call | flops 700710912 | bytes 7667712 | tf_op jit(solution)/shard_map/pallas_call | solution.py:129
  211.8 11.1 %shard_map.51 = f32[2,288,192]{2,1,0:T(8,128)} custom-call(s32[3]{0:T(128)} %pad_add_fusion.1.sc_ref, f32[8,2,288,192]{3,2,1,0:T(8,128)} %get-tuple-element.48.v_ref, bf16[8,2,192,192]{3,2,1,0:T(8,128)(2,1)} %collective-permute-done.25.lo_ref, bf16[8,2,192,192]{3,2,1,0:T(8,128)(2,1)} %collective-permute-done.26.hi_ref, bf16[8,288,192]{2,1,0:T(8,128)(2,1)} %copy-done.1, ...), custom_call_target="tpu_custom_call" | custom-call | flops 700710912 | bytes 7667712 | tf_op jit(solution)/shard_map/pallas_call | solution.py:129
  222.9 3.2 %add_subtract_fusion = f32[2,288,192]{2,1,0:T(8,128)} fusion(f32[2,288,192]{2,1,0:T(8,128)S(1)} %copy-done.7, f32[2,288,192]{2,1,0:T(8,128)} %shard_map.51, f32[288,192]{1,0:T(8,128)S(1)} %get-tuple-element.84, f32[2]{0:T(128)S(1)} %get-tuple-element.54, f32[288,192]{1,0:T(8,128)} %get-tuple-element.85, f32[2]{0:T(128)S(1)} %get-tuple-element.55, ...), kind=kLoop, calls=%fused_computation.5 | loop fusion | flops 3760128 | bytes 4866176 | tf_op jit(solution)/shard_map/sub | solution.py:256
  (98 shorter events, 30.3 us)
Async XLA Ops:
  5.3 30.2 %collective-permute-start = (bf16[8,2,192,192]{3,2,1,0:T(8,128)(2,1)}, bf16[8,2,192,192]{3,2,1,0:T(8,128)(2,1)}, u32[]{:S(2)}, u32[]{:S(2)}) collective-permute-start(bf16[8,2,192,192]{3,2,1,0:T(8,128)(2,1)} %get-tuple-element.92), channel_id=1, source_target_pairs={{0,1},{1,2},{2,3},{3,4},{4,5},{5,6},{6,7},{7,8},{8,9},{9,10},{10,1... | collective-permute-start | bytes 3538952 | tf_op jit(solution)/shard_map/ppermute | solution.py:146
  5.3 30.2 %collective-permute-start.1 = (bf16[8,2,192,192]{3,2,1,0:T(8,128)(2,1)}, bf16[8,2,192,192]{3,2,1,0:T(8,128)(2,1)}, u32[]{:S(2)}, u32[]{:S(2)}) collective-permute-start(bf16[8,2,192,192]{3,2,1,0:T(8,128)(2,1)} %get-tuple-element.91), channel_id=1, source_target_pairs={{1,0},{2,1},{3,2},{4,3},{5,4},{6,5},{7,6},{8,7},{9,8},{10,9},{11,1... | collective-permute-start | bytes 3538952 | tf_op jit(solution)/shard_map/ppermute | solution.py:146
  14.8 18.5 %collective-permute-start.2 = (bf16[2,288,192]{2,1,0:T(8,128)(2,1)S(1)}, bf16[2,288,192]{2,1,0:T(8,128)(2,1)S(1)}, u32[]{:S(2)}, u32[]{:S(2)}) collective-permute-start(bf16[2,288,192]{2,1,0:T(8,128)(2,1)S(1)} %get-tuple-element.72), channel_id=1, source_target_pairs={{0,64},{1,65},{2,66},{3,67},{4,68},{5,69},{6,70},{7,71},{8,72},{9,... | collective-permute-start | bytes 663560 | tf_op jit(solution)/shard_map/ppermute | solution.py:198
  15.6 19.8 %collective-permute-start.3 = (bf16[2,288,192]{2,1,0:T(8,128)(2,1)S(1)}, bf16[2,288,192]{2,1,0:T(8,128)(2,1)S(1)}, u32[]{:S(2)}, u32[]{:S(2)}) collective-permute-start(bf16[2,288,192]{2,1,0:T(8,128)(2,1)S(1)} %get-tuple-element.71), channel_id=1, source_target_pairs={{0,192},{1,193},{2,194},{3,195},{4,196},{5,197},{6,198},{7,199},{8... | collective-permute-start | bytes 663560 | tf_op jit(solution)/shard_map/ppermute | solution.py:198
  36.2 68.2 %collective-permute-start.21 = (bf16[8,2,192,192]{3,2,1,0:T(8,128)(2,1)}, bf16[8,2,192,192]{3,2,1,0:T(8,128)(2,1)S(1)}, u32[]{:S(2)}, u32[]{:S(2)}) collective-permute-start(bf16[8,2,192,192]{3,2,1,0:T(8,128)(2,1)} %get-tuple-element.43), channel_id=1, source_target_pairs={{0,1},{1,2},{2,3},{3,4},{4,5},{5,6},{6,7},{7,8},{8,9},{9,10},{10,1... | collective-permute-start | bytes 3538952 | tf_op jit(solution)/shard_map/ppermute | solution.py:146
  36.2 68.2 %collective-permute-start.22 = (bf16[8,2,192,192]{3,2,1,0:T(8,128)(2,1)}, bf16[8,2,192,192]{3,2,1,0:T(8,128)(2,1)}, u32[]{:S(2)}, u32[]{:S(2)}) collective-permute-start(bf16[8,2,192,192]{3,2,1,0:T(8,128)(2,1)} %get-tuple-element.44), channel_id=1, source_target_pairs={{1,0},{2,1},{3,2},{4,3},{5,4},{6,5},{7,6},{8,7},{9,8},{10,9},{11,1... | collective-permute-start | bytes 3538952 | tf_op jit(solution)/shard_map/ppermute | solution.py:146
  42.2 21.4 %collective-permute-start.6 = (bf16[2,288,192]{2,1,0:T(8,128)(2,1)S(1)}, bf16[2,288,192]{2,1,0:T(8,128)(2,1)}, u32[]{:S(2)}, u32[]{:S(2)}) collective-permute-start(bf16[2,288,192]{2,1,0:T(8,128)(2,1)S(1)} %get-tuple-element.30), channel_id=1, source_target_pairs={{0,64},{1,65},{2,66},{3,67},{4,68},{5,69},{6,70},{7,71},{8,72},{9,... | collective-permute-start | bytes 663560 | tf_op jit(solution)/shard_map/ppermute | solution.py:198
  43.3 34.8 %collective-permute-start.7 = (bf16[2,288,192]{2,1,0:T(8,128)(2,1)S(1)}, bf16[2,288,192]{2,1,0:T(8,128)(2,1)S(1)}, u32[]{:S(2)}, u32[]{:S(2)}) collective-permute-start(bf16[2,288,192]{2,1,0:T(8,128)(2,1)S(1)} %get-tuple-element.31), channel_id=1, source_target_pairs={{0,192},{1,193},{2,194},{3,195},{4,196},{5,197},{6,198},{7,199},{8... | collective-permute-start | bytes 663560 | tf_op jit(solution)/shard_map/ppermute | solution.py:198
  45.0 33.2 %collective-permute-start.4 = (bf16[2,288,192]{2,1,0:T(8,128)(2,1)}, bf16[2,288,192]{2,1,0:T(8,128)(2,1)S(1)}, u32[]{:S(2)}, u32[]{:S(2)}) collective-permute-start(bf16[2,288,192]{2,1,0:T(8,128)(2,1)} %copy-done.15), channel_id=1, source_target_pairs={{0,64},{1,65},{2,66},{3,67},{4,68},{5,69},{6,70},{7,71},{8,72},{9,... | collective-permute-start | bytes 663560 | tf_op jit(solution)/shard_map/ppermute | solution.py:198
  63.5 15.7 %collective-permute-start.5 = (bf16[2,288,192]{2,1,0:T(8,128)(2,1)}, bf16[2,288,192]{2,1,0:T(8,128)(2,1)S(1)}, u32[]{:S(2)}, u32[]{:S(2)}) collective-permute-start(bf16[2,288,192]{2,1,0:T(8,128)(2,1)} %copy-done.14), channel_id=1, source_target_pairs={{0,192},{1,193},{2,194},{3,195},{4,196},{5,197},{6,198},{7,199},{8... | collective-permute-start | bytes 663560 | tf_op jit(solution)/shard_map/ppermute | solution.py:198
  78.1 51.1 %collective-permute-start.17 = (bf16[8,2,192,192]{3,2,1,0:T(8,128)(2,1)}, bf16[8,2,192,192]{3,2,1,0:T(8,128)(2,1)}, u32[]{:S(2)}, u32[]{:S(2)}) collective-permute-start(bf16[8,2,192,192]{3,2,1,0:T(8,128)(2,1)} %get-tuple-element.38), channel_id=1, source_target_pairs={{0,1},{1,2},{2,3},{3,4},{4,5},{5,6},{6,7},{7,8},{8,9},{9,10},{10,1... | collective-permute-start | bytes 3538952 | tf_op jit(solution)/shard_map/ppermute | solution.py:146
  78.8 6.9 %collective-permute-start.8 = (bf16[2,288,192]{2,1,0:T(8,128)(2,1)}, bf16[2,288,192]{2,1,0:T(8,128)(2,1)S(1)}, u32[]{:S(2)}, u32[]{:S(2)}) collective-permute-start(bf16[2,288,192]{2,1,0:T(8,128)(2,1)} %collective-permute-done.6), channel_id=1, source_target_pairs={{0,64},{1,65},{2,66},{3,67},{4,68},{5,69},{6,70},{7,71},{8,72},{9,... | collective-permute-start | bytes 663560 | tf_op jit(solution)/shard_map/ppermute | solution.py:198
  79.2 25.1 %collective-permute-start.9 = (bf16[2,288,192]{2,1,0:T(8,128)(2,1)}, bf16[2,288,192]{2,1,0:T(8,128)(2,1)S(1)}, u32[]{:S(2)}, u32[]{:S(2)}) collective-permute-start(bf16[2,288,192]{2,1,0:T(8,128)(2,1)} %copy-done.16), channel_id=1, source_target_pairs={{0,192},{1,193},{2,194},{3,195},{4,196},{5,197},{6,198},{7,199},{8... | collective-permute-start | bytes 663560 | tf_op jit(solution)/shard_map/ppermute | solution.py:198
  85.7 43.5 %collective-permute-start.18 = (bf16[8,2,192,192]{3,2,1,0:T(8,128)(2,1)}, bf16[8,2,192,192]{3,2,1,0:T(8,128)(2,1)}, u32[]{:S(2)}, u32[]{:S(2)}) collective-permute-start(bf16[8,2,192,192]{3,2,1,0:T(8,128)(2,1)} %get-tuple-element.39), channel_id=1, source_target_pairs={{1,0},{2,1},{3,2},{4,3},{5,4},{6,5},{7,6},{8,7},{9,8},{10,9},{11,1... | collective-permute-start | bytes 3538952 | tf_op jit(solution)/shard_map/ppermute | solution.py:146
  117.5 29.7 %collective-permute-start.23 = (bf16[8,2,192,192]{3,2,1,0:T(8,128)(2,1)}, bf16[8,2,192,192]{3,2,1,0:T(8,128)(2,1)S(1)}, u32[]{:S(2)}, u32[]{:S(2)}) collective-permute-start(bf16[8,2,192,192]{3,2,1,0:T(8,128)(2,1)} %get-tuple-element.46), channel_id=1, source_target_pairs={{0,1},{1,2},{2,3},{3,4},{4,5},{5,6},{6,7},{7,8},{8,9},{9,10},{10,1... | collective-permute-start | bytes 3538952 | tf_op jit(solution)/shard_map/ppermute | solution.py:146
  117.5 29.7 %collective-permute-start.24 = (bf16[8,2,192,192]{3,2,1,0:T(8,128)(2,1)}, bf16[8,2,192,192]{3,2,1,0:T(8,128)(2,1)}, u32[]{:S(2)}, u32[]{:S(2)}) collective-permute-start(bf16[8,2,192,192]{3,2,1,0:T(8,128)(2,1)} %get-tuple-element.47), channel_id=1, source_target_pairs={{1,0},{2,1},{3,2},{4,3},{5,4},{6,5},{7,6},{8,7},{9,8},{10,9},{11,1... | collective-permute-start | bytes 3538952 | tf_op jit(solution)/shard_map/ppermute | solution.py:146
  129.2 37.3 %collective-permute-start.11 = (f32[2,8,2]{1,2,0:T(2,128)S(1)}, f32[2,8,2]{1,2,0:T(2,128)}, u32[]{:S(2)}, u32[]{:S(2)}) collective-permute-start(f32[2,8,2]{1,2,0:T(2,128)S(1)} %fusion.7), channel_id=1, source_target_pairs={{0,2},{1,3},{2,0},{3,1},{4,6},{5,7},{6,4},{7,5},{8,10},{9,11},{10,... | collective-permute-start | bytes 392 | tf_op jit(solution)/shard_map/ppermute | solution.py:175
  141.2 59.5 %collective-permute-start.19 = (bf16[8,2,192,192]{3,2,1,0:T(8,128)(2,1)}, bf16[8,2,192,192]{3,2,1,0:T(8,128)(2,1)}, u32[]{:S(2)}, u32[]{:S(2)}) collective-permute-start(bf16[8,2,192,192]{3,2,1,0:T(8,128)(2,1)} %get-tuple-element.41), channel_id=1, source_target_pairs={{0,1},{1,2},{2,3},{3,4},{4,5},{5,6},{6,7},{7,8},{8,9},{9,10},{10,1... | collective-permute-start | bytes 3538952 | tf_op jit(solution)/shard_map/ppermute | solution.py:146
  141.4 59.4 %collective-permute-start.20 = (bf16[8,2,192,192]{3,2,1,0:T(8,128)(2,1)}, bf16[8,2,192,192]{3,2,1,0:T(8,128)(2,1)}, u32[]{:S(2)}, u32[]{:S(2)}) collective-permute-start(bf16[8,2,192,192]{3,2,1,0:T(8,128)(2,1)} %get-tuple-element.42), channel_id=1, source_target_pairs={{1,0},{2,1},{3,2},{4,3},{5,4},{6,5},{7,6},{8,7},{9,8},{10,9},{11,1... | collective-permute-start | bytes 3538952 | tf_op jit(solution)/shard_map/ppermute | solution.py:146
  160.5 51.2 %collective-permute-start.25 = (bf16[8,2,192,192]{3,2,1,0:T(8,128)(2,1)}, bf16[8,2,192,192]{3,2,1,0:T(8,128)(2,1)}, u32[]{:S(2)}, u32[]{:S(2)}) collective-permute-start(bf16[8,2,192,192]{3,2,1,0:T(8,128)(2,1)} %get-tuple-element.49), channel_id=1, source_target_pairs={{0,1},{1,2},{2,3},{3,4},{4,5},{5,6},{6,7},{7,8},{8,9},{9,10},{10,1... | collective-permute-start | bytes 3538952 | tf_op jit(solution)/shard_map/ppermute | solution.py:146
  160.5 51.2 %collective-permute-start.26 = (bf16[8,2,192,192]{3,2,1,0:T(8,128)(2,1)}, bf16[8,2,192,192]{3,2,1,0:T(8,128)(2,1)}, u32[]{:S(2)}, u32[]{:S(2)}) collective-permute-start(bf16[8,2,192,192]{3,2,1,0:T(8,128)(2,1)} %get-tuple-element.50), channel_id=1, source_target_pairs={{1,0},{2,1},{3,2},{4,3},{5,4},{6,5},{7,6},{8,7},{9,8},{10,9},{11,1... | collective-permute-start | bytes 3538952 | tf_op jit(solution)/shard_map/ppermute | solution.py:146
  167.1 12.8 %collective-permute-start.12 = (f32[2,8,2]{1,2,0:T(2,128)S(1)}, f32[2,8,2]{1,2,0:T(2,128)S(1)}, u32[]{:S(2)}, u32[]{:S(2)}) collective-permute-start(f32[2,8,2]{1,2,0:T(2,128)S(1)} %fusion.10), channel_id=1, source_target_pairs={{0,4},{1,5},{2,6},{3,7},{4,0},{5,1},{6,2},{7,3},{8,12},{9,13},{10,... | collective-permute-start | bytes 392 | tf_op jit(solution)/shard_map/ppermute | solution.py:175
  179.9 7.5 %collective-permute-start.13 = (f32[2,8,2]{1,2,0:T(2,128)S(1)}, f32[2,8,2]{1,2,0:T(2,128)S(1)}, u32[]{:S(2)}, u32[]{:S(2)}) collective-permute-start(f32[2,8,2]{1,2,0:T(2,128)S(1)} %add.122), channel_id=1, source_target_pairs={{0,8},{1,9},{2,10},{3,11},{4,12},{5,13},{6,14},{7,15},{8,0},{9,1},... | collective-permute-start | bytes 392 | tf_op jit(solution)/shard_map/ppermute | solution.py:175
  191.0 5.1 %collective-permute-start.15 = (f32[2,8,2]{1,2,0:T(2,128)S(1)}, f32[2,8,2]{1,2,0:T(2,128)S(1)}, u32[]{:S(2)}, u32[]{:S(2)}) collective-permute-start(f32[2,8,2]{1,2,0:T(2,128)S(1)} %add.124), channel_id=1, source_target_pairs={{0,32},{1,33},{2,34},{3,35},{4,36},{5,37},{6,38},{7,39},{8,40},{9,... | collective-permute-start | bytes 392 | tf_op jit(solution)/shard_map/ppermute | solution.py:175
  (20 other events, 131.6 us)

commit v8 on v4

--- a/solution.py
+++ b/solution.py
@@ -50,17 +50,23 @@
     return (beside + coupling * q) * (1.0 / 6.0)
 
 
-def sweep_kernel(final, sc_ref, v_ref, lo_ref, hi_ref, p_ref, t_ref, c_ref, *rest):
+def sweep_kernel(final, has_init, sc_ref, v_ref, lo_ref, hi_ref, p_ref, t_ref, c_ref, *rest):
     y0 = sc_ref[0]
     part = p_ref[...].astype(jnp.float32)
     row_count = part.shape[0]
     halo = lo_ref.shape[-2]
     if final:
-        acc_ref, wide = rest
+        if has_init:
+            m_ref, init_ref, acc_ref, wide = rest
+        else:
+            m_ref, acc_ref, wide = rest
 
         @pl.when(pl.program_id(0) == 0)
         def _():
-            acc_ref[...] = jnp.zeros_like(acc_ref)
+            if has_init:
+                acc_ref[...] = init_ref[...]
+            else:
+                acc_ref[...] = jnp.zeros_like(acc_ref)
 
     else:
         out_ref, fwd_ref, bwd_ref, wide = rest
@@ -76,14 +82,15 @@
             wide,
         )
         if final:
-            acc_ref[j] = acc_ref[j] + new * part
+            shift = (0.5 * coupling) * m_ref[pl.program_id(0), j]
+            acc_ref[j] = acc_ref[j] - (new - shift) * part
         else:
             out_ref[j] = new
             fwd_ref[j] = new[row_count - halo : row_count].astype(jnp.bfloat16)
             bwd_ref[j] = new[0:halo].astype(jnp.bfloat16)
 
 
-def sweep_call(final, v, from_warm, lo, hi, partner, targets, tmat, scalars):
+def sweep_call(final, v, from_warm, lo, hi, partner, targets, tmat, scalars, means=None, init=None):
     orb, tgt, halo, width = lo.shape
     row_count = targets.shape[1]
     if from_warm:
@@ -97,7 +104,14 @@
     t_spec = pl.BlockSpec((tgt, row_count, width), lambda i, sc: (0, 0, 0))
     c_spec = pl.BlockSpec((width, width), lambda i, sc: (0, 0))
     cells = orb * tgt * row_count * width
+    in_specs = [v_spec, h_spec, h_spec, p_spec, t_spec, c_spec]
+    extra = []
     if final:
+        in_specs.append(pl.BlockSpec(memory_space=pltpu.SMEM))
+        extra.append(means)
+        if init is not None:
+            in_specs.append(pl.BlockSpec((tgt, row_count, width), lambda i, sc: (0, 0, 0)))
+            extra.append(init)
         out_shape = jax.ShapeDtypeStruct((tgt, row_count, width), jnp.float32)
         out_specs = pl.BlockSpec((tgt, row_count, width), lambda i, sc: (0, 0, 0))
         out_bytes = tgt * row_count * width * 4
@@ -122,12 +136,12 @@
     grid_spec = pltpu.PrefetchScalarGridSpec(
         num_scalar_prefetch=1,
         grid=(orb,),
-        in_specs=[v_spec, h_spec, h_spec, p_spec, t_spec, c_spec],
+        in_specs=in_specs,
         out_specs=out_specs,
         scratch_shapes=[pltpu.VMEM((row_count + 2 * halo, width), jnp.float32)],
     )
     return pl.pallas_call(
-        functools.partial(sweep_kernel, final),
+        functools.partial(sweep_kernel, final, init is not None),
         grid_spec=grid_spec,
         out_shape=out_shape,
         compiler_params=pltpu.CompilerParams(dimension_semantics=("arbitrary",)),
@@ -136,7 +150,7 @@
             transcendentals=0,
             bytes_accessed=in_bytes + out_bytes,
         ),
-    )(scalars, v, lo, hi, partner, targets, tmat)
+    )(scalars, v, lo, hi, partner, targets, tmat, *extra)
 
 
 def exchange_halos(fwd, bwd):
@@ -151,14 +165,16 @@
     return warm_block[:, :, row_count - GY :], warm_block[:, :, :GY]
 
 
-def finish_stream(potential, fwd, bwd, partner, targets, tmat, scalars):
+def finish_stream(potential, fwd, bwd, partner, targets, tmat, scalars, means, init):
     for sweep_index in range(1, SWEEPS - 1):
         lo, hi = exchange_halos(fwd, bwd)
         potential, fwd, bwd = sweep_call(
             False, potential, False, lo, hi, partner, targets, tmat, scalars
         )
     lo, hi = exchange_halos(fwd, bwd)
-    return sweep_call(True, potential, False, lo, hi, partner, targets, tmat, scalars)
+    return sweep_call(
+        True, potential, False, lo, hi, partner, targets, tmat, scalars, means, init
+    )
 
 
 def butterfly_sum(x, axis):
@@ -204,15 +220,6 @@
     return jnp.sum(part[:, None] * targets[None], axis=(2, 3))
 
 
-def mean_term(block, means):
-    part = block.astype(jnp.float32)
-    total = None
-    for i in range(block.shape[0]):
-        term = means[i][:, None, None] * part[i][None]
-        total = term if total is None else total + term
-    return total
-
-
 def body(targets, partner_pool, owners, warm_start):
     row_count = targets.shape[1]
     cell_count = GX * GY * GZ
@@ -245,10 +252,12 @@
     sums = jnp.stack([pair_sums(own_block, targets), pair_sums(rem_block, targets)])
     means = butterfly_sum(sums, "domain") / cell_count
 
-    own_acc = finish_stream(potential, fwd, bwd, partner_pool, targets, tmat, own_scalars)
-    rem_acc = finish_stream(*rem_state, rem_block, targets, tmat, rem_scalars)
-    correction = mean_term(own_block, means[0]) + mean_term(rem_block, means[1])
-    return (0.5 * coupling) * correction - (own_acc + rem_acc)
+    own_acc = finish_stream(
+        potential, fwd, bwd, partner_pool, targets, tmat, own_scalars, means[0], None
+    )
+    return finish_stream(
+        *rem_state, rem_block, targets, tmat, rem_scalars, means[1], own_acc
+    )
 
 
 def solution(mesh):

time: 217 us -> 214 us (0.986)
  local copies, waits for them, and re-layouts: 17.7 us -> 14.5 us
    sub x1 -> x0, other arithmetic: 3.2 us -> none  [body(): return 0.5 * coupling * correction - (own_acc + rem_acc)]
    convert_element_type x2, other arithmetic: 1.69 us -> 4.51 us  [pair_sums(): part = block.astype(jnp.float32)]
    mul x2 -> x0, local copies, waits for them, and re-layouts: 2.42 us -> none  [mean_term(): term = means[i][:, None, None] * part[i][None]]
    unnamed x31 -> x15, local copies, waits for them, and re-layouts: 5.12 us -> 3.98 us
  transfers between devices with their start and end apart: 23 -> 23, of which waited for: 10 -> 11; matrix products, arithmetic and copies ran while one was open for 6% -> 7% of each run, Pallas kernels for 27% -> 28%
where the time goes in v8:
time: 214 us; the launch traced here: 212 us
  waiting for transfers between devices  81.7 us (38%)
  Pallas kernels  69.8 us (33%)
  starting transfers between devices  36.2 us (17%)
  local copies, waits for them, and re-layouts  14.5 us (7%)
  other arithmetic  9.09 us (4%)
    pallas_call x6, Pallas kernels, sweep_call(): pl.pallas_call(functools.partial(sweep_kernel, final, init is not None),...  69.8 us
    ppermute x6, starting transfers between devices, exchange_halos(): lax.ppermute(bwd, 'domain', backward)  32 us
    ppermute x7, waiting for transfers between devices, butterfly_sum(): total = total + lax.ppermute(x, axis, pairs)  30.4 us
    ppermute x1, waiting for transfers between devices, swap_over_y(): lax.ppermute(plus, axes, shift(1))  25.8 us
    ppermute x1, waiting for transfers between devices, swap_over_y(): plus = lax.ppermute(block[:half], axes, shift(1))  20.7 us
    convert_element_type x2, other arithmetic, pair_sums(): part = block.astype(jnp.float32)  4.51 us
  transfers between devices with their start and end apart: 23, of which 11 were waited for; matrix products, arithmetic and copies ran while one was open for 7% of the time, Pallas kernels for 28%

profile of v8, /device:TPU:16, one launch (start us, length us, event | category | flops | bytes accessed | tf_op | source)
XLA Modules:
  0.0 212.1 jit_solution(11912042160526767212)
XLA Ops:
  0.7 2.7 %dynamic-slice_bitcast_fusion = (bf16[8,2,288,192]{3,2,1,0:T(8,128)(2,1)S(1)}, bf16[8,2,288,192]{3,2,1,0:T(8,128)(2,1)S(1)}) fusion(bf16[2,8,2,288,192]{4,3,2,1,0:T(8,128)(2,1)} %v_ref.3, s32[]{:T(128)} %select_n.36, s32[]{:T(128)S(6)} %select_n.37), kind=kLoop, calls=%fused_computation.2 | loop fusion | bytes 7077896 | tf_op jit(solution)/shard_map/jit(dynamic_index_in_dim)/squeeze | solution.py:164
  5.3 8.2 %collective-permute-start.1 = (bf16[8,2,192,192]{3,2,1,0:T(8,128)(2,1)}, bf16[8,2,192,192]{3,2,1,0:T(8,128)(2,1)}, u32[]{:S(2)}, u32[]{:S(2)}) collective-permute-start(bf16[8,2,192,192]{3,2,1,0:T(8,128)(2,1)} %get-tuple-element.47), channel_id=1, source_target_pairs={{1,0},{2,1},{3,2},{4,3},{5,4},{6,5},{7,6},{8,7},{9,8},{10,9},{11,1... | collective-permute-start | bytes 3538952 | tf_op jit(solution)/shard_map/ppermute | solution.py:160
  18.9 20.7 %collective-permute-done.2 = bf16[4,288,192]{2,1,0:T(8,128)(2,1)S(1)} collective-permute-done((bf16[4,288,192]{2,1,0:T(8,128)(2,1)S(1)}, bf16[4,288,192]{2,1,0:T(8,128)(2,1)S(1)}, u32[]{:S(2)}, u32[]{:S(2)}) %collective-permute-start.2) | collective-permute-done | bytes 442400 | tf_op jit(solution)/shard_map/ppermute | solution.py:211
  39.6 2.3 %collective-permute-done.3 = bf16[4,288,192]{2,1,0:T(8,128)(2,1)} collective-permute-done((bf16[4,288,192]{2,1,0:T(8,128)(2,1)S(1)}, bf16[4,288,192]{2,1,0:T(8,128)(2,1)}, u32[]{:S(2)}, u32[]{:S(2)}) %collective-permute-start.3) | collective-permute-done | bytes 442400 | tf_op jit(solution)/shard_map/ppermute | solution.py:212
  41.9 6.0 %collective-permute-start.5 = (bf16[8,2,192,192]{3,2,1,0:T(8,128)(2,1)}, bf16[8,2,192,192]{3,2,1,0:T(8,128)(2,1)}, u32[]{:S(2)}, u32[]{:S(2)}) collective-permute-start(bf16[8,2,192,192]{3,2,1,0:T(8,128)(2,1)} %get-tuple-element.24), channel_id=1, source_target_pairs={{1,0},{2,1},{3,2},{4,3},{5,4},{6,5},{7,6},{8,7},{9,8},{10,9},{11,1... | collective-permute-start | bytes 3538952 | tf_op jit(solution)/shard_map/ppermute | solution.py:160
  51.9 11.6 %shard_map.48 = (f32[8,2,288,192]{3,2,1,0:T(8,128)}, bf16[8,2,192,192]{3,2,1,0:T(8,128)(2,1)}, bf16[8,2,192,192]{3,2,1,0:T(8,128)(2,1)}) custom-call(s32[3]{0:T(128)} %pad_add_fusion.1.sc_ref, bf16[2,8,2,288,192]{4,3,2,1,0:T(8,128)(2,1)} %v_ref.3, bf16[8,2,192,192]{3,2,1,0:T(8,128)(2,1)} %collective-permute-done.lo_ref, ...), custom_call_target="tpu_custom_call" | custom-call | flops 700710912 | bytes 11354112 | tf_op jit(solution)/shard_map/pallas_call | solution.py:143
  63.5 25.8 %collective-permute-done.6 = bf16[4,288,192]{2,1,0:T(8,128)(2,1)S(1)} collective-permute-done((bf16[4,288,192]{2,1,0:T(8,128)(2,1)S(1)}, bf16[4,288,192]{2,1,0:T(8,128)(2,1)S(1)}, u32[]{:S(2)}, u32[]{:S(2)}) %collective-permute-start.6) | collective-permute-done | bytes 442400 | tf_op jit(solution)/shard_map/ppermute | solution.py:214
  89.3 2.5 %collective-permute-done.7 = bf16[4,288,192]{2,1,0:T(8,128)(2,1)} collective-permute-done((bf16[4,288,192]{2,1,0:T(8,128)(2,1)}, bf16[4,288,192]{2,1,0:T(8,128)(2,1)}, u32[]{:S(2)}, u32[]{:S(2)}) %collective-permute-start.7) | collective-permute-done | bytes 442400 | tf_op jit(solution)/shard_map/ppermute | solution.py:214
  94.5 11.6 %shard_map.46 = (f32[8,2,288,192]{3,2,1,0:T(8,128)}, bf16[8,2,192,192]{3,2,1,0:T(8,128)(2,1)}, bf16[8,2,192,192]{3,2,1,0:T(8,128)(2,1)}) custom-call(s32[3]{0:T(128)} %pad_add_fusion.sc_ref, bf16[2,8,2,288,192]{4,3,2,1,0:T(8,128)(2,1)} %v_ref.3, bf16[8,2,192,192]{3,2,1,0:T(8,128)(2,1)} %copy-done.4, bf16[8,2,192,192]{3,2,1,0:T(8,128)(2,1)} %collective-permute-done.5.hi_ref, ...), custom_call_target="tpu_custom_call" | custom-call | flops 700710912 | bytes 11354112 | tf_op jit(solution)/shard_map/pallas_call | solution.py:143
  106.1 6.0 %collective-permute-start.9 = (bf16[8,2,192,192]{3,2,1,0:T(8,128)(2,1)}, bf16[8,2,192,192]{3,2,1,0:T(8,128)(2,1)S(1)}, u32[]{:S(2)}, u32[]{:S(2)}) collective-permute-start(bf16[8,2,192,192]{3,2,1,0:T(8,128)(2,1)} %get-tuple-element.29), channel_id=1, source_target_pairs={{1,0},{2,1},{3,2},{4,3},{5,4},{6,5},{7,6},{8,7},{9,8},{10,9},{11,1... | collective-permute-start | bytes 3538952 | tf_op jit(solution)/shard_map/ppermute | solution.py:160
  112.0 2.9 %dynamic-slice_convert_fusion = f32[8,288,192]{2,1,0:T(8,128)} fusion(bf16[32,288,192]{2,1,0:T(8,128)(2,1)} %p_ref.5, s32[]{:T(128)S(6)} %select_n.38), kind=kLoop, calls=%fused_computation.4 | loop fusion | flops 442368 | bytes 2654212 | tf_op jit(solution)/shard_map/convert_element_type | solution.py:219
  116.5 12.0 %shard_map.49 = (f32[8,2,288,192]{3,2,1,0:T(8,128)}, bf16[8,2,192,192]{3,2,1,0:T(8,128)(2,1)}, bf16[8,2,192,192]{3,2,1,0:T(8,128)(2,1)}) custom-call(s32[3]{0:T(128)} %pad_add_fusion.1.sc_ref, f32[8,2,288,192]{3,2,1,0:T(8,128)} %get-tuple-element.35.v_ref, bf16[8,2,192,192]{3,2,1,0:T(8,128)(2,1)} %collective-permute-done.19.lo_ref, ...), custom_call_target="tpu_custom_call" | custom-call | flops 700710912 | bytes 13123584 | tf_op jit(solution)/shard_map/pallas_call | solution.py:143
  128.6 6.0 %collective-permute-start.22 = (bf16[8,2,192,192]{3,2,1,0:T(8,128)(2,1)}, bf16[8,2,192,192]{3,2,1,0:T(8,128)(2,1)}, u32[]{:S(2)}, u32[]{:S(2)}) collective-permute-start(bf16[8,2,192,192]{3,2,1,0:T(8,128)(2,1)} %get-tuple-element.40), channel_id=1, source_target_pairs={{1,0},{2,1},{3,2},{4,3},{5,4},{6,5},{7,6},{8,7},{9,8},{10,9},{11,1... | collective-permute-start | bytes 3538952 | tf_op jit(solution)/shard_map/ppermute | solution.py:160
  136.9 12.2 %shard_map.47 = (f32[8,2,288,192]{3,2,1,0:T(8,128)}, bf16[8,2,192,192]{3,2,1,0:T(8,128)(2,1)}, bf16[8,2,192,192]{3,2,1,0:T(8,128)(2,1)}) custom-call(s32[3]{0:T(128)} %pad_add_fusion.sc_ref, f32[8,2,288,192]{3,2,1,0:T(8,128)} %get-tuple-element.27.v_ref, bf16[8,2,192,192]{3,2,1,0:T(8,128)(2,1)} %copy-done.5, bf16[8,2,192,192]{3,2,1,0:T(8,128)(2,1)} %copy-done.6, ...), custom_call_target="tpu_custom_call" | custom-call | flops 700710912 | bytes 13123584 | tf_op jit(solution)/shard_map/pallas_call | solution.py:143
  149.1 6.0 %collective-permute-start.11 = (bf16[8,2,192,192]{3,2,1,0:T(8,128)(2,1)}, bf16[8,2,192,192]{3,2,1,0:T(8,128)(2,1)}, u32[]{:S(2)}, u32[]{:S(2)}) collective-permute-start(bf16[8,2,192,192]{3,2,1,0:T(8,128)(2,1)} %get-tuple-element.32), channel_id=1, source_target_pairs={{1,0},{2,1},{3,2},{4,3},{5,4},{6,5},{7,6},{8,7},{9,8},{10,9},{11,1... | collective-permute-start | bytes 3538952 | tf_op jit(solution)/shard_map/ppermute | solution.py:160
  155.1 2.6 %multiply_reduce_fusion.1 = (f32[8,2]{1,0:T(8,128)S(1)}, f32[8,2]{1,0:T(8,128)S(1)}) fusion(f32[2,288,192]{2,1,0:T(8,128)S(1)} %copy-done, f32[8,288,192]{2,1,0:T(8,128)S(1)} %copy-done.3, f32[8,288,192]{2,1,0:T(8,128)} %convert_element_type.25), kind=kLoop, calls=%fused_computation.1 | loop fusion | flops 3538912 | bytes 3981440 | tf_op jit(solution)/shard_map/reduce_sum | solution.py:220
  159.1 5.0 %collective-permute-done.13 = f32[2,8,2]{1,2,0:T(2,128)S(1)} collective-permute-done((f32[2,8,2]{1,2,0:T(2,128)S(1)}, f32[2,8,2]{1,2,0:T(2,128)S(1)}, u32[]{:S(2)}, u32[]{:S(2)}) %collective-permute-start.13) | collective-permute-done | bytes 160 | tf_op jit(solution)/shard_map/ppermute | solution.py:191
  164.1 4.5 %collective-permute-done.14 = f32[2,8,2]{1,2,0:T(2,128)S(1)} collective-permute-done((f32[2,8,2]{1,2,0:T(2,128)S(1)}, f32[2,8,2]{1,2,0:T(2,128)S(1)}, u32[]{:S(2)}, u32[]{:S(2)}) %collective-permute-start.14) | collective-permute-done | bytes 160 | tf_op jit(solution)/shard_map/ppermute | solution.py:191
  168.6 7.5 %collective-permute-done.15 = f32[2,8,2]{1,2,0:T(2,128)S(1)} collective-permute-done((f32[2,8,2]{1,2,0:T(2,128)S(1)}, f32[2,8,2]{1,2,0:T(2,128)S(1)}, u32[]{:S(2)}, u32[]{:S(2)}) %collective-permute-start.15) | collective-permute-done | bytes 160 | tf_op jit(solution)/shard_map/ppermute | solution.py:191
  176.1 3.6 %collective-permute-done.16 = f32[2,8,2]{1,2,0:T(2,128)S(1)} collective-permute-done((f32[2,8,2]{1,2,0:T(2,128)S(1)}, f32[2,8,2]{1,2,0:T(2,128)S(1)}, u32[]{:S(2)}, u32[]{:S(2)}) %collective-permute-start.16) | collective-permute-done | bytes 160 | tf_op jit(solution)/shard_map/ppermute | solution.py:191
  179.7 5.1 %collective-permute-done.17 = f32[2,8,2]{1,2,0:T(2,128)S(1)} collective-permute-done((f32[2,8,2]{1,2,0:T(2,128)S(1)}, f32[2,8,2]{1,2,0:T(2,128)S(1)}, u32[]{:S(2)}, u32[]{:S(2)}) %collective-permute-start.17) | collective-permute-done | bytes 160 | tf_op jit(solution)/shard_map/ppermute | solution.py:191
  184.8 3.6 %collective-permute-done.18 = f32[2,8,2]{1,2,0:T(2,128)S(1)} collective-permute-done((f32[2,8,2]{1,2,0:T(2,128)S(1)}, f32[2,8,2]{1,2,0:T(2,128)S(1)}, u32[]{:S(2)}, u32[]{:S(2)}) %collective-permute-start.18) | collective-permute-done | bytes 160 | tf_op jit(solution)/shard_map/ppermute | solution.py:191
  189.7 11.1 %shard_map.50.rest_1_ = f32[2,288,192]{2,1,0:T(8,128)} custom-call(s32[3]{0:T(128)} %pad_add_fusion.1.sc_ref, f32[8,2,288,192]{3,2,1,0:T(8,128)} %get-tuple-element.38.v_ref, bf16[8,2,192,192]{3,2,1,0:T(8,128)(2,1)} %collective-permute-done.21.lo_ref, bf16[8,2,192,192]{3,2,1,0:T(8,128)(2,1)} %collective-permute-done.22.hi_ref, bf16[32,288,192]{2,1,0:T(8,128)(2,1)} %p_ref.5, ...), custom_call_target="tpu_custom_call" | custom-call | flops 700710912 | bytes 7667712 | tf_op jit(solution)/shard_map/pallas_call | solution.py:143
  200.8 11.3 %shard_map.51 = f32[2,288,192]{2,1,0:T(8,128)} custom-call(s32[3]{0:T(128)} %pad_add_fusion.sc_ref, f32[8,2,288,192]{3,2,1,0:T(8,128)} %get-tuple-element.30.v_ref, bf16[8,2,192,192]{3,2,1,0:T(8,128)(2,1)} %collective-permute-done.10.lo_ref, bf16[8,2,192,192]{3,2,1,0:T(8,128)(2,1)} %collective-permute-done.11.hi_ref, bf16[8,288,192]{2,1,0:T(8,128)(2,1)} %copy-done.1, ...), custom_call_target="tpu_custom_call" | custom-call | flops 700710912 | bytes 7667712 | tf_op jit(solution)/shard_map/pallas_call | solution.py:143
  (67 shorter events, 20.8 us)
Async XLA Ops:
  5.3 36.6 %collective-permute-start = (bf16[8,2,192,192]{3,2,1,0:T(8,128)(2,1)}, bf16[8,2,192,192]{3,2,1,0:T(8,128)(2,1)}, u32[]{:S(2)}, u32[]{:S(2)}) collective-permute-start(bf16[8,2,192,192]{3,2,1,0:T(8,128)(2,1)} %get-tuple-element.48), channel_id=1, source_target_pairs={{0,1},{1,2},{2,3},{3,4},{4,5},{5,6},{6,7},{7,8},{8,9},{9,10},{10,1... | collective-permute-start | bytes 3538952 | tf_op jit(solution)/shard_map/ppermute | solution.py:160
  5.3 36.6 %collective-permute-start.1 = (bf16[8,2,192,192]{3,2,1,0:T(8,128)(2,1)}, bf16[8,2,192,192]{3,2,1,0:T(8,128)(2,1)}, u32[]{:S(2)}, u32[]{:S(2)}) collective-permute-start(bf16[8,2,192,192]{3,2,1,0:T(8,128)(2,1)} %get-tuple-element.47), channel_id=1, source_target_pairs={{1,0},{2,1},{3,2},{4,3},{5,4},{6,5},{7,6},{8,7},{9,8},{10,9},{11,1... | collective-permute-start | bytes 3538952 | tf_op jit(solution)/shard_map/ppermute | solution.py:160
  14.8 24.8 %collective-permute-start.2 = (bf16[4,288,192]{2,1,0:T(8,128)(2,1)S(1)}, bf16[4,288,192]{2,1,0:T(8,128)(2,1)S(1)}, u32[]{:S(2)}, u32[]{:S(2)}) collective-permute-start(bf16[4,288,192]{2,1,0:T(8,128)(2,1)S(1)} %get-tuple-element.44), channel_id=1, source_target_pairs={{0,64},{1,65},{2,66},{3,67},{4,68},{5,69},{6,70},{7,71},{8,72},{9,... | collective-permute-start | bytes 1327112 | tf_op jit(solution)/shard_map/ppermute | solution.py:211
  15.6 26.3 %collective-permute-start.3 = (bf16[4,288,192]{2,1,0:T(8,128)(2,1)S(1)}, bf16[4,288,192]{2,1,0:T(8,128)(2,1)}, u32[]{:S(2)}, u32[]{:S(2)}) collective-permute-start(bf16[4,288,192]{2,1,0:T(8,128)(2,1)S(1)} %get-tuple-element.43), channel_id=1, source_target_pairs={{0,192},{1,193},{2,194},{3,195},{4,196},{5,197},{6,198},{7,199},{8... | collective-permute-start | bytes 1327112 | tf_op jit(solution)/shard_map/ppermute | solution.py:212
  41.9 51.0 %collective-permute-start.4 = (bf16[8,2,192,192]{3,2,1,0:T(8,128)(2,1)}, bf16[8,2,192,192]{3,2,1,0:T(8,128)(2,1)S(1)}, u32[]{:S(2)}, u32[]{:S(2)}) collective-permute-start(bf16[8,2,192,192]{3,2,1,0:T(8,128)(2,1)} %get-tuple-element.23), channel_id=1, source_target_pairs={{0,1},{1,2},{2,3},{3,4},{4,5},{5,6},{6,7},{7,8},{8,9},{9,10},{10,1... | collective-permute-start | bytes 3538952 | tf_op jit(solution)/shard_map/ppermute | solution.py:160
  41.9 51.0 %collective-permute-start.5 = (bf16[8,2,192,192]{3,2,1,0:T(8,128)(2,1)}, bf16[8,2,192,192]{3,2,1,0:T(8,128)(2,1)}, u32[]{:S(2)}, u32[]{:S(2)}) collective-permute-start(bf16[8,2,192,192]{3,2,1,0:T(8,128)(2,1)} %get-tuple-element.24), channel_id=1, source_target_pairs={{1,0},{2,1},{3,2},{4,3},{5,4},{6,5},{7,6},{8,7},{9,8},{10,9},{11,1... | collective-permute-start | bytes 3538952 | tf_op jit(solution)/shard_map/ppermute | solution.py:160
  47.9 41.4 %collective-permute-start.6 = (bf16[4,288,192]{2,1,0:T(8,128)(2,1)S(1)}, bf16[4,288,192]{2,1,0:T(8,128)(2,1)S(1)}, u32[]{:S(2)}, u32[]{:S(2)}) collective-permute-start(bf16[4,288,192]{2,1,0:T(8,128)(2,1)S(1)} %collective-permute-done.2), channel_id=1, source_target_pairs={{0,64},{1,65},{2,66},{3,67},{4,68},{5,69},{6,70},{7,71},{8,72},{9,... | collective-permute-start | bytes 1327112 | tf_op jit(solution)/shard_map/ppermute | solution.py:214
  48.1 43.6 %collective-permute-start.7 = (bf16[4,288,192]{2,1,0:T(8,128)(2,1)}, bf16[4,288,192]{2,1,0:T(8,128)(2,1)}, u32[]{:S(2)}, u32[]{:S(2)}) collective-permute-start(bf16[4,288,192]{2,1,0:T(8,128)(2,1)} %collective-permute-done.3), channel_id=1, source_target_pairs={{0,192},{1,193},{2,194},{3,195},{4,196},{5,197},{6,198},{7,199},{8... | collective-permute-start | bytes 1327112 | tf_op jit(solution)/shard_map/ppermute | solution.py:214
  63.5 53.1 %collective-permute-start.19 = (bf16[8,2,192,192]{3,2,1,0:T(8,128)(2,1)}, bf16[8,2,192,192]{3,2,1,0:T(8,128)(2,1)}, u32[]{:S(2)}, u32[]{:S(2)}) collective-permute-start(bf16[8,2,192,192]{3,2,1,0:T(8,128)(2,1)} %get-tuple-element.36), channel_id=1, source_target_pairs={{0,1},{1,2},{2,3},{3,4},{4,5},{5,6},{6,7},{7,8},{8,9},{9,10},{10,1... | collective-permute-start | bytes 3538952 | tf_op jit(solution)/shard_map/ppermute | solution.py:160
  89.3 27.3 %collective-permute-start.20 = (bf16[8,2,192,192]{3,2,1,0:T(8,128)(2,1)}, bf16[8,2,192,192]{3,2,1,0:T(8,128)(2,1)}, u32[]{:S(2)}, u32[]{:S(2)}) collective-permute-start(bf16[8,2,192,192]{3,2,1,0:T(8,128)(2,1)} %get-tuple-element.37), channel_id=1, source_target_pairs={{1,0},{2,1},{3,2},{4,3},{5,4},{6,5},{7,6},{8,7},{9,8},{10,9},{11,1... | collective-permute-start | bytes 3538952 | tf_op jit(solution)/shard_map/ppermute | solution.py:160
  106.0 28.5 %collective-permute-start.8 = (bf16[8,2,192,192]{3,2,1,0:T(8,128)(2,1)}, bf16[8,2,192,192]{3,2,1,0:T(8,128)(2,1)S(1)}, u32[]{:S(2)}, u32[]{:S(2)}) collective-permute-start(bf16[8,2,192,192]{3,2,1,0:T(8,128)(2,1)} %get-tuple-element.28), channel_id=1, source_target_pairs={{0,1},{1,2},{2,3},{3,4},{4,5},{5,6},{6,7},{7,8},{8,9},{9,10},{10,1... | collective-permute-start | bytes 3538952 | tf_op jit(solution)/shard_map/ppermute | solution.py:160
  106.1 28.5 %collective-permute-start.9 = (bf16[8,2,192,192]{3,2,1,0:T(8,128)(2,1)}, bf16[8,2,192,192]{3,2,1,0:T(8,128)(2,1)S(1)}, u32[]{:S(2)}, u32[]{:S(2)}) collective-permute-start(bf16[8,2,192,192]{3,2,1,0:T(8,128)(2,1)} %get-tuple-element.29), channel_id=1, source_target_pairs={{1,0},{2,1},{3,2},{4,3},{5,4},{6,5},{7,6},{8,7},{9,8},{10,9},{11,1... | collective-permute-start | bytes 3538952 | tf_op jit(solution)/shard_map/ppermute | solution.py:160
  128.6 61.2 %collective-permute-start.21 = (bf16[8,2,192,192]{3,2,1,0:T(8,128)(2,1)}, bf16[8,2,192,192]{3,2,1,0:T(8,128)(2,1)}, u32[]{:S(2)}, u32[]{:S(2)}) collective-permute-start(bf16[8,2,192,192]{3,2,1,0:T(8,128)(2,1)} %get-tuple-element.39), channel_id=1, source_target_pairs={{0,1},{1,2},{2,3},{3,4},{4,5},{5,6},{6,7},{7,8},{8,9},{9,10},{10,1... | collective-permute-start | bytes 3538952 | tf_op jit(solution)/shard_map/ppermute | solution.py:160
  128.6 61.2 %collective-permute-start.22 = (bf16[8,2,192,192]{3,2,1,0:T(8,128)(2,1)}, bf16[8,2,192,192]{3,2,1,0:T(8,128)(2,1)}, u32[]{:S(2)}, u32[]{:S(2)}) collective-permute-start(bf16[8,2,192,192]{3,2,1,0:T(8,128)(2,1)} %get-tuple-element.40), channel_id=1, source_target_pairs={{1,0},{2,1},{3,2},{4,3},{5,4},{6,5},{7,6},{8,7},{9,8},{10,9},{11,1... | collective-permute-start | bytes 3538952 | tf_op jit(solution)/shard_map/ppermute | solution.py:160
  136.9 18.2 %copy-start.3 = (f32[8,288,192]{2,1,0:T(8,128)S(1)}, f32[8,288,192]{2,1,0:T(8,128)}, u32[]{:S(2)}) copy-start(f32[8,288,192]{2,1,0:T(8,128)} %dynamic-slice_convert_fusion) | copy-start | bytes 5308420
  149.1 51.7 %collective-permute-start.10 = (bf16[8,2,192,192]{3,2,1,0:T(8,128)(2,1)}, bf16[8,2,192,192]{3,2,1,0:T(8,128)(2,1)}, u32[]{:S(2)}, u32[]{:S(2)}) collective-permute-start(bf16[8,2,192,192]{3,2,1,0:T(8,128)(2,1)} %get-tuple-element.31), channel_id=1, source_target_pairs={{0,1},{1,2},{2,3},{3,4},{4,5},{5,6},{6,7},{7,8},{8,9},{9,10},{10,1... | collective-permute-start | bytes 3538952 | tf_op jit(solution)/shard_map/ppermute | solution.py:160
  149.1 51.7 %collective-permute-start.11 = (bf16[8,2,192,192]{3,2,1,0:T(8,128)(2,1)}, bf16[8,2,192,192]{3,2,1,0:T(8,128)(2,1)}, u32[]{:S(2)}, u32[]{:S(2)}) collective-permute-start(bf16[8,2,192,192]{3,2,1,0:T(8,128)(2,1)} %get-tuple-element.32), channel_id=1, source_target_pairs={{1,0},{2,1},{3,2},{4,3},{5,4},{6,5},{7,6},{8,7},{9,8},{10,9},{11,1... | collective-permute-start | bytes 3538952 | tf_op jit(solution)/shard_map/ppermute | solution.py:160
  157.9 1.2 collective-permute-start.12
  159.1 5.1 %collective-permute-start.13 = (f32[2,8,2]{1,2,0:T(2,128)S(1)}, f32[2,8,2]{1,2,0:T(2,128)S(1)}, u32[]{:S(2)}, u32[]{:S(2)}) collective-permute-start(f32[2,8,2]{1,2,0:T(2,128)S(1)} %fusion.7), channel_id=1, source_target_pairs={{0,2},{1,3},{2,0},{3,1},{4,6},{5,7},{6,4},{7,5},{8,10},{9,11},{10,... | collective-permute-start | bytes 392 | tf_op jit(solution)/shard_map/ppermute | solution.py:191
  164.1 4.5 %collective-permute-start.14 = (f32[2,8,2]{1,2,0:T(2,128)S(1)}, f32[2,8,2]{1,2,0:T(2,128)S(1)}, u32[]{:S(2)}, u32[]{:S(2)}) collective-permute-start(f32[2,8,2]{1,2,0:T(2,128)S(1)} %fusion.10), channel_id=1, source_target_pairs={{0,4},{1,5},{2,6},{3,7},{4,0},{5,1},{6,2},{7,3},{8,12},{9,13},{10,... | collective-permute-start | bytes 392 | tf_op jit(solution)/shard_map/ppermute | solution.py:191
  168.6 7.5 %collective-permute-start.15 = (f32[2,8,2]{1,2,0:T(2,128)S(1)}, f32[2,8,2]{1,2,0:T(2,128)S(1)}, u32[]{:S(2)}, u32[]{:S(2)}) collective-permute-start(f32[2,8,2]{1,2,0:T(2,128)S(1)} %add.74), channel_id=1, source_target_pairs={{0,8},{1,9},{2,10},{3,11},{4,12},{5,13},{6,14},{7,15},{8,0},{9,1},... | collective-permute-start | bytes 392 | tf_op jit(solution)/shard_map/ppermute | solution.py:191
  176.1 3.6 %collective-permute-start.16 = (f32[2,8,2]{1,2,0:T(2,128)S(1)}, f32[2,8,2]{1,2,0:T(2,128)S(1)}, u32[]{:S(2)}, u32[]{:S(2)}) collective-permute-start(f32[2,8,2]{1,2,0:T(2,128)S(1)} %add.75), channel_id=1, source_target_pairs={{0,16},{1,17},{2,18},{3,19},{4,20},{5,21},{6,22},{7,23},{8,24},{9,... | collective-permute-start | bytes 392 | tf_op jit(solution)/shard_map/ppermute | solution.py:191
  179.7 5.1 %collective-permute-start.17 = (f32[2,8,2]{1,2,0:T(2,128)S(1)}, f32[2,8,2]{1,2,0:T(2,128)S(1)}, u32[]{:S(2)}, u32[]{:S(2)}) collective-permute-start(f32[2,8,2]{1,2,0:T(2,128)S(1)} %add.76), channel_id=1, source_target_pairs={{0,32},{1,33},{2,34},{3,35},{4,36},{5,37},{6,38},{7,39},{8,40},{9,... | collective-permute-start | bytes 392 | tf_op jit(solution)/shard_map/ppermute | solution.py:191
  184.8 3.6 %collective-permute-start.18 = (f32[2,8,2]{1,2,0:T(2,128)S(1)}, f32[2,8,2]{1,2,0:T(2,128)S(1)}, u32[]{:S(2)}, u32[]{:S(2)}) collective-permute-start(f32[2,8,2]{1,2,0:T(2,128)S(1)} %add.77), channel_id=1, source_target_pairs={{0,64},{1,65},{2,66},{3,67},{4,68},{5,69},{6,70},{7,71},{8,72},{9,... | collective-permute-start | bytes 392 | tf_op jit(solution)/shard_map/ppermute | solution.py:191
  (6 other events, 32.0 us)

commit v9 on v8

--- a/solution.py
+++ b/solution.py
@@ -17,6 +17,7 @@
 
 
 coupling = 4.0 * math.pi
+PER_STEP = 2
 
 
 def circulant(width):
@@ -52,8 +53,8 @@
 
 def sweep_kernel(final, has_init, sc_ref, v_ref, lo_ref, hi_ref, p_ref, t_ref, c_ref, *rest):
     y0 = sc_ref[0]
-    part = p_ref[...].astype(jnp.float32)
-    row_count = part.shape[0]
+    pb = p_ref.shape[0]
+    row_count = p_ref.shape[1]
     halo = lo_ref.shape[-2]
     if final:
         if has_init:
@@ -70,37 +71,40 @@
 
     else:
         out_ref, fwd_ref, bwd_ref, wide = rest
-    for j in range(v_ref.shape[0]):
-        q = part * t_ref[j]
-        new = stencil(
-            y0,
-            v_ref[j].astype(jnp.float32),
-            lo_ref[j].astype(jnp.float32),
-            hi_ref[j].astype(jnp.float32),
-            q,
-            c_ref,
-            wide,
-        )
-        if final:
-            shift = (0.5 * coupling) * m_ref[pl.program_id(0), j]
-            acc_ref[j] = acc_ref[j] - (new - shift) * part
-        else:
-            out_ref[j] = new
-            fwd_ref[j] = new[row_count - halo : row_count].astype(jnp.bfloat16)
-            bwd_ref[j] = new[0:halo].astype(jnp.bfloat16)
+    for k in range(pb):
+        part = p_ref[k].astype(jnp.float32)
+        for j in range(v_ref.shape[1]):
+            q = part * t_ref[j]
+            new = stencil(
+                y0,
+                v_ref[k, j].astype(jnp.float32),
+                lo_ref[k, j].astype(jnp.float32),
+                hi_ref[k, j].astype(jnp.float32),
+                q,
+                c_ref,
+                wide,
+            )
+            if final:
+                shift = (0.5 * coupling) * m_ref[pl.program_id(0) * pb + k, j]
+                acc_ref[j] = acc_ref[j] - (new - shift) * part
+            else:
+                out_ref[k, j] = new
+                fwd_ref[k, j] = new[row_count - halo : row_count].astype(jnp.bfloat16)
+                bwd_ref[k, j] = new[0:halo].astype(jnp.bfloat16)
 
 
 def sweep_call(final, v, from_warm, lo, hi, partner, targets, tmat, scalars, means=None, init=None):
     orb, tgt, halo, width = lo.shape
     row_count = targets.shape[1]
+    pb = PER_STEP
     if from_warm:
         v_spec = pl.BlockSpec(
-            (None, None, tgt, row_count, width), lambda i, sc: (sc[1], i, 0, 0, 0)
+            (None, pb, tgt, row_count, width), lambda i, sc: (sc[1], i, 0, 0, 0)
         )
     else:
-        v_spec = pl.BlockSpec((None, tgt, row_count, width), lambda i, sc: (i, 0, 0, 0))
-    h_spec = pl.BlockSpec((None, tgt, halo, width), lambda i, sc: (i, 0, 0, 0))
-    p_spec = pl.BlockSpec((None, row_count, width), lambda i, sc: (sc[2] + i, 0, 0))
+        v_spec = pl.BlockSpec((pb, tgt, row_count, width), lambda i, sc: (i, 0, 0, 0))
+    h_spec = pl.BlockSpec((pb, tgt, halo, width), lambda i, sc: (i, 0, 0, 0))
+    p_spec = pl.BlockSpec((pb, row_count, width), lambda i, sc: (sc[2] // pb + i, 0, 0))
     t_spec = pl.BlockSpec((tgt, row_count, width), lambda i, sc: (0, 0, 0))
     c_spec = pl.BlockSpec((width, width), lambda i, sc: (0, 0))
     cells = orb * tgt * row_count * width
@@ -122,7 +126,7 @@
             jax.ShapeDtypeStruct((orb, tgt, halo, width), jnp.bfloat16),
         )
         out_specs = (
-            pl.BlockSpec((None, tgt, row_count, width), lambda i, sc: (i, 0, 0, 0)),
+            pl.BlockSpec((pb, tgt, row_count, width), lambda i, sc: (i, 0, 0, 0)),
             h_spec,
             h_spec,
         )
@@ -135,7 +139,7 @@
     )
     grid_spec = pltpu.PrefetchScalarGridSpec(
         num_scalar_prefetch=1,
-        grid=(orb,),
+        grid=(orb // pb,),
         in_specs=in_specs,
         out_specs=out_specs,
         scratch_shapes=[pltpu.VMEM((row_count + 2 * halo, width), jnp.float32)],

time: 214 us -> 205 us (0.958)
  Pallas kernels: 69.8 us -> 60.7 us
    pallas_call x6, Pallas kernels: 69.8 us -> 60.7 us  [sweep_call(): pl.pallas_call(functools.partial(sweep_kernel, final, init is not None),...]
  transfers between devices with their start and end apart: 23 -> 23, of which waited for: 11 -> 11; matrix products, arithmetic and copies ran while one was open for 7% -> 7% of each run, Pallas kernels for 28% -> 25%
where the time goes in v9:
time: 205 us
  waiting for transfers between devices  83.2 us (41%)
  Pallas kernels  60.7 us (30%)
  starting transfers between devices  36.3 us (18%)
  local copies, waits for them, and re-layouts  14.5 us (7%)
  other arithmetic  9.09 us (4%)
    pallas_call x6, Pallas kernels, sweep_call(): pl.pallas_call(functools.partial(sweep_kernel, final, init is not None),...  60.7 us
    ppermute x6, starting transfers between devices, exchange_halos(): lax.ppermute(bwd, 'domain', backward)  32 us
    ppermute x7, waiting for transfers between devices, butterfly_sum(): total = total + lax.ppermute(x, axis, pairs)  30.4 us
    ppermute x1, waiting for transfers between devices, swap_over_y(): lax.ppermute(plus, axes, shift(1))  27.3 us
    ppermute x1, waiting for transfers between devices, swap_over_y(): plus = lax.ppermute(block[:half], axes, shift(1))  20.7 us
    convert_element_type x2, other arithmetic, pair_sums(): part = block.astype(jnp.float32)  4.51 us
  transfers between devices with their start and end apart: 23, of which 11 were waited for; matrix products, arithmetic and copies ran while one was open for 7% of the time, Pallas kernels for 25%

profile of v9, /device:TPU:16, one launch (start us, length us, event | category | flops | bytes accessed | tf_op | source)
XLA Modules:
  0.0 204.6 jit_solution(2722445301791134716)
XLA Ops:
  0.7 2.7 %dynamic-slice_bitcast_fusion = (bf16[8,2,288,192]{3,2,1,0:T(8,128)(2,1)S(1)}, bf16[8,2,288,192]{3,2,1,0:T(8,128)(2,1)S(1)}) fusion(bf16[2,8,2,288,192]{4,3,2,1,0:T(8,128)(2,1)} %v_ref.3, s32[]{:T(128)} %select_n.36, s32[]{:T(128)S(6)} %select_n.37), kind=kLoop, calls=%fused_computation.2 | loop fusion | bytes 7077896 | tf_op jit(solution)/shard_map/jit(dynamic_index_in_dim)/squeeze | solution.py:168
  5.3 8.2 %collective-permute-start.1 = (bf16[8,2,192,192]{3,2,1,0:T(8,128)(2,1)}, bf16[8,2,192,192]{3,2,1,0:T(8,128)(2,1)}, u32[]{:S(2)}, u32[]{:S(2)}) collective-permute-start(bf16[8,2,192,192]{3,2,1,0:T(8,128)(2,1)} %get-tuple-element.47), channel_id=1, source_target_pairs={{1,0},{2,1},{3,2},{4,3},{5,4},{6,5},{7,6},{8,7},{9,8},{10,9},{11,1... | collective-permute-start | bytes 3538952 | tf_op jit(solution)/shard_map/ppermute | solution.py:164
  18.9 20.7 %collective-permute-done.2 = bf16[4,288,192]{2,1,0:T(8,128)(2,1)S(1)} collective-permute-done((bf16[4,288,192]{2,1,0:T(8,128)(2,1)S(1)}, bf16[4,288,192]{2,1,0:T(8,128)(2,1)S(1)}, u32[]{:S(2)}, u32[]{:S(2)}) %collective-permute-start.2) | collective-permute-done | bytes 442400 | tf_op jit(solution)/shard_map/ppermute | solution.py:215
  39.6 2.3 %collective-permute-done.3 = bf16[4,288,192]{2,1,0:T(8,128)(2,1)} collective-permute-done((bf16[4,288,192]{2,1,0:T(8,128)(2,1)S(1)}, bf16[4,288,192]{2,1,0:T(8,128)(2,1)}, u32[]{:S(2)}, u32[]{:S(2)}) %collective-permute-start.3) | collective-permute-done | bytes 442400 | tf_op jit(solution)/shard_map/ppermute | solution.py:216
  41.9 6.0 %collective-permute-start.5 = (bf16[8,2,192,192]{3,2,1,0:T(8,128)(2,1)}, bf16[8,2,192,192]{3,2,1,0:T(8,128)(2,1)}, u32[]{:S(2)}, u32[]{:S(2)}) collective-permute-start(bf16[8,2,192,192]{3,2,1,0:T(8,128)(2,1)} %get-tuple-element.24), channel_id=1, source_target_pairs={{1,0},{2,1},{3,2},{4,3},{5,4},{6,5},{7,6},{8,7},{9,8},{10,9},{11,1... | collective-permute-start | bytes 3538952 | tf_op jit(solution)/shard_map/ppermute | solution.py:164
  51.9 10.1 %shard_map.48 = (f32[8,2,288,192]{3,2,1,0:T(8,128)}, bf16[8,2,192,192]{3,2,1,0:T(8,128)(2,1)}, bf16[8,2,192,192]{3,2,1,0:T(8,128)(2,1)}) custom-call(s32[3]{0:T(128)} %pad_add_fusion.1.sc_ref, bf16[2,8,2,288,192]{4,3,2,1,0:T(8,128)(2,1)} %v_ref.3, bf16[8,2,192,192]{3,2,1,0:T(8,128)(2,1)} %collective-permute-done.lo_ref, ...), custom_call_target="tpu_custom_call" | custom-call | flops 700710912 | bytes 11354112 | tf_op jit(solution)/shard_map/pallas_call | solution.py:147
  62.0 27.3 %collective-permute-done.6 = bf16[4,288,192]{2,1,0:T(8,128)(2,1)S(1)} collective-permute-done((bf16[4,288,192]{2,1,0:T(8,128)(2,1)S(1)}, bf16[4,288,192]{2,1,0:T(8,128)(2,1)S(1)}, u32[]{:S(2)}, u32[]{:S(2)}) %collective-permute-start.6) | collective-permute-done | bytes 442400 | tf_op jit(solution)/shard_map/ppermute | solution.py:218
  89.3 2.5 %collective-permute-done.7 = bf16[4,288,192]{2,1,0:T(8,128)(2,1)} collective-permute-done((bf16[4,288,192]{2,1,0:T(8,128)(2,1)}, bf16[4,288,192]{2,1,0:T(8,128)(2,1)}, u32[]{:S(2)}, u32[]{:S(2)}) %collective-permute-start.7) | collective-permute-done | bytes 442400 | tf_op jit(solution)/shard_map/ppermute | solution.py:218
  94.5 9.9 %shard_map.46 = (f32[8,2,288,192]{3,2,1,0:T(8,128)}, bf16[8,2,192,192]{3,2,1,0:T(8,128)(2,1)}, bf16[8,2,192,192]{3,2,1,0:T(8,128)(2,1)}) custom-call(s32[3]{0:T(128)} %pad_add_fusion.sc_ref, bf16[2,8,2,288,192]{4,3,2,1,0:T(8,128)(2,1)} %v_ref.3, bf16[8,2,192,192]{3,2,1,0:T(8,128)(2,1)} %copy-done.4, bf16[8,2,192,192]{3,2,1,0:T(8,128)(2,1)} %collective-permute-done.5.hi_ref, ...), custom_call_target="tpu_custom_call" | custom-call | flops 700710912 | bytes 11354112 | tf_op jit(solution)/shard_map/pallas_call | solution.py:147
  104.5 5.9 %collective-permute-start.9 = (bf16[8,2,192,192]{3,2,1,0:T(8,128)(2,1)}, bf16[8,2,192,192]{3,2,1,0:T(8,128)(2,1)S(1)}, u32[]{:S(2)}, u32[]{:S(2)}) collective-permute-start(bf16[8,2,192,192]{3,2,1,0:T(8,128)(2,1)} %get-tuple-element.29), channel_id=1, source_target_pairs={{1,0},{2,1},{3,2},{4,3},{5,4},{6,5},{7,6},{8,7},{9,8},{10,9},{11,1... | collective-permute-start | bytes 3538952 | tf_op jit(solution)/shard_map/ppermute | solution.py:164
  110.5 2.9 %dynamic-slice_convert_fusion = f32[8,288,192]{2,1,0:T(8,128)} fusion(bf16[32,288,192]{2,1,0:T(8,128)(2,1)} %p_ref.5, s32[]{:T(128)S(6)} %select_n.38), kind=kLoop, calls=%fused_computation.4 | loop fusion | flops 442368 | bytes 2654212 | tf_op jit(solution)/shard_map/convert_element_type | solution.py:223
  115.0 10.4 %shard_map.49 = (f32[8,2,288,192]{3,2,1,0:T(8,128)}, bf16[8,2,192,192]{3,2,1,0:T(8,128)(2,1)}, bf16[8,2,192,192]{3,2,1,0:T(8,128)(2,1)}) custom-call(s32[3]{0:T(128)} %pad_add_fusion.1.sc_ref, f32[8,2,288,192]{3,2,1,0:T(8,128)} %get-tuple-element.35.v_ref, bf16[8,2,192,192]{3,2,1,0:T(8,128)(2,1)} %collective-permute-done.19.lo_ref, ...), custom_call_target="tpu_custom_call" | custom-call | flops 700710912 | bytes 13123584 | tf_op jit(solution)/shard_map/pallas_call | solution.py:147
  125.4 6.0 %collective-permute-start.22 = (bf16[8,2,192,192]{3,2,1,0:T(8,128)(2,1)}, bf16[8,2,192,192]{3,2,1,0:T(8,128)(2,1)}, u32[]{:S(2)}, u32[]{:S(2)}) collective-permute-start(bf16[8,2,192,192]{3,2,1,0:T(8,128)(2,1)} %get-tuple-element.40), channel_id=1, source_target_pairs={{1,0},{2,1},{3,2},{4,3},{5,4},{6,5},{7,6},{8,7},{9,8},{10,9},{11,1... | collective-permute-start | bytes 3538952 | tf_op jit(solution)/shard_map/ppermute | solution.py:164
  133.8 10.9 %shard_map.47 = (f32[8,2,288,192]{3,2,1,0:T(8,128)}, bf16[8,2,192,192]{3,2,1,0:T(8,128)(2,1)}, bf16[8,2,192,192]{3,2,1,0:T(8,128)(2,1)}) custom-call(s32[3]{0:T(128)} %pad_add_fusion.sc_ref, f32[8,2,288,192]{3,2,1,0:T(8,128)} %get-tuple-element.27.v_ref, bf16[8,2,192,192]{3,2,1,0:T(8,128)(2,1)} %copy-done.5, bf16[8,2,192,192]{3,2,1,0:T(8,128)(2,1)} %copy-done.6, ...), custom_call_target="tpu_custom_call" | custom-call | flops 700710912 | bytes 13123584 | tf_op jit(solution)/shard_map/pallas_call | solution.py:147
  144.7 6.0 %collective-permute-start.11 = (bf16[8,2,192,192]{3,2,1,0:T(8,128)(2,1)}, bf16[8,2,192,192]{3,2,1,0:T(8,128)(2,1)}, u32[]{:S(2)}, u32[]{:S(2)}) collective-permute-start(bf16[8,2,192,192]{3,2,1,0:T(8,128)(2,1)} %get-tuple-element.32), channel_id=1, source_target_pairs={{1,0},{2,1},{3,2},{4,3},{5,4},{6,5},{7,6},{8,7},{9,8},{10,9},{11,1... | collective-permute-start | bytes 3538952 | tf_op jit(solution)/shard_map/ppermute | solution.py:164
  150.7 2.6 %multiply_reduce_fusion.1 = (f32[8,2]{1,0:T(8,128)S(1)}, f32[8,2]{1,0:T(8,128)S(1)}) fusion(f32[2,288,192]{2,1,0:T(8,128)S(1)} %copy-done, f32[8,288,192]{2,1,0:T(8,128)S(1)} %copy-done.3, f32[8,288,192]{2,1,0:T(8,128)} %convert_element_type.25), kind=kLoop, calls=%fused_computation.1 | loop fusion | flops 3538912 | bytes 3981440 | tf_op jit(solution)/shard_map/reduce_sum | solution.py:224
  154.6 5.1 %collective-permute-done.13 = f32[2,8,2]{1,2,0:T(2,128)S(1)} collective-permute-done((f32[2,8,2]{1,2,0:T(2,128)S(1)}, f32[2,8,2]{1,2,0:T(2,128)S(1)}, u32[]{:S(2)}, u32[]{:S(2)}) %collective-permute-start.13) | collective-permute-done | bytes 160 | tf_op jit(solution)/shard_map/ppermute | solution.py:195
  159.7 4.5 %collective-permute-done.14 = f32[2,8,2]{1,2,0:T(2,128)S(1)} collective-permute-done((f32[2,8,2]{1,2,0:T(2,128)S(1)}, f32[2,8,2]{1,2,0:T(2,128)S(1)}, u32[]{:S(2)}, u32[]{:S(2)}) %collective-permute-start.14) | collective-permute-done | bytes 160 | tf_op jit(solution)/shard_map/ppermute | solution.py:195
  164.2 7.5 %collective-permute-done.15 = f32[2,8,2]{1,2,0:T(2,128)S(1)} collective-permute-done((f32[2,8,2]{1,2,0:T(2,128)S(1)}, f32[2,8,2]{1,2,0:T(2,128)S(1)}, u32[]{:S(2)}, u32[]{:S(2)}) %collective-permute-start.15) | collective-permute-done | bytes 160 | tf_op jit(solution)/shard_map/ppermute | solution.py:195
  171.7 3.6 %collective-permute-done.16 = f32[2,8,2]{1,2,0:T(2,128)S(1)} collective-permute-done((f32[2,8,2]{1,2,0:T(2,128)S(1)}, f32[2,8,2]{1,2,0:T(2,128)S(1)}, u32[]{:S(2)}, u32[]{:S(2)}) %collective-permute-start.16) | collective-permute-done | bytes 160 | tf_op jit(solution)/shard_map/ppermute | solution.py:195
  175.3 5.1 %collective-permute-done.17 = f32[2,8,2]{1,2,0:T(2,128)S(1)} collective-permute-done((f32[2,8,2]{1,2,0:T(2,128)S(1)}, f32[2,8,2]{1,2,0:T(2,128)S(1)}, u32[]{:S(2)}, u32[]{:S(2)}) %collective-permute-start.17) | collective-permute-done | bytes 160 | tf_op jit(solution)/shard_map/ppermute | solution.py:195
  180.4 3.6 %collective-permute-done.18 = f32[2,8,2]{1,2,0:T(2,128)S(1)} collective-permute-done((f32[2,8,2]{1,2,0:T(2,128)S(1)}, f32[2,8,2]{1,2,0:T(2,128)S(1)}, u32[]{:S(2)}, u32[]{:S(2)}) %collective-permute-start.18) | collective-permute-done | bytes 160 | tf_op jit(solution)/shard_map/ppermute | solution.py:195
  185.3 9.5 %shard_map.50.rest_1_ = f32[2,288,192]{2,1,0:T(8,128)} custom-call(s32[3]{0:T(128)} %pad_add_fusion.1.sc_ref, f32[8,2,288,192]{3,2,1,0:T(8,128)} %get-tuple-element.38.v_ref, bf16[8,2,192,192]{3,2,1,0:T(8,128)(2,1)} %collective-permute-done.21.lo_ref, bf16[8,2,192,192]{3,2,1,0:T(8,128)(2,1)} %collective-permute-done.22.hi_ref, bf16[32,288,192]{2,1,0:T(8,128)(2,1)} %p_ref.5, ...), custom_call_target="tpu_custom_call" | custom-call | flops 700710912 | bytes 7667712 | tf_op jit(solution)/shard_map/pallas_call | solution.py:147
  194.8 9.7 %shard_map.51 = f32[2,288,192]{2,1,0:T(8,128)} custom-call(s32[3]{0:T(128)} %pad_add_fusion.sc_ref, f32[8,2,288,192]{3,2,1,0:T(8,128)} %get-tuple-element.30.v_ref, bf16[8,2,192,192]{3,2,1,0:T(8,128)(2,1)} %collective-permute-done.10.lo_ref, bf16[8,2,192,192]{3,2,1,0:T(8,128)(2,1)} %collective-permute-done.11.hi_ref, bf16[8,288,192]{2,1,0:T(8,128)(2,1)} %copy-done.1, ...), custom_call_target="tpu_custom_call" | custom-call | flops 700710912 | bytes 7667712 | tf_op jit(solution)/shard_map/pallas_call | solution.py:147
  (67 shorter events, 20.9 us)
Async XLA Ops:
  5.3 36.6 %collective-permute-start = (bf16[8,2,192,192]{3,2,1,0:T(8,128)(2,1)}, bf16[8,2,192,192]{3,2,1,0:T(8,128)(2,1)}, u32[]{:S(2)}, u32[]{:S(2)}) collective-permute-start(bf16[8,2,192,192]{3,2,1,0:T(8,128)(2,1)} %get-tuple-element.48), channel_id=1, source_target_pairs={{0,1},{1,2},{2,3},{3,4},{4,5},{5,6},{6,7},{7,8},{8,9},{9,10},{10,1... | collective-permute-start | bytes 3538952 | tf_op jit(solution)/shard_map/ppermute | solution.py:164
  5.3 36.6 %collective-permute-start.1 = (bf16[8,2,192,192]{3,2,1,0:T(8,128)(2,1)}, bf16[8,2,192,192]{3,2,1,0:T(8,128)(2,1)}, u32[]{:S(2)}, u32[]{:S(2)}) collective-permute-start(bf16[8,2,192,192]{3,2,1,0:T(8,128)(2,1)} %get-tuple-element.47), channel_id=1, source_target_pairs={{1,0},{2,1},{3,2},{4,3},{5,4},{6,5},{7,6},{8,7},{9,8},{10,9},{11,1... | collective-permute-start | bytes 3538952 | tf_op jit(solution)/shard_map/ppermute | solution.py:164
  14.8 24.8 %collective-permute-start.2 = (bf16[4,288,192]{2,1,0:T(8,128)(2,1)S(1)}, bf16[4,288,192]{2,1,0:T(8,128)(2,1)S(1)}, u32[]{:S(2)}, u32[]{:S(2)}) collective-permute-start(bf16[4,288,192]{2,1,0:T(8,128)(2,1)S(1)} %get-tuple-element.44), channel_id=1, source_target_pairs={{0,64},{1,65},{2,66},{3,67},{4,68},{5,69},{6,70},{7,71},{8,72},{9,... | collective-permute-start | bytes 1327112 | tf_op jit(solution)/shard_map/ppermute | solution.py:215
  15.6 26.3 %collective-permute-start.3 = (bf16[4,288,192]{2,1,0:T(8,128)(2,1)S(1)}, bf16[4,288,192]{2,1,0:T(8,128)(2,1)}, u32[]{:S(2)}, u32[]{:S(2)}) collective-permute-start(bf16[4,288,192]{2,1,0:T(8,128)(2,1)S(1)} %get-tuple-element.43), channel_id=1, source_target_pairs={{0,192},{1,193},{2,194},{3,195},{4,196},{5,197},{6,198},{7,199},{8... | collective-permute-start | bytes 1327112 | tf_op jit(solution)/shard_map/ppermute | solution.py:216
  41.9 51.0 %collective-permute-start.4 = (bf16[8,2,192,192]{3,2,1,0:T(8,128)(2,1)}, bf16[8,2,192,192]{3,2,1,0:T(8,128)(2,1)S(1)}, u32[]{:S(2)}, u32[]{:S(2)}) collective-permute-start(bf16[8,2,192,192]{3,2,1,0:T(8,128)(2,1)} %get-tuple-element.23), channel_id=1, source_target_pairs={{0,1},{1,2},{2,3},{3,4},{4,5},{5,6},{6,7},{7,8},{8,9},{9,10},{10,1... | collective-permute-start | bytes 3538952 | tf_op jit(solution)/shard_map/ppermute | solution.py:164
  41.9 51.0 %collective-permute-start.5 = (bf16[8,2,192,192]{3,2,1,0:T(8,128)(2,1)}, bf16[8,2,192,192]{3,2,1,0:T(8,128)(2,1)}, u32[]{:S(2)}, u32[]{:S(2)}) collective-permute-start(bf16[8,2,192,192]{3,2,1,0:T(8,128)(2,1)} %get-tuple-element.24), channel_id=1, source_target_pairs={{1,0},{2,1},{3,2},{4,3},{5,4},{6,5},{7,6},{8,7},{9,8},{10,9},{11,1... | collective-permute-start | bytes 3538952 | tf_op jit(solution)/shard_map/ppermute | solution.py:164
  47.9 41.4 %collective-permute-start.6 = (bf16[4,288,192]{2,1,0:T(8,128)(2,1)S(1)}, bf16[4,288,192]{2,1,0:T(8,128)(2,1)S(1)}, u32[]{:S(2)}, u32[]{:S(2)}) collective-permute-start(bf16[4,288,192]{2,1,0:T(8,128)(2,1)S(1)} %collective-permute-done.2), channel_id=1, source_target_pairs={{0,64},{1,65},{2,66},{3,67},{4,68},{5,69},{6,70},{7,71},{8,72},{9,... | collective-permute-start | bytes 1327112 | tf_op jit(solution)/shard_map/ppermute | solution.py:218
  48.1 43.6 %collective-permute-start.7 = (bf16[4,288,192]{2,1,0:T(8,128)(2,1)}, bf16[4,288,192]{2,1,0:T(8,128)(2,1)}, u32[]{:S(2)}, u32[]{:S(2)}) collective-permute-start(bf16[4,288,192]{2,1,0:T(8,128)(2,1)} %collective-permute-done.3), channel_id=1, source_target_pairs={{0,192},{1,193},{2,194},{3,195},{4,196},{5,197},{6,198},{7,199},{8... | collective-permute-start | bytes 1327112 | tf_op jit(solution)/shard_map/ppermute | solution.py:218
  62.0 53.0 %collective-permute-start.19 = (bf16[8,2,192,192]{3,2,1,0:T(8,128)(2,1)}, bf16[8,2,192,192]{3,2,1,0:T(8,128)(2,1)}, u32[]{:S(2)}, u32[]{:S(2)}) collective-permute-start(bf16[8,2,192,192]{3,2,1,0:T(8,128)(2,1)} %get-tuple-element.36), channel_id=1, source_target_pairs={{0,1},{1,2},{2,3},{3,4},{4,5},{5,6},{6,7},{7,8},{8,9},{9,10},{10,1... | collective-permute-start | bytes 3538952 | tf_op jit(solution)/shard_map/ppermute | solution.py:164
  89.3 25.7 %collective-permute-start.20 = (bf16[8,2,192,192]{3,2,1,0:T(8,128)(2,1)}, bf16[8,2,192,192]{3,2,1,0:T(8,128)(2,1)}, u32[]{:S(2)}, u32[]{:S(2)}) collective-permute-start(bf16[8,2,192,192]{3,2,1,0:T(8,128)(2,1)} %get-tuple-element.37), channel_id=1, source_target_pairs={{1,0},{2,1},{3,2},{4,3},{5,4},{6,5},{7,6},{8,7},{9,8},{10,9},{11,1... | collective-permute-start | bytes 3538952 | tf_op jit(solution)/shard_map/ppermute | solution.py:164
  104.4 27.0 %collective-permute-start.8 = (bf16[8,2,192,192]{3,2,1,0:T(8,128)(2,1)}, bf16[8,2,192,192]{3,2,1,0:T(8,128)(2,1)S(1)}, u32[]{:S(2)}, u32[]{:S(2)}) collective-permute-start(bf16[8,2,192,192]{3,2,1,0:T(8,128)(2,1)} %get-tuple-element.28), channel_id=1, source_target_pairs={{0,1},{1,2},{2,3},{3,4},{4,5},{5,6},{6,7},{7,8},{8,9},{9,10},{10,1... | collective-permute-start | bytes 3538952 | tf_op jit(solution)/shard_map/ppermute | solution.py:164
  104.5 26.9 %collective-permute-start.9 = (bf16[8,2,192,192]{3,2,1,0:T(8,128)(2,1)}, bf16[8,2,192,192]{3,2,1,0:T(8,128)(2,1)S(1)}, u32[]{:S(2)}, u32[]{:S(2)}) collective-permute-start(bf16[8,2,192,192]{3,2,1,0:T(8,128)(2,1)} %get-tuple-element.29), channel_id=1, source_target_pairs={{1,0},{2,1},{3,2},{4,3},{5,4},{6,5},{7,6},{8,7},{9,8},{10,9},{11,1... | collective-permute-start | bytes 3538952 | tf_op jit(solution)/shard_map/ppermute | solution.py:164
  125.4 59.9 %collective-permute-start.21 = (bf16[8,2,192,192]{3,2,1,0:T(8,128)(2,1)}, bf16[8,2,192,192]{3,2,1,0:T(8,128)(2,1)}, u32[]{:S(2)}, u32[]{:S(2)}) collective-permute-start(bf16[8,2,192,192]{3,2,1,0:T(8,128)(2,1)} %get-tuple-element.39), channel_id=1, source_target_pairs={{0,1},{1,2},{2,3},{3,4},{4,5},{5,6},{6,7},{7,8},{8,9},{9,10},{10,1... | collective-permute-start | bytes 3538952 | tf_op jit(solution)/shard_map/ppermute | solution.py:164
  125.4 59.9 %collective-permute-start.22 = (bf16[8,2,192,192]{3,2,1,0:T(8,128)(2,1)}, bf16[8,2,192,192]{3,2,1,0:T(8,128)(2,1)}, u32[]{:S(2)}, u32[]{:S(2)}) collective-permute-start(bf16[8,2,192,192]{3,2,1,0:T(8,128)(2,1)} %get-tuple-element.40), channel_id=1, source_target_pairs={{1,0},{2,1},{3,2},{4,3},{5,4},{6,5},{7,6},{8,7},{9,8},{10,9},{11,1... | collective-permute-start | bytes 3538952 | tf_op jit(solution)/shard_map/ppermute | solution.py:164
  133.8 16.9 %copy-start.3 = (f32[8,288,192]{2,1,0:T(8,128)S(1)}, f32[8,288,192]{2,1,0:T(8,128)}, u32[]{:S(2)}) copy-start(f32[8,288,192]{2,1,0:T(8,128)} %dynamic-slice_convert_fusion) | copy-start | bytes 5308420
  144.7 50.1 %collective-permute-start.10 = (bf16[8,2,192,192]{3,2,1,0:T(8,128)(2,1)}, bf16[8,2,192,192]{3,2,1,0:T(8,128)(2,1)}, u32[]{:S(2)}, u32[]{:S(2)}) collective-permute-start(bf16[8,2,192,192]{3,2,1,0:T(8,128)(2,1)} %get-tuple-element.31), channel_id=1, source_target_pairs={{0,1},{1,2},{2,3},{3,4},{4,5},{5,6},{6,7},{7,8},{8,9},{9,10},{10,1... | collective-permute-start | bytes 3538952 | tf_op jit(solution)/shard_map/ppermute | solution.py:164
  144.7 50.1 %collective-permute-start.11 = (bf16[8,2,192,192]{3,2,1,0:T(8,128)(2,1)}, bf16[8,2,192,192]{3,2,1,0:T(8,128)(2,1)}, u32[]{:S(2)}, u32[]{:S(2)}) collective-permute-start(bf16[8,2,192,192]{3,2,1,0:T(8,128)(2,1)} %get-tuple-element.32), channel_id=1, source_target_pairs={{1,0},{2,1},{3,2},{4,3},{5,4},{6,5},{7,6},{8,7},{9,8},{10,9},{11,1... | collective-permute-start | bytes 3538952 | tf_op jit(solution)/shard_map/ppermute | solution.py:164
  153.5 1.2 collective-permute-start.12
  154.6 5.1 %collective-permute-start.13 = (f32[2,8,2]{1,2,0:T(2,128)S(1)}, f32[2,8,2]{1,2,0:T(2,128)S(1)}, u32[]{:S(2)}, u32[]{:S(2)}) collective-permute-start(f32[2,8,2]{1,2,0:T(2,128)S(1)} %fusion.7), channel_id=1, source_target_pairs={{0,2},{1,3},{2,0},{3,1},{4,6},{5,7},{6,4},{7,5},{8,10},{9,11},{10,... | collective-permute-start | bytes 392 | tf_op jit(solution)/shard_map/ppermute | solution.py:195
  159.7 4.5 %collective-permute-start.14 = (f32[2,8,2]{1,2,0:T(2,128)S(1)}, f32[2,8,2]{1,2,0:T(2,128)S(1)}, u32[]{:S(2)}, u32[]{:S(2)}) collective-permute-start(f32[2,8,2]{1,2,0:T(2,128)S(1)} %fusion.10), channel_id=1, source_target_pairs={{0,4},{1,5},{2,6},{3,7},{4,0},{5,1},{6,2},{7,3},{8,12},{9,13},{10,... | collective-permute-start | bytes 392 | tf_op jit(solution)/shard_map/ppermute | solution.py:195
  164.2 7.5 %collective-permute-start.15 = (f32[2,8,2]{1,2,0:T(2,128)S(1)}, f32[2,8,2]{1,2,0:T(2,128)S(1)}, u32[]{:S(2)}, u32[]{:S(2)}) collective-permute-start(f32[2,8,2]{1,2,0:T(2,128)S(1)} %add.74), channel_id=1, source_target_pairs={{0,8},{1,9},{2,10},{3,11},{4,12},{5,13},{6,14},{7,15},{8,0},{9,1},... | collective-permute-start | bytes 392 | tf_op jit(solution)/shard_map/ppermute | solution.py:195
  171.7 3.6 %collective-permute-start.16 = (f32[2,8,2]{1,2,0:T(2,128)S(1)}, f32[2,8,2]{1,2,0:T(2,128)S(1)}, u32[]{:S(2)}, u32[]{:S(2)}) collective-permute-start(f32[2,8,2]{1,2,0:T(2,128)S(1)} %add.75), channel_id=1, source_target_pairs={{0,16},{1,17},{2,18},{3,19},{4,20},{5,21},{6,22},{7,23},{8,24},{9,... | collective-permute-start | bytes 392 | tf_op jit(solution)/shard_map/ppermute | solution.py:195
  175.3 5.1 %collective-permute-start.17 = (f32[2,8,2]{1,2,0:T(2,128)S(1)}, f32[2,8,2]{1,2,0:T(2,128)S(1)}, u32[]{:S(2)}, u32[]{:S(2)}) collective-permute-start(f32[2,8,2]{1,2,0:T(2,128)S(1)} %add.76), channel_id=1, source_target_pairs={{0,32},{1,33},{2,34},{3,35},{4,36},{5,37},{6,38},{7,39},{8,40},{9,... | collective-permute-start | bytes 392 | tf_op jit(solution)/shard_map/ppermute | solution.py:195
  180.4 3.6 %collective-permute-start.18 = (f32[2,8,2]{1,2,0:T(2,128)S(1)}, f32[2,8,2]{1,2,0:T(2,128)S(1)}, u32[]{:S(2)}, u32[]{:S(2)}) collective-permute-start(f32[2,8,2]{1,2,0:T(2,128)S(1)} %add.77), channel_id=1, source_target_pairs={{0,64},{1,65},{2,66},{3,67},{4,68},{5,69},{6,70},{7,71},{8,72},{9,... | collective-permute-start | bytes 392 | tf_op jit(solution)/shard_map/ppermute | solution.py:195
  (6 other events, 30.7 us)

commit v10 on v9

--- a/solution.py
+++ b/solution.py
@@ -17,7 +17,7 @@
 
 
 coupling = 4.0 * math.pi
-PER_STEP = 2
+PER_STEP = 4
 
 
 def circulant(width):

time: 205 us -> 207 us (level)
  no operation moved by 1% of the time
where the time goes in v10:
time: 207 us; the launch traced here: 206 us
  waiting for transfers between devices  83.3 us (40%)
  Pallas kernels  62.5 us (30%)
  starting transfers between devices  36.3 us (18%)
  local copies, waits for them, and re-layouts  14.5 us (7%)
  other arithmetic  9.09 us (4%)
    pallas_call x6, Pallas kernels, sweep_call(): pl.pallas_call(functools.partial(sweep_kernel, final, init is not None),...  62.5 us
    ppermute x6, starting transfers between devices, exchange_halos(): lax.ppermute(bwd, 'domain', backward)  32 us
    ppermute x7, waiting for transfers between devices, butterfly_sum(): total = total + lax.ppermute(x, axis, pairs)  30.6 us
    ppermute x1, waiting for transfers between devices, swap_over_y(): lax.ppermute(plus, axes, shift(1))  27.2 us
    ppermute x1, waiting for transfers between devices, swap_over_y(): plus = lax.ppermute(block[:half], axes, shift(1))  20.7 us
    convert_element_type x2, other arithmetic, pair_sums(): part = block.astype(jnp.float32)  4.51 us
  transfers between devices with their start and end apart: 23, of which 11 were waited for; matrix products, arithmetic and copies ran while one was open for 7% of the time, Pallas kernels for 25%

profile of v10, /device:TPU:16, one launch (start us, length us, event | category | flops | bytes accessed | tf_op | source)
XLA Modules:
  0.0 206.4 jit_solution(1927014410938704760)
XLA Ops:
  0.7 2.7 %dynamic-slice_bitcast_fusion = (bf16[8,2,288,192]{3,2,1,0:T(8,128)(2,1)S(1)}, bf16[8,2,288,192]{3,2,1,0:T(8,128)(2,1)S(1)}) fusion(bf16[2,8,2,288,192]{4,3,2,1,0:T(8,128)(2,1)} %v_ref.3, s32[]{:T(128)} %select_n.36, s32[]{:T(128)S(6)} %select_n.37), kind=kLoop, calls=%fused_computation.2 | loop fusion | bytes 7077896 | tf_op jit(solution)/shard_map/jit(dynamic_index_in_dim)/squeeze | solution.py:168
  5.3 8.2 %collective-permute-start.1 = (bf16[8,2,192,192]{3,2,1,0:T(8,128)(2,1)}, bf16[8,2,192,192]{3,2,1,0:T(8,128)(2,1)}, u32[]{:S(2)}, u32[]{:S(2)}) collective-permute-start(bf16[8,2,192,192]{3,2,1,0:T(8,128)(2,1)} %get-tuple-element.47), channel_id=1, source_target_pairs={{1,0},{2,1},{3,2},{4,3},{5,4},{6,5},{7,6},{8,7},{9,8},{10,9},{11,1... | collective-permute-start | bytes 3538952 | tf_op jit(solution)/shard_map/ppermute | solution.py:164
  18.9 20.7 %collective-permute-done.2 = bf16[4,288,192]{2,1,0:T(8,128)(2,1)S(1)} collective-permute-done((bf16[4,288,192]{2,1,0:T(8,128)(2,1)S(1)}, bf16[4,288,192]{2,1,0:T(8,128)(2,1)S(1)}, u32[]{:S(2)}, u32[]{:S(2)}) %collective-permute-start.2) | collective-permute-done | bytes 442400 | tf_op jit(solution)/shard_map/ppermute | solution.py:215
  39.6 2.3 %collective-permute-done.3 = bf16[4,288,192]{2,1,0:T(8,128)(2,1)} collective-permute-done((bf16[4,288,192]{2,1,0:T(8,128)(2,1)S(1)}, bf16[4,288,192]{2,1,0:T(8,128)(2,1)}, u32[]{:S(2)}, u32[]{:S(2)}) %collective-permute-start.3) | collective-permute-done | bytes 442400 | tf_op jit(solution)/shard_map/ppermute | solution.py:216
  41.9 6.0 %collective-permute-start.5 = (bf16[8,2,192,192]{3,2,1,0:T(8,128)(2,1)}, bf16[8,2,192,192]{3,2,1,0:T(8,128)(2,1)}, u32[]{:S(2)}, u32[]{:S(2)}) collective-permute-start(bf16[8,2,192,192]{3,2,1,0:T(8,128)(2,1)} %get-tuple-element.24), channel_id=1, source_target_pairs={{1,0},{2,1},{3,2},{4,3},{5,4},{6,5},{7,6},{8,7},{9,8},{10,9},{11,1... | collective-permute-start | bytes 3538952 | tf_op jit(solution)/shard_map/ppermute | solution.py:164
  51.9 10.2 %shard_map.48 = (f32[8,2,288,192]{3,2,1,0:T(8,128)}, bf16[8,2,192,192]{3,2,1,0:T(8,128)(2,1)}, bf16[8,2,192,192]{3,2,1,0:T(8,128)(2,1)}) custom-call(s32[3]{0:T(128)} %pad_add_fusion.1.sc_ref, bf16[2,8,2,288,192]{4,3,2,1,0:T(8,128)(2,1)} %v_ref.3, bf16[8,2,192,192]{3,2,1,0:T(8,128)(2,1)} %collective-permute-done.lo_ref, ...), custom_call_target="tpu_custom_call" | custom-call | flops 700710912 | bytes 11354112 | tf_op jit(solution)/shard_map/pallas_call | solution.py:147
  62.1 27.2 %collective-permute-done.6 = bf16[4,288,192]{2,1,0:T(8,128)(2,1)S(1)} collective-permute-done((bf16[4,288,192]{2,1,0:T(8,128)(2,1)S(1)}, bf16[4,288,192]{2,1,0:T(8,128)(2,1)S(1)}, u32[]{:S(2)}, u32[]{:S(2)}) %collective-permute-start.6) | collective-permute-done | bytes 442400 | tf_op jit(solution)/shard_map/ppermute | solution.py:218
  89.3 2.5 %collective-permute-done.7 = bf16[4,288,192]{2,1,0:T(8,128)(2,1)} collective-permute-done((bf16[4,288,192]{2,1,0:T(8,128)(2,1)}, bf16[4,288,192]{2,1,0:T(8,128)(2,1)}, u32[]{:S(2)}, u32[]{:S(2)}) %collective-permute-start.7) | collective-permute-done | bytes 442400 | tf_op jit(solution)/shard_map/ppermute | solution.py:218
  94.5 10.1 %shard_map.46 = (f32[8,2,288,192]{3,2,1,0:T(8,128)}, bf16[8,2,192,192]{3,2,1,0:T(8,128)(2,1)}, bf16[8,2,192,192]{3,2,1,0:T(8,128)(2,1)}) custom-call(s32[3]{0:T(128)} %pad_add_fusion.sc_ref, bf16[2,8,2,288,192]{4,3,2,1,0:T(8,128)(2,1)} %v_ref.3, bf16[8,2,192,192]{3,2,1,0:T(8,128)(2,1)} %copy-done.4, bf16[8,2,192,192]{3,2,1,0:T(8,128)(2,1)} %collective-permute-done.5.hi_ref, ...), custom_call_target="tpu_custom_call" | custom-call | flops 700710912 | bytes 11354112 | tf_op jit(solution)/shard_map/pallas_call | solution.py:147
  104.6 6.0 %collective-permute-start.9 = (bf16[8,2,192,192]{3,2,1,0:T(8,128)(2,1)}, bf16[8,2,192,192]{3,2,1,0:T(8,128)(2,1)S(1)}, u32[]{:S(2)}, u32[]{:S(2)}) collective-permute-start(bf16[8,2,192,192]{3,2,1,0:T(8,128)(2,1)} %get-tuple-element.29), channel_id=1, source_target_pairs={{1,0},{2,1},{3,2},{4,3},{5,4},{6,5},{7,6},{8,7},{9,8},{10,9},{11,1... | collective-permute-start | bytes 3538952 | tf_op jit(solution)/shard_map/ppermute | solution.py:164
  110.5 2.9 %dynamic-slice_convert_fusion = f32[8,288,192]{2,1,0:T(8,128)} fusion(bf16[32,288,192]{2,1,0:T(8,128)(2,1)} %p_ref.5, s32[]{:T(128)S(6)} %select_n.38), kind=kLoop, calls=%fused_computation.4 | loop fusion | flops 442368 | bytes 2654212 | tf_op jit(solution)/shard_map/convert_element_type | solution.py:223
  115.0 10.7 %shard_map.49 = (f32[8,2,288,192]{3,2,1,0:T(8,128)}, bf16[8,2,192,192]{3,2,1,0:T(8,128)(2,1)}, bf16[8,2,192,192]{3,2,1,0:T(8,128)(2,1)}) custom-call(s32[3]{0:T(128)} %pad_add_fusion.1.sc_ref, f32[8,2,288,192]{3,2,1,0:T(8,128)} %get-tuple-element.35.v_ref, bf16[8,2,192,192]{3,2,1,0:T(8,128)(2,1)} %collective-permute-done.19.lo_ref, ...), custom_call_target="tpu_custom_call" | custom-call | flops 700710912 | bytes 13123584 | tf_op jit(solution)/shard_map/pallas_call | solution.py:147
  125.7 6.0 %collective-permute-start.22 = (bf16[8,2,192,192]{3,2,1,0:T(8,128)(2,1)}, bf16[8,2,192,192]{3,2,1,0:T(8,128)(2,1)}, u32[]{:S(2)}, u32[]{:S(2)}) collective-permute-start(bf16[8,2,192,192]{3,2,1,0:T(8,128)(2,1)} %get-tuple-element.40), channel_id=1, source_target_pairs={{1,0},{2,1},{3,2},{4,3},{5,4},{6,5},{7,6},{8,7},{9,8},{10,9},{11,1... | collective-permute-start | bytes 3538952 | tf_op jit(solution)/shard_map/ppermute | solution.py:164
  134.1 11.6 %shard_map.47 = (f32[8,2,288,192]{3,2,1,0:T(8,128)}, bf16[8,2,192,192]{3,2,1,0:T(8,128)(2,1)}, bf16[8,2,192,192]{3,2,1,0:T(8,128)(2,1)}) custom-call(s32[3]{0:T(128)} %pad_add_fusion.sc_ref, f32[8,2,288,192]{3,2,1,0:T(8,128)} %get-tuple-element.27.v_ref, bf16[8,2,192,192]{3,2,1,0:T(8,128)(2,1)} %copy-done.5, bf16[8,2,192,192]{3,2,1,0:T(8,128)(2,1)} %copy-done.6, ...), custom_call_target="tpu_custom_call" | custom-call | flops 700710912 | bytes 13123584 | tf_op jit(solution)/shard_map/pallas_call | solution.py:147
  145.6 6.0 %collective-permute-start.11 = (bf16[8,2,192,192]{3,2,1,0:T(8,128)(2,1)}, bf16[8,2,192,192]{3,2,1,0:T(8,128)(2,1)}, u32[]{:S(2)}, u32[]{:S(2)}) collective-permute-start(bf16[8,2,192,192]{3,2,1,0:T(8,128)(2,1)} %get-tuple-element.32), channel_id=1, source_target_pairs={{1,0},{2,1},{3,2},{4,3},{5,4},{6,5},{7,6},{8,7},{9,8},{10,9},{11,1... | collective-permute-start | bytes 3538952 | tf_op jit(solution)/shard_map/ppermute | solution.py:164
  151.6 2.6 %multiply_reduce_fusion.1 = (f32[8,2]{1,0:T(8,128)S(1)}, f32[8,2]{1,0:T(8,128)S(1)}) fusion(f32[2,288,192]{2,1,0:T(8,128)S(1)} %copy-done, f32[8,288,192]{2,1,0:T(8,128)S(1)} %copy-done.3, f32[8,288,192]{2,1,0:T(8,128)} %convert_element_type.25), kind=kLoop, calls=%fused_computation.1 | loop fusion | flops 3538912 | bytes 3981440 | tf_op jit(solution)/shard_map/reduce_sum | solution.py:224
  155.6 5.3 %collective-permute-done.13 = f32[2,8,2]{1,2,0:T(2,128)S(1)} collective-permute-done((f32[2,8,2]{1,2,0:T(2,128)S(1)}, f32[2,8,2]{1,2,0:T(2,128)S(1)}, u32[]{:S(2)}, u32[]{:S(2)}) %collective-permute-start.13) | collective-permute-done | bytes 160 | tf_op jit(solution)/shard_map/ppermute | solution.py:195
  160.9 4.5 %collective-permute-done.14 = f32[2,8,2]{1,2,0:T(2,128)S(1)} collective-permute-done((f32[2,8,2]{1,2,0:T(2,128)S(1)}, f32[2,8,2]{1,2,0:T(2,128)S(1)}, u32[]{:S(2)}, u32[]{:S(2)}) %collective-permute-start.14) | collective-permute-done | bytes 160 | tf_op jit(solution)/shard_map/ppermute | solution.py:195
  165.3 7.5 %collective-permute-done.15 = f32[2,8,2]{1,2,0:T(2,128)S(1)} collective-permute-done((f32[2,8,2]{1,2,0:T(2,128)S(1)}, f32[2,8,2]{1,2,0:T(2,128)S(1)}, u32[]{:S(2)}, u32[]{:S(2)}) %collective-permute-start.15) | collective-permute-done | bytes 160 | tf_op jit(solution)/shard_map/ppermute | solution.py:195
  172.8 3.6 %collective-permute-done.16 = f32[2,8,2]{1,2,0:T(2,128)S(1)} collective-permute-done((f32[2,8,2]{1,2,0:T(2,128)S(1)}, f32[2,8,2]{1,2,0:T(2,128)S(1)}, u32[]{:S(2)}, u32[]{:S(2)}) %collective-permute-start.16) | collective-permute-done | bytes 160 | tf_op jit(solution)/shard_map/ppermute | solution.py:195
  176.4 5.1 %collective-permute-done.17 = f32[2,8,2]{1,2,0:T(2,128)S(1)} collective-permute-done((f32[2,8,2]{1,2,0:T(2,128)S(1)}, f32[2,8,2]{1,2,0:T(2,128)S(1)}, u32[]{:S(2)}, u32[]{:S(2)}) %collective-permute-start.17) | collective-permute-done | bytes 160 | tf_op jit(solution)/shard_map/ppermute | solution.py:195
  181.6 3.6 %collective-permute-done.18 = f32[2,8,2]{1,2,0:T(2,128)S(1)} collective-permute-done((f32[2,8,2]{1,2,0:T(2,128)S(1)}, f32[2,8,2]{1,2,0:T(2,128)S(1)}, u32[]{:S(2)}, u32[]{:S(2)}) %collective-permute-start.18) | collective-permute-done | bytes 160 | tf_op jit(solution)/shard_map/ppermute | solution.py:195
  186.5 9.8 %shard_map.50.rest_1_ = f32[2,288,192]{2,1,0:T(8,128)} custom-call(s32[3]{0:T(128)} %pad_add_fusion.1.sc_ref, f32[8,2,288,192]{3,2,1,0:T(8,128)} %get-tuple-element.38.v_ref, bf16[8,2,192,192]{3,2,1,0:T(8,128)(2,1)} %collective-permute-done.21.lo_ref, bf16[8,2,192,192]{3,2,1,0:T(8,128)(2,1)} %collective-permute-done.22.hi_ref, bf16[32,288,192]{2,1,0:T(8,128)(2,1)} %p_ref.5, ...), custom_call_target="tpu_custom_call" | custom-call | flops 700710912 | bytes 7667712 | tf_op jit(solution)/shard_map/pallas_call | solution.py:147
  196.3 10.0 %shard_map.51 = f32[2,288,192]{2,1,0:T(8,128)} custom-call(s32[3]{0:T(128)} %pad_add_fusion.sc_ref, f32[8,2,288,192]{3,2,1,0:T(8,128)} %get-tuple-element.30.v_ref, bf16[8,2,192,192]{3,2,1,0:T(8,128)(2,1)} %collective-permute-done.10.lo_ref, bf16[8,2,192,192]{3,2,1,0:T(8,128)(2,1)} %collective-permute-done.11.hi_ref, bf16[8,288,192]{2,1,0:T(8,128)(2,1)} %copy-done.1, ...), custom_call_target="tpu_custom_call" | custom-call | flops 700710912 | bytes 7667712 | tf_op jit(solution)/shard_map/pallas_call | solution.py:147
  (67 shorter events, 20.8 us)
Async XLA Ops:
  5.3 36.6 %collective-permute-start = (bf16[8,2,192,192]{3,2,1,0:T(8,128)(2,1)}, bf16[8,2,192,192]{3,2,1,0:T(8,128)(2,1)}, u32[]{:S(2)}, u32[]{:S(2)}) collective-permute-start(bf16[8,2,192,192]{3,2,1,0:T(8,128)(2,1)} %get-tuple-element.48), channel_id=1, source_target_pairs={{0,1},{1,2},{2,3},{3,4},{4,5},{5,6},{6,7},{7,8},{8,9},{9,10},{10,1... | collective-permute-start | bytes 3538952 | tf_op jit(solution)/shard_map/ppermute | solution.py:164
  5.3 36.6 %collective-permute-start.1 = (bf16[8,2,192,192]{3,2,1,0:T(8,128)(2,1)}, bf16[8,2,192,192]{3,2,1,0:T(8,128)(2,1)}, u32[]{:S(2)}, u32[]{:S(2)}) collective-permute-start(bf16[8,2,192,192]{3,2,1,0:T(8,128)(2,1)} %get-tuple-element.47), channel_id=1, source_target_pairs={{1,0},{2,1},{3,2},{4,3},{5,4},{6,5},{7,6},{8,7},{9,8},{10,9},{11,1... | collective-permute-start | bytes 3538952 | tf_op jit(solution)/shard_map/ppermute | solution.py:164
  14.8 24.8 %collective-permute-start.2 = (bf16[4,288,192]{2,1,0:T(8,128)(2,1)S(1)}, bf16[4,288,192]{2,1,0:T(8,128)(2,1)S(1)}, u32[]{:S(2)}, u32[]{:S(2)}) collective-permute-start(bf16[4,288,192]{2,1,0:T(8,128)(2,1)S(1)} %get-tuple-element.44), channel_id=1, source_target_pairs={{0,64},{1,65},{2,66},{3,67},{4,68},{5,69},{6,70},{7,71},{8,72},{9,... | collective-permute-start | bytes 1327112 | tf_op jit(solution)/shard_map/ppermute | solution.py:215
  15.6 26.3 %collective-permute-start.3 = (bf16[4,288,192]{2,1,0:T(8,128)(2,1)S(1)}, bf16[4,288,192]{2,1,0:T(8,128)(2,1)}, u32[]{:S(2)}, u32[]{:S(2)}) collective-permute-start(bf16[4,288,192]{2,1,0:T(8,128)(2,1)S(1)} %get-tuple-element.43), channel_id=1, source_target_pairs={{0,192},{1,193},{2,194},{3,195},{4,196},{5,197},{6,198},{7,199},{8... | collective-permute-start | bytes 1327112 | tf_op jit(solution)/shard_map/ppermute | solution.py:216
  41.9 51.0 %collective-permute-start.4 = (bf16[8,2,192,192]{3,2,1,0:T(8,128)(2,1)}, bf16[8,2,192,192]{3,2,1,0:T(8,128)(2,1)S(1)}, u32[]{:S(2)}, u32[]{:S(2)}) collective-permute-start(bf16[8,2,192,192]{3,2,1,0:T(8,128)(2,1)} %get-tuple-element.23), channel_id=1, source_target_pairs={{0,1},{1,2},{2,3},{3,4},{4,5},{5,6},{6,7},{7,8},{8,9},{9,10},{10,1... | collective-permute-start | bytes 3538952 | tf_op jit(solution)/shard_map/ppermute | solution.py:164
  41.9 51.0 %collective-permute-start.5 = (bf16[8,2,192,192]{3,2,1,0:T(8,128)(2,1)}, bf16[8,2,192,192]{3,2,1,0:T(8,128)(2,1)}, u32[]{:S(2)}, u32[]{:S(2)}) collective-permute-start(bf16[8,2,192,192]{3,2,1,0:T(8,128)(2,1)} %get-tuple-element.24), channel_id=1, source_target_pairs={{1,0},{2,1},{3,2},{4,3},{5,4},{6,5},{7,6},{8,7},{9,8},{10,9},{11,1... | collective-permute-start | bytes 3538952 | tf_op jit(solution)/shard_map/ppermute | solution.py:164
  47.9 41.4 %collective-permute-start.6 = (bf16[4,288,192]{2,1,0:T(8,128)(2,1)S(1)}, bf16[4,288,192]{2,1,0:T(8,128)(2,1)S(1)}, u32[]{:S(2)}, u32[]{:S(2)}) collective-permute-start(bf16[4,288,192]{2,1,0:T(8,128)(2,1)S(1)} %collective-permute-done.2), channel_id=1, source_target_pairs={{0,64},{1,65},{2,66},{3,67},{4,68},{5,69},{6,70},{7,71},{8,72},{9,... | collective-permute-start | bytes 1327112 | tf_op jit(solution)/shard_map/ppermute | solution.py:218
  48.1 43.6 %collective-permute-start.7 = (bf16[4,288,192]{2,1,0:T(8,128)(2,1)}, bf16[4,288,192]{2,1,0:T(8,128)(2,1)}, u32[]{:S(2)}, u32[]{:S(2)}) collective-permute-start(bf16[4,288,192]{2,1,0:T(8,128)(2,1)} %collective-permute-done.3), channel_id=1, source_target_pairs={{0,192},{1,193},{2,194},{3,195},{4,196},{5,197},{6,198},{7,199},{8... | collective-permute-start | bytes 1327112 | tf_op jit(solution)/shard_map/ppermute | solution.py:218
  62.1 53.0 %collective-permute-start.19 = (bf16[8,2,192,192]{3,2,1,0:T(8,128)(2,1)}, bf16[8,2,192,192]{3,2,1,0:T(8,128)(2,1)}, u32[]{:S(2)}, u32[]{:S(2)}) collective-permute-start(bf16[8,2,192,192]{3,2,1,0:T(8,128)(2,1)} %get-tuple-element.36), channel_id=1, source_target_pairs={{0,1},{1,2},{2,3},{3,4},{4,5},{5,6},{6,7},{7,8},{8,9},{9,10},{10,1... | collective-permute-start | bytes 3538952 | tf_op jit(solution)/shard_map/ppermute | solution.py:164
  89.3 25.8 %collective-permute-start.20 = (bf16[8,2,192,192]{3,2,1,0:T(8,128)(2,1)}, bf16[8,2,192,192]{3,2,1,0:T(8,128)(2,1)}, u32[]{:S(2)}, u32[]{:S(2)}) collective-permute-start(bf16[8,2,192,192]{3,2,1,0:T(8,128)(2,1)} %get-tuple-element.37), channel_id=1, source_target_pairs={{1,0},{2,1},{3,2},{4,3},{5,4},{6,5},{7,6},{8,7},{9,8},{10,9},{11,1... | collective-permute-start | bytes 3538952 | tf_op jit(solution)/shard_map/ppermute | solution.py:164
  104.6 27.1 %collective-permute-start.8 = (bf16[8,2,192,192]{3,2,1,0:T(8,128)(2,1)}, bf16[8,2,192,192]{3,2,1,0:T(8,128)(2,1)S(1)}, u32[]{:S(2)}, u32[]{:S(2)}) collective-permute-start(bf16[8,2,192,192]{3,2,1,0:T(8,128)(2,1)} %get-tuple-element.28), channel_id=1, source_target_pairs={{0,1},{1,2},{2,3},{3,4},{4,5},{5,6},{6,7},{7,8},{8,9},{9,10},{10,1... | collective-permute-start | bytes 3538952 | tf_op jit(solution)/shard_map/ppermute | solution.py:164
  104.6 27.1 %collective-permute-start.9 = (bf16[8,2,192,192]{3,2,1,0:T(8,128)(2,1)}, bf16[8,2,192,192]{3,2,1,0:T(8,128)(2,1)S(1)}, u32[]{:S(2)}, u32[]{:S(2)}) collective-permute-start(bf16[8,2,192,192]{3,2,1,0:T(8,128)(2,1)} %get-tuple-element.29), channel_id=1, source_target_pairs={{1,0},{2,1},{3,2},{4,3},{5,4},{6,5},{7,6},{8,7},{9,8},{10,9},{11,1... | collective-permute-start | bytes 3538952 | tf_op jit(solution)/shard_map/ppermute | solution.py:164
  125.7 60.8 %collective-permute-start.21 = (bf16[8,2,192,192]{3,2,1,0:T(8,128)(2,1)}, bf16[8,2,192,192]{3,2,1,0:T(8,128)(2,1)}, u32[]{:S(2)}, u32[]{:S(2)}) collective-permute-start(bf16[8,2,192,192]{3,2,1,0:T(8,128)(2,1)} %get-tuple-element.39), channel_id=1, source_target_pairs={{0,1},{1,2},{2,3},{3,4},{4,5},{5,6},{6,7},{7,8},{8,9},{9,10},{10,1... | collective-permute-start | bytes 3538952 | tf_op jit(solution)/shard_map/ppermute | solution.py:164
  125.7 60.8 %collective-permute-start.22 = (bf16[8,2,192,192]{3,2,1,0:T(8,128)(2,1)}, bf16[8,2,192,192]{3,2,1,0:T(8,128)(2,1)}, u32[]{:S(2)}, u32[]{:S(2)}) collective-permute-start(bf16[8,2,192,192]{3,2,1,0:T(8,128)(2,1)} %get-tuple-element.40), channel_id=1, source_target_pairs={{1,0},{2,1},{3,2},{4,3},{5,4},{6,5},{7,6},{8,7},{9,8},{10,9},{11,1... | collective-permute-start | bytes 3538952 | tf_op jit(solution)/shard_map/ppermute | solution.py:164
  134.1 17.6 %copy-start.3 = (f32[8,288,192]{2,1,0:T(8,128)S(1)}, f32[8,288,192]{2,1,0:T(8,128)}, u32[]{:S(2)}) copy-start(f32[8,288,192]{2,1,0:T(8,128)} %dynamic-slice_convert_fusion) | copy-start | bytes 5308420
  145.6 50.7 %collective-permute-start.10 = (bf16[8,2,192,192]{3,2,1,0:T(8,128)(2,1)}, bf16[8,2,192,192]{3,2,1,0:T(8,128)(2,1)}, u32[]{:S(2)}, u32[]{:S(2)}) collective-permute-start(bf16[8,2,192,192]{3,2,1,0:T(8,128)(2,1)} %get-tuple-element.31), channel_id=1, source_target_pairs={{0,1},{1,2},{2,3},{3,4},{4,5},{5,6},{6,7},{7,8},{8,9},{9,10},{10,1... | collective-permute-start | bytes 3538952 | tf_op jit(solution)/shard_map/ppermute | solution.py:164
  145.6 50.7 %collective-permute-start.11 = (bf16[8,2,192,192]{3,2,1,0:T(8,128)(2,1)}, bf16[8,2,192,192]{3,2,1,0:T(8,128)(2,1)}, u32[]{:S(2)}, u32[]{:S(2)}) collective-permute-start(bf16[8,2,192,192]{3,2,1,0:T(8,128)(2,1)} %get-tuple-element.32), channel_id=1, source_target_pairs={{1,0},{2,1},{3,2},{4,3},{5,4},{6,5},{7,6},{8,7},{9,8},{10,9},{11,1... | collective-permute-start | bytes 3538952 | tf_op jit(solution)/shard_map/ppermute | solution.py:164
  154.4 1.2 collective-permute-start.12
  155.6 5.3 %collective-permute-start.13 = (f32[2,8,2]{1,2,0:T(2,128)S(1)}, f32[2,8,2]{1,2,0:T(2,128)S(1)}, u32[]{:S(2)}, u32[]{:S(2)}) collective-permute-start(f32[2,8,2]{1,2,0:T(2,128)S(1)} %fusion.7), channel_id=1, source_target_pairs={{0,2},{1,3},{2,0},{3,1},{4,6},{5,7},{6,4},{7,5},{8,10},{9,11},{10,... | collective-permute-start | bytes 392 | tf_op jit(solution)/shard_map/ppermute | solution.py:195
  160.9 4.5 %collective-permute-start.14 = (f32[2,8,2]{1,2,0:T(2,128)S(1)}, f32[2,8,2]{1,2,0:T(2,128)S(1)}, u32[]{:S(2)}, u32[]{:S(2)}) collective-permute-start(f32[2,8,2]{1,2,0:T(2,128)S(1)} %fusion.10), channel_id=1, source_target_pairs={{0,4},{1,5},{2,6},{3,7},{4,0},{5,1},{6,2},{7,3},{8,12},{9,13},{10,... | collective-permute-start | bytes 392 | tf_op jit(solution)/shard_map/ppermute | solution.py:195
  165.3 7.5 %collective-permute-start.15 = (f32[2,8,2]{1,2,0:T(2,128)S(1)}, f32[2,8,2]{1,2,0:T(2,128)S(1)}, u32[]{:S(2)}, u32[]{:S(2)}) collective-permute-start(f32[2,8,2]{1,2,0:T(2,128)S(1)} %add.74), channel_id=1, source_target_pairs={{0,8},{1,9},{2,10},{3,11},{4,12},{5,13},{6,14},{7,15},{8,0},{9,1},... | collective-permute-start | bytes 392 | tf_op jit(solution)/shard_map/ppermute | solution.py:195
  172.8 3.6 %collective-permute-start.16 = (f32[2,8,2]{1,2,0:T(2,128)S(1)}, f32[2,8,2]{1,2,0:T(2,128)S(1)}, u32[]{:S(2)}, u32[]{:S(2)}) collective-permute-start(f32[2,8,2]{1,2,0:T(2,128)S(1)} %add.75), channel_id=1, source_target_pairs={{0,16},{1,17},{2,18},{3,19},{4,20},{5,21},{6,22},{7,23},{8,24},{9,... | collective-permute-start | bytes 392 | tf_op jit(solution)/shard_map/ppermute | solution.py:195
  176.4 5.1 %collective-permute-start.17 = (f32[2,8,2]{1,2,0:T(2,128)S(1)}, f32[2,8,2]{1,2,0:T(2,128)S(1)}, u32[]{:S(2)}, u32[]{:S(2)}) collective-permute-start(f32[2,8,2]{1,2,0:T(2,128)S(1)} %add.76), channel_id=1, source_target_pairs={{0,32},{1,33},{2,34},{3,35},{4,36},{5,37},{6,38},{7,39},{8,40},{9,... | collective-permute-start | bytes 392 | tf_op jit(solution)/shard_map/ppermute | solution.py:195
  181.5 3.6 %collective-permute-start.18 = (f32[2,8,2]{1,2,0:T(2,128)S(1)}, f32[2,8,2]{1,2,0:T(2,128)S(1)}, u32[]{:S(2)}, u32[]{:S(2)}) collective-permute-start(f32[2,8,2]{1,2,0:T(2,128)S(1)} %add.77), channel_id=1, source_target_pairs={{0,64},{1,65},{2,66},{3,67},{4,68},{5,69},{6,70},{7,71},{8,72},{9,... | collective-permute-start | bytes 392 | tf_op jit(solution)/shard_map/ppermute | solution.py:195
  (6 other events, 31.4 us)
